TPU v7x, 512 devices: a whole 4x4x16 slice. The times are simulated.
512 devices in a mesh: lon: 32 (over y_lo, z), lat: 16 (over y_hi, x, core).
Axes of the slice: x: 4, y: 4 (y_hi: 2, y_lo: 2; y = y_hi * 2 + y_lo), z: 16, core: 2. Of those that a mesh axis runs over, the one named last changes fastest.
Arguments:
- tracers: float32 [5, 75, 128, 4096], P(None, None, 'lat', 'lon'), may hold values from -6 to 6
- courant: float32 [2, 75, 128, 4096], P(None, None, 'lat', 'lon'), may hold values from -0.25 to 0.25
- diffusivity: float32 [75], replicated, may hold values from 0.02 to 0.12
- melt_coef: float32 [5], replicated, may hold values from -1 to 1
- berg_profile: float32 [75, 196608], P(None, ('lon', 'lat')), may hold values from 0.05 to 0.5
- berg_mass: float32 [196608], P(('lon', 'lat')), may hold values from 1 to 16
- berg_cell: int32 [2, 196608], P(None, ('lon', 'lat')), may hold values from 0 to 1023
- send_east: int32 [2, 16384], P(None, ('lon', 'lat')), may hold values from 0 to 383, as said below
- send_west: int32 [2, 16384], P(None, ('lon', 'lat')), may hold values from 0 to 383, as said below
Outputs:
- tracers_out: float32 [5, 75, 128, 4096], P(None, None, 'lat', 'lon')
- mass_out: float32 [196608], P(('lon', 'lat'))
Inputs may be any that keep to these rules, and one draw needn't show every extreme that they name: In each step, the 32 entries of one block in send_east and its 32 entries in send_west are all different slots of that block. `send_west`: different from the same block's send_east entries of that step, and from each other.
All inputs are finite; a program needn't handle non-finite values.
Results may differ from a plain program's by a relative error of at most 0.0001.
Values sent between devices are 32-bit elements; how exact they have to be, the bound alone decides.
No kernel may reach another device: no remote copies, remote signals or barrier semaphores. Data moves between devices by JAX's collectives and lax.ppermute only.
A program may use at most 64 MiB of HBM per device.

v0:
```python
import jax
import jax.numpy as jnp
from jax import lax
from jax.sharding import PartitionSpec as P

STEPS = 2


def extended(block, sides, width, periodic):
    for axis, dim in sides:
        count = lax.axis_size(axis)
        forward = [(i, i + 1) for i in range(count - 1)]
        if periodic:
            forward.append((count - 1, 0))
        backward = [(target, source) for source, target in forward]
        low = lax.ppermute(
            lax.slice_in_dim(block, block.shape[dim] - width, None, axis=dim), axis, forward
        )
        high = lax.ppermute(lax.slice_in_dim(block, 0, width, axis=dim), axis, backward)
        block = jnp.concatenate([low, block, high], axis=dim)
    return block


def passed_along(value, axis, steps):
    count = lax.axis_size(axis)
    pairs = [(source, (source + steps) % count) for source in range(count)]
    return lax.ppermute(value, axis, pairs)


def lat_halo(moving):
    return extended(moving, (("lat", 2),), 1, False)


def lon_halo(moving):
    return extended(moving, (("lon", 3),), 1, True)


def transport(state, lon_ext, lat_ext, lon_vel, lat_vel, courant, diffusivity):
    east_vel = courant[0]
    north_vel = courant[1]
    west_vel = lon_vel[0][..., :-2]
    south_vel = lat_vel[1][..., :-2, :]
    east_side = lon_ext[..., 2:]
    west_side = lon_ext[..., :-2]
    north_side = lat_ext[..., 2:, :]
    south_side = lat_ext[..., :-2, :]
    flux_east = jnp.maximum(east_vel, 0.0) * state + jnp.minimum(east_vel, 0.0) * east_side
    flux_west = jnp.maximum(west_vel, 0.0) * west_side + jnp.minimum(west_vel, 0.0) * state
    flux_north = jnp.maximum(north_vel, 0.0) * state + jnp.minimum(north_vel, 0.0) * north_side
    flux_south = jnp.maximum(south_vel, 0.0) * south_side + jnp.minimum(south_vel, 0.0) * state
    mixing = east_side + west_side + north_side + south_side - 4.0 * state
    return (
        state
        - (flux_east - flux_west)
        - (flux_north - flux_south)
        + diffusivity[None, :, None, None] * mixing
    )


def per_device(
    tracers,
    courant,
    diffusivity,
    melt_coef,
    berg_profile,
    berg_mass,
    berg_cell,
    send_east,
    send_west,
):
    fields = tracers.shape[0]
    levels = tracers.shape[1]
    row_count = tracers.shape[2]
    col_count = tracers.shape[3]
    records = jnp.concatenate([berg_profile, berg_mass[None, :]], axis=0)
    state = tracers
    for step_index in range(STEPS):
        east_slots = send_east[step_index]
        west_slots = send_west[step_index]
        east_out = records[:, east_slots]
        west_out = records[:, west_slots]
        moving = jnp.concatenate([state, courant], axis=0)
        lon_ext = lon_halo(moving)
        east_in = passed_along(east_out, "lon", 1)
        west_in = passed_along(west_out, "lon", -1)
        lat_ext = lat_halo(moving)
        lon_vel = lon_ext[fields:]
        lat_vel = lat_ext[fields:]
        records = records.at[:, east_slots].set(east_in)
        records = records.at[:, west_slots].set(west_in)
        profile = records[:levels]
        mass_now = records[levels]
        berg_cells = berg_cell[step_index]
        flat_temp = state[0].reshape(levels, row_count * col_count)
        water_temp = flat_temp[:, berg_cells]
        melt_rate = profile * jax.nn.softplus(water_temp + 1.8) * jnp.sqrt(mass_now)[None]
        source = (
            jnp.zeros((levels, row_count * col_count), jnp.float32).at[:, berg_cells].add(melt_rate)
        )
        mass_new = mass_now / (1.0 + 0.05 * jnp.sum(melt_rate, axis=0))
        advected = transport(
            state, lon_ext[:fields], lat_ext[:fields], lon_vel, lat_vel, courant, diffusivity
        )
        state = (
            advected
            + melt_coef[:, None, None, None] * source.reshape(levels, row_count, col_count)[None]
        )
        records = jnp.concatenate([profile, mass_new[None]], axis=0)
    return (state, records[levels])


def solution(mesh):
    in_specs = (
        P(None, None, "lat", "lon"),
        P(None, None, "lat", "lon"),
        P(),
        P(),
        P(None, ("lon", "lat")),
        P(("lon", "lat")),
        P(None, ("lon", "lat")),
        P(None, ("lon", "lat")),
        P(None, ("lon", "lat")),
    )
    out_specs = (P(None, None, "lat", "lon"), P(("lon", "lat")))
    return jax.shard_map(
        per_device, mesh=mesh, in_specs=in_specs, out_specs=out_specs, check_vma=False
    )
```

profile of v0, /device:TPU:7, one launch (start us, length us, event | category | flops | bytes accessed | tf_op | source)
XLA Modules:
  0.0 121.7 jit_solution(9639901620746029512)
XLA Ops:
  0.6 0.8 fusion.48
  1.5 0.8 broadcast_in_dim.3
  2.3 1.0 copy.102
  3.3 0.6 pad_clamp_fusion.2
  4.0 0.6 gather_fusion
  4.6 3.5 %collective-permute-start.4 = (f32[76,32]{0,1:T(8,128)S(1)}, f32[76,32]{0,1:T(8,128)}, u32[]{:S(2)}, u32[]{:S(2)}) collective-permute-start(f32[76,32]{0,1:T(8,128)S(1)} %bitcast.108), channel_id=1, source_target_pairs={{0,16},{16,32},{32,48},{48,64},{64,80},{80,96},{96,112},{112,128},... | collective-permute-start | bytes 29192 | tf_op jit(solution)/shard_map/ppermute | solution.py:27
  8.1 0.8 fusion.49
  8.9 0.6 pad_clamp_fusion.1
  9.5 1.2 gather_fusion.1
  10.7 10.5 %collective-permute-start.5 = (f32[76,32]{0,1:T(8,128)}, f32[76,32]{0,1:T(8,128)}, u32[]{:S(2)}, u32[]{:S(2)}) collective-permute-start(f32[76,32]{0,1:T(8,128)} %bitcast.13), channel_id=1, source_target_pairs={{0,496},{16,0},{32,16},{48,32},{64,48},{80,64},{96,80},{112,96},{1... | collective-permute-start | bytes 29192 | tf_op jit(solution)/shard_map/ppermute | solution.py:27
  21.2 1.5 %copy.91 = f32[2,75,8,128]{1,2,3,0:T(8,128)S(1)} copy(f32[2,75,8,128]{3,2,1,0:T(8,128)} %param.10) | data formatting | bytes 1228800 | tf_op args[1]
  22.7 2.4 %copy.93 = f32[5,75,8,128]{1,2,3,0:T(8,128)} copy(f32[5,75,8,128]{3,2,1,0:T(8,128)S(1)} %copy-done.6) | data formatting | bytes 3072000 | tf_op args[0]
  25.1 1.6 %fusion.34 = (f32[7,75,8,1]{1,2,3,0:T(8,128)}, f32[7,75,8,1]{1,2,3,0:T(8,128)}, f32[7,75,8,1]{1,2,3,0:T(8,128)}, f32[7,75,8,1]{1,2,3,0:T(8,128)}) fusion(f32[5,75,8,128]{1,2,3,0:T(8,128)} %copy.93, f32[2,75,8,128]{1,2,3,0:T(8,128)S(1)} %copy.91), kind=kLoop, calls=%fused_computation.103 | loop fusion | flops 8400 | bytes 2217600 | tf_op jit(solution)/shard_map/concatenate | solution.py:82
  26.7 3.4 %collective-permute-start = (f32[7,75,8,1]{1,2,3,0:T(8,128)}, f32[7,75,8,1]{1,2,3,0:T(8,128)}, u32[]{:S(2)}, u32[]{:S(2)}) collective-permute-start(f32[7,75,8,1]{1,2,3,0:T(8,128)} %get-tuple-element.12), channel_id=1, source_target_pairs={{16,0},{32,16},{48,32},{64,48},{80,64},{96,80},{112,96},{128,112},... | collective-permute-start | bytes 50408 | tf_op jit(solution)/shard_map/ppermute | solution.py:19
  30.0 2.1 %collective-permute-start.1 = (f32[7,75,8,1]{1,2,3,0:T(8,128)}, f32[7,75,8,1]{1,2,3,0:T(8,128)}, u32[]{:S(2)}, u32[]{:S(2)}) collective-permute-start(f32[7,75,8,1]{1,2,3,0:T(8,128)} %get-tuple-element.18), channel_id=1, source_target_pairs={{0,16},{16,32},{32,48},{48,64},{64,80},{80,96},{96,112},{112,128},... | collective-permute-start | bytes 50408 | tf_op jit(solution)/shard_map/ppermute | solution.py:16
  32.1 1.4 %fusion.13 = (f32[7,75,1,128]{1,2,3,0:T(1,128)}, f32[7,75,1,128]{1,2,3,0:T(1,128)S(1)}) fusion(f32[5,75,8,128]{1,2,3,0:T(8,128)S(1)} %copy-done.2, f32[2,75,8,128]{1,2,3,0:T(8,128)S(1)} %copy.91), kind=kLoop, calls=%fused_computation.66 | loop fusion | flops 134400 | bytes 2688000 | tf_op jit(solution)/shard_map/concatenate | solution.py:82
  33.5 1.2 %copy.97 = f32[7,75,1,128]{3,1,2,0:T(8,128)} copy(f32[7,75,1,128]{1,2,3,0:T(1,128)S(1)} %get-tuple-element.21) | data formatting | bytes 537600 | tf_op jit(solution)/shard_map/slice | solution.py:17
  34.8 5.8 %collective-permute-start.3 = (f32[7,75,1,128]{3,1,2,0:T(8,128)}, f32[7,75,1,128]{3,1,2,0:T(8,128)}, u32[]{:S(2)}, u32[]{:S(2)}) collective-permute-start(f32[7,75,1,128]{3,1,2,0:T(8,128)} %copy.97), channel_id=1, source_target_pairs={{0,1},{1,2},{2,3},{3,4},{4,5},{5,6},{6,7},{7,8},{8,9},{9,10},{10,1... | collective-permute-start | bytes 806408 | tf_op jit(solution)/shard_map/ppermute | solution.py:16
  40.6 0.9 maximum_bitcast_fusion.1
  41.6 0.6 pad_clamp_fusion.3
  42.2 0.6 pad_clamp_fusion
  42.8 1.0 copy.104
  43.8 1.2 copy.87
  45.1 0.3 copy.89
  45.3 0.3 copy.94
  45.6 1.2 copy.96
  46.8 2.3 %gather_fusion.2 = f32[384,75]{1,0:T(8,128)S(1)} fusion(f32[75,1024]{0,1:T(8,128)} %bitcast.105, s32[1024]{0:T(1024)} %pad_clamp_fusion.3), kind=kCustom, calls=%fused_computation.2 | custom fusion | bytes 231936 | tf_op jit(solution)/shard_map/gather | solution.py:95
  49.2 1.9 %collective-permute-start.2 = (f32[7,75,1,128]{1,2,3,0:T(1,128)}, f32[7,75,1,128]{1,2,3,0:T(1,128)}, u32[]{:S(2)}, u32[]{:S(2)}) collective-permute-start(f32[7,75,1,128]{1,2,3,0:T(1,128)} %get-tuple-element.20), channel_id=1, source_target_pairs={{1,0},{2,1},{3,2},{4,3},{5,4},{6,5},{7,6},{8,7},{9,8},{10,9},{11,1... | collective-permute-start | bytes 806408 | tf_op jit(solution)/shard_map/ppermute | solution.py:19
  51.1 1.0 scatter_custom_fusion
  52.1 1.0 scatter_custom_fusion.1
  53.3 0.2 fusion.54
  53.5 0.3 copy-done.13
  54.2 1.3 %gather_fusion.3 = f32[32,76]{1,0:T(8,128)} fusion(f32[76,384]{0,1:T(8,128)S(1)} %pad_maximum_fusion.23, s32[1024]{0:T(1024)} %get-tuple-element.42), kind=kCustom, calls=%fused_computation.3 | custom fusion | bytes 19584 | tf_op jit(solution)/shard_map/gather | solution.py:80
  55.5 1.9 %collective-permute-start.10 = (f32[76,32]{0,1:T(8,128)}, f32[76,32]{0,1:T(8,128)}, u32[]{:S(2)}, u32[]{:S(2)}) collective-permute-start(f32[76,32]{0,1:T(8,128)} %bitcast.24), channel_id=1, source_target_pairs={{0,16},{16,32},{32,48},{48,64},{64,80},{80,96},{96,112},{112,128},... | collective-permute-start | bytes 29192 | tf_op jit(solution)/shard_map/ppermute | solution.py:27
  57.4 0.7 gather_fusion.4
  58.1 3.1 %scatter_custom_fusion.2 = f32[75,1024]{0,1:T(8,128)} fusion(s32[384]{0:T(512)} %copy-done.16, f32[]{:T(128)} %constant.8.clone.1, f32[384,75]{1,0:T(8,128)} %copy-done.10, f32[384]{0:T(512)} %copy-done.13, f32[76,384]{0,1:T(8,128)S(1)} %scatter_custom_fusion.1), kind=kCustom, calls=%fused_computation.75 | custom fusion | flops 288000 | bytes 623104 | tf_op jit(solution)/shard_map/scatter-add | solution.py:98
  61.2 2.1 %copy.105 = f32[75,8,128]{0,1,2:T(8,128)} copy(f32[75,8,128]{0,2,1:T(8,128)} %bitcast.107) | data formatting | bytes 614400 | tf_op jit(solution)/shard_map/mul | solution.py:106
  63.4 5.5 %collective-permute-start.11 = (f32[76,32]{0,1:T(8,128)S(1)}, f32[76,32]{0,1:T(8,128)S(1)}, u32[]{:S(2)}, u32[]{:S(2)}) collective-permute-start(f32[76,32]{0,1:T(8,128)S(1)} %bitcast.109), channel_id=1, source_target_pairs={{0,496},{16,0},{32,16},{48,32},{64,48},{80,64},{96,80},{112,96},{1... | collective-permute-start | bytes 29192 | tf_op jit(solution)/shard_map/ppermute | solution.py:27
  68.8 0.7 fusion.11
  69.6 1.0 slice_maximum_fusion.3
  70.6 1.0 scatter_custom_fusion.3
  71.6 0.9 scatter_custom_fusion.4
  72.5 0.3 slice_reduce_fusion
  72.8 1.9 %copy.98 = f32[7,75,1,128]{1,2,3,0:T(1,128)} copy(f32[7,75,1,128]{3,1,2,0:T(8,128)} %collective-permute-done.3) | data formatting | bytes 537600 | tf_op jit(solution)/shard_map/ppermute | solution.py:16
  74.7 1.3 %fusion.9 = f32[75,10,128]{0,1,2:T(8,128)S(1)} fusion(f32[7,75,1,128]{1,2,3,0:T(1,128)} %collective-permute-done.2, f32[7,75,1,128]{1,2,3,0:T(1,128)} %copy.98, f32[5,75,8,128]{1,2,3,0:T(8,128)} %copy.93, f32[2,75,8,128]{1,2,3,0:T(8,128)S(1)} %copy.91), kind=kLoop, calls=%fused_computation.44 | loop fusion | flops 288000 | bytes 3072000 | tf_op jit(solution)/shard_map/squeeze | solution.py:42
  76.0 0.4 copy-done.3
  77.0 5.1 %multiply_add_fusion.1 = f32[5,75,8,128]{1,2,3,0:T(8,128)S(1)} fusion(f32[5,75,8,128]{1,2,3,0:T(8,128)S(1)} %copy-done.3, f32[2,75,8,128]{1,2,3,0:T(8,128)S(1)} %copy.91, f32[7,75,1,128]{1,2,3,0:T(1,128)S(1)} %copy-done.4, f32[7,75,1,128]{1,2,3,0:T(1,128)} %collective-permute-done.2, f32[7,75,8,1]{1,2,3,0:T(8,128)} %collective-permute-done.1, ...), kind=kLoop, calls=%fused_computation.38 | loop fusion | flops 12672000 | bytes 7022720 | tf_op jit(solution)/shard_map/add | solution.py:105
  82.1 1.7 %fusion.12 = (f32[7,75,1,128]{1,2,3,0:T(1,128)}, f32[7,75,1,128]{1,2,3,0:T(1,128)}) fusion(f32[5,75,8,128]{1,2,3,0:T(8,128)S(1)} %multiply_add_fusion.1, f32[2,75,8,128]{1,2,3,0:T(8,128)S(1)} %copy.91), kind=kLoop, calls=%fused_computation.65 | loop fusion | flops 134400 | bytes 2688000 | tf_op jit(solution)/shard_map/concatenate | solution.py:82
  83.9 0.9 copy.108
  84.8 0.6 fusion.32
  85.4 4.2 %collective-permute-start.6 = (f32[7,75,8,1]{1,2,3,0:T(8,128)}, f32[7,75,8,1]{1,2,3,0:T(8,128)}, u32[]{:S(2)}, u32[]{:S(2)}) collective-permute-start(f32[7,75,8,1]{1,2,3,0:T(8,128)} %get-tuple-element.22), channel_id=1, source_target_pairs={{16,0},{32,16},{48,32},{64,48},{80,64},{96,80},{112,96},{128,112},... | collective-permute-start | bytes 50408 | tf_op jit(solution)/shard_map/ppermute | solution.py:19
  89.6 1.9 %collective-permute-start.7 = (f32[7,75,8,1]{1,2,3,0:T(8,128)}, f32[7,75,8,1]{1,2,3,0:T(8,128)}, u32[]{:S(2)}, u32[]{:S(2)}) collective-permute-start(f32[7,75,8,1]{1,2,3,0:T(8,128)} %get-tuple-element.23), channel_id=1, source_target_pairs={{0,16},{16,32},{32,48},{48,64},{64,80},{80,96},{96,112},{112,128},... | collective-permute-start | bytes 50408 | tf_op jit(solution)/shard_map/ppermute | solution.py:16
  91.6 2.6 %collective-permute-start.8 = (f32[7,75,1,128]{1,2,3,0:T(1,128)}, f32[7,75,1,128]{1,2,3,0:T(1,128)}, u32[]{:S(2)}, u32[]{:S(2)}) collective-permute-start(f32[7,75,1,128]{1,2,3,0:T(1,128)} %get-tuple-element.16), channel_id=1, source_target_pairs={{1,0},{2,1},{3,2},{4,3},{5,4},{6,5},{7,6},{8,7},{9,8},{10,9},{11,1... | collective-permute-start | bytes 806408 | tf_op jit(solution)/shard_map/ppermute | solution.py:19
  94.2 8.0 %collective-permute-start.9 = (f32[7,75,1,128]{1,2,3,0:T(1,128)}, f32[7,75,1,128]{1,2,3,0:T(1,128)}, u32[]{:S(2)}, u32[]{:S(2)}) collective-permute-start(f32[7,75,1,128]{1,2,3,0:T(1,128)} %get-tuple-element.17), channel_id=1, source_target_pairs={{0,1},{1,2},{2,3},{3,4},{4,5},{5,6},{6,7},{7,8},{8,9},{9,10},{10,1... | collective-permute-start | bytes 806408 | tf_op jit(solution)/shard_map/ppermute | solution.py:16
  102.2 2.2 %gather_fusion.5 = f32[384,75]{1,0:T(8,128)S(1)} fusion(f32[75,1024]{0,1:T(8,128)} %bitcast.104, s32[1024]{0:T(1024)S(1)} %copy-done.14), kind=kCustom, calls=%fused_computation.5 | custom fusion | bytes 231936 | tf_op jit(solution)/shard_map/gather | solution.py:95
  104.4 0.2 fusion.50
  104.7 0.6 add_divide_fusion
  105.3 2.9 %scatter_custom_fusion.5 = f32[75,1024]{0,1:T(8,128)} fusion(s32[384]{0:T(512)} %copy-done.15, f32[]{:T(128)} %constant.8.clone.1, f32[76,384]{0,1:T(8,128)S(1)} %scatter_custom_fusion.4, f32[384,75]{1,0:T(8,128)S(1)} %gather_fusion.5, f32[384]{0:T(512)S(1)} %get-tuple-element.9), kind=kCustom, calls=%fused_computation.73 | custom fusion | flops 288000 | bytes 541184 | tf_op jit(solution)/shard_map/scatter-add | solution.py:98
  108.1 1.3 %copy.109 = f32[75,8,128]{0,1,2:T(8,128)S(1)} copy(f32[75,8,128]{0,2,1:T(8,128)} %bitcast.106) | data formatting | bytes 614400 | tf_op jit(solution)/shard_map/mul | solution.py:106
  109.5 0.9 fusion.10
  110.5 0.7 copy-done.1
  111.2 1.1 fusion.8
  112.4 6.1 %multiply_add_fusion = f32[5,75,8,128]{1,2,3,0:T(8,128)} fusion(f32[5,75,8,128]{1,2,3,0:T(8,128)S(1)} %copy-done.1, f32[2,75,8,128]{1,2,3,0:T(8,128)S(1)} %copy.91, f32[7,75,1,128]{1,2,3,0:T(1,128)} %collective-permute-done.9, f32[7,75,1,128]{1,2,3,0:T(1,128)} %collective-permute-done.8, f32[7,75,8,1]{1,2,3,0:T(8,128)} %collective-permute-done.7, ...), kind=kLoop, calls=%fused_computation.37 | loop fusion | flops 12672000 | bytes 7022720 | tf_op jit(solution)/shard_map/add | solution.py:105
  118.5 3.2 %copy.110 = f32[5,75,8,128]{3,2,1,0:T(8,128)} copy(f32[5,75,8,128]{1,2,3,0:T(8,128)} %multiply_add_fusion) | data formatting | bytes 3072000
  (71 shorter events, 1.6 us)
Async XLA Ops:
  0.6 22.0 %copy-start.6 = (f32[5,75,8,128]{3,2,1,0:T(8,128)S(1)}, f32[5,75,8,128]{3,2,1,0:T(8,128)}, u32[]{:S(2)}) copy-start(f32[5,75,8,128]{3,2,1,0:T(8,128)} %param.9) | copy-start | bytes 4608004
  1.5 23.6 %copy-start.21 = (s32[32]{0:T(128)}, s32[32]{0:T(128)S(1)}, u32[]{:S(2)}) copy-start(s32[32]{0:T(128)S(1)} %get-tuple-element.40) | copy-start | bytes 388
  1.5 23.6 %copy-start.23 = (s32[32]{0:T(128)}, s32[32]{0:T(128)S(1)}, u32[]{:S(2)}) copy-start(s32[32]{0:T(128)S(1)} %get-tuple-element.41) | copy-start | bytes 388
  4.6 44.6 %collective-permute-start.4 = (f32[76,32]{0,1:T(8,128)S(1)}, f32[76,32]{0,1:T(8,128)}, u32[]{:S(2)}, u32[]{:S(2)}) collective-permute-start(f32[76,32]{0,1:T(8,128)S(1)} %bitcast.108), channel_id=1, source_target_pairs={{0,16},{16,32},{32,48},{48,64},{64,80},{80,96},{96,112},{112,128},... | collective-permute-start | bytes 29192 | tf_op jit(solution)/shard_map/ppermute | solution.py:27
  8.9 16.2 %copy-start.22 = (s32[32]{0:T(128)}, s32[32]{0:T(128)S(1)}, u32[]{:S(2)}) copy-start(s32[32]{0:T(128)S(1)} %get-tuple-element.38) | copy-start | bytes 388
  8.9 16.2 %copy-start.24 = (s32[32]{0:T(128)}, s32[32]{0:T(128)S(1)}, u32[]{:S(2)}) copy-start(s32[32]{0:T(128)S(1)} %get-tuple-element.39) | copy-start | bytes 388
  10.7 41.4 %collective-permute-start.5 = (f32[76,32]{0,1:T(8,128)}, f32[76,32]{0,1:T(8,128)}, u32[]{:S(2)}, u32[]{:S(2)}) collective-permute-start(f32[76,32]{0,1:T(8,128)} %bitcast.13), channel_id=1, source_target_pairs={{0,496},{16,0},{32,16},{48,32},{64,48},{80,64},{96,80},{112,96},{1... | collective-permute-start | bytes 29192 | tf_op jit(solution)/shard_map/ppermute | solution.py:27
  25.1 7.0 %copy-start.2 = (f32[5,75,8,128]{1,2,3,0:T(8,128)S(1)}, f32[5,75,8,128]{1,2,3,0:T(8,128)}, u32[]{:S(2)}) copy-start(f32[5,75,8,128]{1,2,3,0:T(8,128)} %copy.93) | copy-start | bytes 4608004
  26.7 36.7 %collective-permute-start = (f32[7,75,8,1]{1,2,3,0:T(8,128)}, f32[7,75,8,1]{1,2,3,0:T(8,128)}, u32[]{:S(2)}, u32[]{:S(2)}) collective-permute-start(f32[7,75,8,1]{1,2,3,0:T(8,128)} %get-tuple-element.12), channel_id=1, source_target_pairs={{16,0},{32,16},{48,32},{64,48},{80,64},{96,80},{112,96},{128,112},... | collective-permute-start | bytes 50408 | tf_op jit(solution)/shard_map/ppermute | solution.py:19
  30.0 10.6 %copy-start.5 = (f32[2,75,8,128]{3,2,1,0:T(8,128)S(1)}, f32[2,75,8,128]{3,2,1,0:T(8,128)}, u32[]{:S(2)}) copy-start(f32[2,75,8,128]{3,2,1,0:T(8,128)} %param.10) | copy-start | bytes 1843204
  30.0 11.5 %copy-start.17 = (s32[2,384]{1,0:T(2,128)S(1)}, s32[2,384]{1,0:T(2,128)}, u32[]{:S(2)}) copy-start(s32[2,384]{1,0:T(2,128)} %param.15) | copy-start | bytes 9220
  30.0 38.8 %collective-permute-start.1 = (f32[7,75,8,1]{1,2,3,0:T(8,128)}, f32[7,75,8,1]{1,2,3,0:T(8,128)}, u32[]{:S(2)}, u32[]{:S(2)}) collective-permute-start(f32[7,75,8,1]{1,2,3,0:T(8,128)} %get-tuple-element.18), channel_id=1, source_target_pairs={{0,16},{16,32},{32,48},{48,64},{64,80},{80,96},{96,112},{112,128},... | collective-permute-start | bytes 50408 | tf_op jit(solution)/shard_map/ppermute | solution.py:16
  33.5 9.2 %slice-start = ((f32[5,75,8,128]{3,2,1,0:T(8,128)}), f32[1,75,8,128]{3,2,1,0:T(8,128)S(1)}, s32[]{:S(2)}) async-start(f32[5,75,8,128]{3,2,1,0:T(8,128)} %param.9), calls=%async_computation | async-start | bytes 614400 | tf_op jit(solution)/shard_map/slice | solution.py:94
  34.8 38.0 %collective-permute-start.3 = (f32[7,75,1,128]{3,1,2,0:T(8,128)}, f32[7,75,1,128]{3,1,2,0:T(8,128)}, u32[]{:S(2)}, u32[]{:S(2)}) collective-permute-start(f32[7,75,1,128]{3,1,2,0:T(8,128)} %copy.97), channel_id=1, source_target_pairs={{0,1},{1,2},{2,3},{3,4},{4,5},{5,6},{6,7},{7,8},{8,9},{9,10},{10,1... | collective-permute-start | bytes 806408 | tf_op jit(solution)/shard_map/ppermute | solution.py:16
  41.6 3.5 %copy-start.15 = (s32[384]{0:T(512)}, s32[384]{0:T(512)S(1)}, u32[]{:S(2)}) copy-start(s32[384]{0:T(512)S(1)} %get-tuple-element.10) | copy-start | bytes 4612
  41.6 3.5 %copy-start.16 = (s32[384]{0:T(512)}, s32[384]{0:T(512)S(1)}, u32[]{:S(2)}) copy-start(s32[384]{0:T(512)S(1)} %get-tuple-element.11) | copy-start | bytes 4612
  49.1 4.9 %copy-start.10 = (f32[384,75]{1,0:T(8,128)}, f32[384,75]{1,0:T(8,128)S(1)}, u32[]{:S(2)}) copy-start(f32[384,75]{1,0:T(8,128)S(1)} %gather_fusion.2) | copy-start | bytes 345604
  49.2 25.5 %collective-permute-start.2 = (f32[7,75,1,128]{1,2,3,0:T(1,128)}, f32[7,75,1,128]{1,2,3,0:T(1,128)}, u32[]{:S(2)}, u32[]{:S(2)}) collective-permute-start(f32[7,75,1,128]{1,2,3,0:T(1,128)} %get-tuple-element.20), channel_id=1, source_target_pairs={{1,0},{2,1},{3,2},{4,3},{5,4},{6,5},{7,6},{8,7},{9,8},{10,9},{11,1... | collective-permute-start | bytes 806408 | tf_op jit(solution)/shard_map/ppermute | solution.py:19
  53.3 0.6 copy-start.13
  55.5 15.1 %collective-permute-start.10 = (f32[76,32]{0,1:T(8,128)}, f32[76,32]{0,1:T(8,128)}, u32[]{:S(2)}, u32[]{:S(2)}) collective-permute-start(f32[76,32]{0,1:T(8,128)} %bitcast.24), channel_id=1, source_target_pairs={{0,16},{16,32},{32,48},{48,64},{64,80},{80,96},{96,112},{112,128},... | collective-permute-start | bytes 29192 | tf_op jit(solution)/shard_map/ppermute | solution.py:27
  63.4 8.2 %collective-permute-start.11 = (f32[76,32]{0,1:T(8,128)S(1)}, f32[76,32]{0,1:T(8,128)S(1)}, u32[]{:S(2)}, u32[]{:S(2)}) collective-permute-start(f32[76,32]{0,1:T(8,128)S(1)} %bitcast.109), channel_id=1, source_target_pairs={{0,496},{16,0},{32,16},{48,32},{64,48},{80,64},{96,80},{112,96},{1... | collective-permute-start | bytes 29192 | tf_op jit(solution)/shard_map/ppermute | solution.py:27
  74.6 1.8 %copy-start.3 = (f32[5,75,8,128]{1,2,3,0:T(8,128)S(1)}, f32[5,75,8,128]{1,2,3,0:T(8,128)}, u32[]{:S(2)}) copy-start(f32[5,75,8,128]{1,2,3,0:T(8,128)} %copy.93) | copy-start | bytes 4608004
  74.6 1.9 %copy-start.4 = (f32[7,75,1,128]{1,2,3,0:T(1,128)S(1)}, f32[7,75,1,128]{1,2,3,0:T(1,128)}, u32[]{:S(2)}) copy-start(f32[7,75,1,128]{1,2,3,0:T(1,128)} %copy.98) | copy-start | bytes 806404
  74.6 2.0 %copy-start.7 = (f32[75,8,128]{0,1,2:T(8,128)S(1)}, f32[75,8,128]{0,1,2:T(8,128)}, u32[]{:S(2)}) copy-start(f32[75,8,128]{0,1,2:T(8,128)} %get-tuple-element.34) | copy-start | bytes 921604
  74.7 2.2 %copy-start.8 = (f32[75,8,128]{0,1,2:T(8,128)S(1)}, f32[75,8,128]{0,1,2:T(8,128)}, u32[]{:S(2)}) copy-start(f32[75,8,128]{0,1,2:T(8,128)} %get-tuple-element.35) | copy-start | bytes 921604
  74.7 2.3 %copy-start.9 = (f32[75,8,128]{0,1,2:T(8,128)S(1)}, f32[75,8,128]{0,1,2:T(8,128)}, u32[]{:S(2)}) copy-start(f32[75,8,128]{0,1,2:T(8,128)} %copy.105) | copy-start | bytes 921604
  74.7 2.3 %copy-start.18 = (f32[5]{0:T(128)S(1)}, f32[5]{0:T(128)}, u32[]{:S(2)}) copy-start(f32[5]{0:T(128)} %param.12) | copy-start | bytes 64
  74.7 2.3 %copy-start.19 = (f32[75]{0:T(128)S(1)}, f32[75]{0:T(128)}, u32[]{:S(2)}) copy-start(f32[75]{0:T(128)} %param.11) | copy-start | bytes 904
  82.1 2.7 %copy-start = (f32[5,75,8,128]{1,2,3,0:T(8,128)}, f32[5,75,8,128]{1,2,3,0:T(8,128)S(1)}, u32[]{:S(2)}) copy-start(f32[5,75,8,128]{1,2,3,0:T(8,128)S(1)} %multiply_add_fusion.1) | copy-start | bytes 4608004
  82.1 2.6 %copy-start.11 = (f32[7,75,8,1]{1,2,3,0:T(8,128)S(1)}, f32[7,75,8,1]{1,2,3,0:T(8,128)}, u32[]{:S(2)}) copy-start(f32[7,75,8,1]{1,2,3,0:T(8,128)} %get-tuple-element.13) | copy-start | bytes 50404
  82.1 2.6 %copy-start.12 = (f32[7,75,8,1]{1,2,3,0:T(8,128)S(1)}, f32[7,75,8,1]{1,2,3,0:T(8,128)}, u32[]{:S(2)}) copy-start(f32[7,75,8,1]{1,2,3,0:T(8,128)} %get-tuple-element.19) | copy-start | bytes 50404
  83.9 18.4 %copy-start.14 = (s32[1024]{0:T(1024)S(1)}, s32[1024]{0:T(1024)}, u32[]{:S(2)}) copy-start(s32[1024]{0:T(1024)} %pad_clamp_fusion) | copy-start | bytes 12292
  85.4 24.1 %collective-permute-start.6 = (f32[7,75,8,1]{1,2,3,0:T(8,128)}, f32[7,75,8,1]{1,2,3,0:T(8,128)}, u32[]{:S(2)}, u32[]{:S(2)}) collective-permute-start(f32[7,75,8,1]{1,2,3,0:T(8,128)} %get-tuple-element.22), channel_id=1, source_target_pairs={{16,0},{32,16},{48,32},{64,48},{80,64},{96,80},{112,96},{128,112},... | collective-permute-start | bytes 50408 | tf_op jit(solution)/shard_map/ppermute | solution.py:19
  89.6 19.9 %collective-permute-start.7 = (f32[7,75,8,1]{1,2,3,0:T(8,128)}, f32[7,75,8,1]{1,2,3,0:T(8,128)}, u32[]{:S(2)}, u32[]{:S(2)}) collective-permute-start(f32[7,75,8,1]{1,2,3,0:T(8,128)} %get-tuple-element.23), channel_id=1, source_target_pairs={{0,16},{16,32},{32,48},{48,64},{64,80},{80,96},{96,112},{112,128},... | collective-permute-start | bytes 50408 | tf_op jit(solution)/shard_map/ppermute | solution.py:16
  91.6 18.9 %collective-permute-start.8 = (f32[7,75,1,128]{1,2,3,0:T(1,128)}, f32[7,75,1,128]{1,2,3,0:T(1,128)}, u32[]{:S(2)}, u32[]{:S(2)}) collective-permute-start(f32[7,75,1,128]{1,2,3,0:T(1,128)} %get-tuple-element.16), channel_id=1, source_target_pairs={{1,0},{2,1},{3,2},{4,3},{5,4},{6,5},{7,6},{8,7},{9,8},{10,9},{11,1... | collective-permute-start | bytes 806408 | tf_op jit(solution)/shard_map/ppermute | solution.py:19
  94.2 16.3 %collective-permute-start.9 = (f32[7,75,1,128]{1,2,3,0:T(1,128)}, f32[7,75,1,128]{1,2,3,0:T(1,128)}, u32[]{:S(2)}, u32[]{:S(2)}) collective-permute-start(f32[7,75,1,128]{1,2,3,0:T(1,128)} %get-tuple-element.17), channel_id=1, source_target_pairs={{0,1},{1,2},{2,3},{3,4},{4,5},{5,6},{6,7},{7,8},{8,9},{9,10},{10,1... | collective-permute-start | bytes 806408 | tf_op jit(solution)/shard_map/ppermute | solution.py:16
  109.5 1.7 %copy-start.1 = (f32[5,75,8,128]{1,2,3,0:T(8,128)S(1)}, f32[5,75,8,128]{1,2,3,0:T(8,128)}, u32[]{:S(2)}) copy-start(f32[5,75,8,128]{1,2,3,0:T(8,128)} %copy-done) | copy-start | bytes 4608004
  110.5 2.0 %copy-start.20 = (f32[75]{0:T(128)S(1)}, f32[75]{0:T(128)}, u32[]{:S(2)}) copy-start(f32[75]{0:T(128)} %param.11) | copy-start | bytes 904
where the time goes:
time: 123 us; the launch traced here: 122 us
  starting transfers between devices  51.4 us (42%)
  local copies, waits for them, and re-layouts  35.1 us (29%)
  other arithmetic  34 us (28%)
    ppermute x4, starting transfers between devices, passed_along(): return lax.ppermute(value, axis, pairs)  21.4 us
    ppermute x4, starting transfers between devices, extended(): lax.ppermute(lax.slice_in_dim(block, block.shape[dim] - width, None, axis...  17.8 us
    ppermute x4, starting transfers between devices, extended(): lax.ppermute(lax.slice_in_dim(block, 0, width, axis=dim), axis, backward)  12.1 us
    add x2, other arithmetic, per_device(): advected + melt_coef[:, None, None, None] * source.reshape(levels, row_co...  11.1 us
    unnamed x54, local copies, waits for them, and re-layouts  10.3 us
    scatter-add x2, other arithmetic, per_device(): jnp.zeros((levels, row_count * col_count), jnp.float32).at[:, berg_cells]  5.99 us
    concatenate x4, other arithmetic, per_device(): moving = jnp.concatenate([state, courant], axis=0)  5.33 us
    gather x2, local copies, waits for them, and re-layouts, per_device(): water_temp = flat_temp[:, berg_cells]  4.46 us
  transfers between devices with their start and end apart: 12, of which 0 were waited for; matrix products, arithmetic and copies ran while one was open for 35% of the time, Pallas kernels for 0%

commit v1 on v0

v1 whole, which is shorter than its diff:
```python
import functools

import jax
import jax.numpy as jnp
from jax import lax
from jax.experimental import pallas as pl
from jax.experimental.pallas import tpu as pltpu
from jax.sharding import PartitionSpec as P

STEPS = 2
HI = lax.Precision.HIGHEST
LANES = 128


def _selector(rows):
    r = lax.broadcasted_iota(jnp.int32, (rows, LANES), 0)
    c = lax.broadcasted_iota(jnp.int32, (rows, LANES), 1)
    return jnp.where(((r == 0) & (c == 0)) | ((r == 1) & (c == LANES - 1)), 1.0, 0.0).astype(jnp.float32)


def _columns(block):
    return lax.dot_general(_selector(8), block, (((1,), (1,)), ((), ())), precision=HI,
                           preferred_element_type=jnp.float32)


def _column_matrix(west, east):
    count = west.shape[-1]
    stack = jnp.concatenate([west, east, jnp.zeros((6, count), jnp.float32)], axis=0)
    return lax.dot_general(stack, _selector(8), (((0,), (0,)), ((), ())), precision=HI,
                           preferred_element_type=jnp.float32)


def _extract_kernel(x_ref, c_ref, sn_ref, ss_ref, se_ref, sw_ref):
    fields = x_ref.shape[0]
    levels = sn_ref.shape[1]
    for f in range(fields):
        block = x_ref[f]
        cols = _columns(block)
        se_ref[f:f + 1, :] = cols[1:2]
        sw_ref[f:f + 1, :] = cols[0:1]
        sn_ref[f] = x_ref[f, pl.ds(7, levels, stride=8), :]
        ss_ref[f] = x_ref[f, pl.ds(0, levels, stride=8), :]
    ucols = _columns(c_ref[0])
    se_ref[fields:fields + 1, :] = ucols[1:2]
    sn_ref[fields] = c_ref[1, pl.ds(7, levels, stride=8), :]


def _step_kernel(with_sends, coef_ref, d_ref, x_ref, c_ref, src_ref, fn_ref, fs_ref, fw_ref, fe_ref,
                 cs_ref, cw_ref, o_ref, *rest):
    if with_sends:
        sn_ref, ss_ref, se_ref, sw_ref, hscr = rest
    else:
        (hscr,) = rest
    fields = x_ref.shape[0]
    count = x_ref.shape[1]
    levels = count // 8
    rows = lax.broadcasted_iota(jnp.int32, (count, LANES), 0) % 8
    lanes = lax.broadcasted_iota(jnp.int32, (count, LANES), 1)
    u = c_ref[0]
    v = c_ref[1]
    d = d_ref[...]
    cw = cw_ref.shape[0] - 1
    zero_row = jnp.zeros((1, count), jnp.float32)
    u_halo = _column_matrix(cw_ref[cw:cw + 1, :], zero_row)
    u_w = jnp.where(lanes == 0, u_halo, pltpu.roll(u, 1, 1))
    hscr[pl.ds(0, levels, stride=8), :] = cs_ref[cs_ref.shape[0] - 1]
    v_s = jnp.where(rows == 0, hscr[...], pltpu.roll(v, 1, 0))
    a_c = 1.0 - jnp.maximum(u, 0.0) + jnp.minimum(u_w, 0.0) - jnp.maximum(v, 0.0) + jnp.minimum(v_s, 0.0) - 4.0 * d
    a_e = d - jnp.minimum(u, 0.0)
    a_w = d + jnp.maximum(u_w, 0.0)
    a_n = d - jnp.minimum(v, 0.0)
    a_s = d + jnp.maximum(v_s, 0.0)
    src = src_ref[...]
    for f in range(fields):
        c = x_ref[f]
        halo = _column_matrix(fw_ref[f:f + 1, :], fe_ref[f:f + 1, :])
        east = jnp.where(lanes == LANES - 1, halo, pltpu.roll(c, LANES - 1, 1))
        west = jnp.where(lanes == 0, halo, pltpu.roll(c, 1, 1))
        hscr[pl.ds(7, levels, stride=8), :] = fn_ref[f]
        hscr[pl.ds(0, levels, stride=8), :] = fs_ref[f]
        hrow = hscr[...]
        north = jnp.where(rows == 7, hrow, pltpu.roll(c, count - 1, 0))
        south = jnp.where(rows == 0, hrow, pltpu.roll(c, 1, 0))
        out = a_c * c + a_e * east + a_w * west + a_n * north + a_s * south + coef_ref[f] * src
        o_ref[f] = out
        if with_sends:
            cols = _columns(out)
            se_ref[f:f + 1, :] = cols[1:2]
            sw_ref[f:f + 1, :] = cols[0:1]
            sn_ref[f] = o_ref[f, pl.ds(7, levels, stride=8), :]
            ss_ref[f] = o_ref[f, pl.ds(0, levels, stride=8), :]


def _vmem():
    return pl.BlockSpec(memory_space=pltpu.VMEM)


def extract(x, c):
    fields, count, _ = x.shape
    levels = count // 8
    return pl.pallas_call(
        _extract_kernel,
        out_shape=(
            jax.ShapeDtypeStruct((fields + 1, levels, LANES), jnp.float32),
            jax.ShapeDtypeStruct((fields, levels, LANES), jnp.float32),
            jax.ShapeDtypeStruct((fields + 1, count), jnp.float32),
            jax.ShapeDtypeStruct((fields, count), jnp.float32),
        ),
        in_specs=[_vmem(), _vmem()],
        out_specs=(_vmem(), _vmem(), _vmem(), _vmem()),
    )(x, c)


def step(with_sends, coef, d, x, c, src, fn, fs, fw, fe, cs, cw):
    fields, count, _ = x.shape
    levels = count // 8
    outs = [jax.ShapeDtypeStruct(x.shape, jnp.float32)]
    if with_sends:
        outs += [
            jax.ShapeDtypeStruct((fields, levels, LANES), jnp.float32),
            jax.ShapeDtypeStruct((fields, levels, LANES), jnp.float32),
            jax.ShapeDtypeStruct((fields, count), jnp.float32),
            jax.ShapeDtypeStruct((fields, count), jnp.float32),
        ]
    return pl.pallas_call(
        functools.partial(_step_kernel, with_sends),
        out_shape=tuple(outs),
        in_specs=[pl.BlockSpec(memory_space=pltpu.SMEM)] + [_vmem()] * 10,
        out_specs=tuple(_vmem() for _ in outs),
        scratch_shapes=[pltpu.VMEM((count, LANES), jnp.float32)],
    )(coef, d, x, c, src, fn, fs, fw, fe, cs, cw)


def shift(value, axis, steps, periodic):
    count = lax.axis_size(axis)
    if periodic:
        pairs = [(s, (s + steps) % count) for s in range(count)]
    else:
        pairs = [(s, s + steps) for s in range(count) if 0 <= s + steps < count]
    return lax.ppermute(value, axis, pairs)


def per_device(tracers, courant, diffusivity, melt_coef, berg_profile, berg_mass, berg_cell,
               send_east, send_west):
    fields, levels, rows, cols = tracers.shape
    count = levels * rows
    x = tracers.reshape(fields, count, cols)
    c = courant.reshape(2, count, cols)
    d = jnp.broadcast_to(diffusivity[:, None, None], (levels, rows, cols)).reshape(count, cols)
    records = jnp.concatenate([berg_profile, berg_mass[None, :]], axis=0)
    sn, ss, se, sw = extract(x, c)
    cs = cw = None
    for step_index in range(STEPS):
        east_slots = send_east[step_index]
        west_slots = send_west[step_index]
        east_out = records[:, east_slots]
        west_out = records[:, west_slots]
        from_s = shift(sn, "lat", 1, False)
        from_n = shift(ss, "lat", -1, False)
        from_w = shift(se, "lon", 1, True)
        from_e = shift(sw, "lon", -1, True)
        east_in = shift(east_out, "lon", 1, True)
        west_in = shift(west_out, "lon", -1, True)
        if cs is None:
            cs, cw = from_s, from_w
        records = records.at[:, east_slots].set(east_in)
        records = records.at[:, west_slots].set(west_in)
        profile = records[:levels]
        mass_now = records[levels]
        berg_cells = berg_cell[step_index]
        flat_temp = x[0].reshape(levels, rows * cols)
        water_temp = flat_temp[:, berg_cells]
        melt_rate = profile * jax.nn.softplus(water_temp + 1.8) * jnp.sqrt(mass_now)[None]
        source = jnp.zeros((levels, rows * cols), jnp.float32).at[:, berg_cells].add(melt_rate)
        mass_new = mass_now / (1.0 + 0.05 * jnp.sum(melt_rate, axis=0))
        src = source.reshape(count, cols)
        last = step_index == STEPS - 1
        result = step(not last, melt_coef, d, x, c, src, from_n, from_s, from_w, from_e, cs, cw)
        if last:
            x = result[0]
        else:
            x, sn, ss, se, sw = result
        records = jnp.concatenate([profile, mass_new[None]], axis=0)
    return (x.reshape(fields, levels, rows, cols), records[levels])


def solution(mesh):
    in_specs = (
        P(None, None, "lat", "lon"),
        P(None, None, "lat", "lon"),
        P(),
        P(),
        P(None, ("lon", "lat")),
        P(("lon", "lat")),
        P(None, ("lon", "lat")),
        P(None, ("lon", "lat")),
        P(None, ("lon", "lat")),
    )
    out_specs = (P(None, None, "lat", "lon"), P(("lon", "lat")))
    return jax.shard_map(
        per_device, mesh=mesh, in_specs=in_specs, out_specs=out_specs, check_vma=False
    )
```

time: 123 us -> 99.9 us (0.81)
  other arithmetic: 34 us -> 7.28 us
  Pallas kernels: 0 us -> 21.6 us
  local copies, waits for them, and re-layouts: 35.1 us -> 16.8 us
    pallas_call x0 -> x3, Pallas kernels: none -> 21.6 us  [the longest x2 17.7 us: step(): pl.pallas_call(functools.partial(_step_kernel, with_sends), out_shape=tup...]
    add x2 -> x0, other arithmetic: 11.1 us -> none  [per_device(): advected + melt_coef[:, None, None, None] * source.reshape(levels, row_co...]
    unnamed x54 -> x23, local copies, waits for them, and re-layouts: 10.3 us -> 2.42 us
    mul x6 -> x0, local copies, waits for them, and re-layouts: 6.45 us -> none  [the longest x2 3.49 us: per_device(): melt_coef[:, None, None, None]]
    concatenate x4 -> x0, other arithmetic: 5.33 us -> none  [per_device(): moving = jnp.concatenate([state, courant], axis=0)]
    squeeze x4 -> x0, other arithmetic: 3.94 us -> none  [the longest x2 2.36 us: transport(): south_vel = lat_vel[1][..., :-2, :]]
    gather x2, local copies, waits for them, and re-layouts: 4.46 us -> 2.25 us  [per_device(): water_temp = flat_temp[:, berg_cells]]
    ppermute x1 -> x0, local copies, waits for them, and re-layouts: 1.89 us -> none  [extended(): lax.ppermute(lax.slice_in_dim(block, block.shape[dim] - width, None, axis...]
  transfers between devices with their start and end apart: 12 -> 12, of which waited for: 0 -> 0; matrix products, arithmetic and copies ran while one was open for 35% -> 19% of each run, Pallas kernels for 0% -> 4%
where the time goes in v1:
time: 99.9 us; the launch traced here: 99.3 us
  starting transfers between devices  52.4 us (52%)
  Pallas kernels  21.6 us (22%)
  local copies, waits for them, and re-layouts  16.8 us (17%)
  other arithmetic  7.28 us (7%)
  between operations  1.06 us (1%)
    ppermute x12, starting transfers between devices, shift(): return lax.ppermute(value, axis, pairs)  52.4 us
    pallas_call x2, Pallas kernels, step(): pl.pallas_call(functools.partial(_step_kernel, with_sends), out_shape=tup...  17.7 us
    scatter-add x2, other arithmetic, per_device(): jnp.zeros((levels, rows * cols), jnp.float32).at[:, berg_cells]  4.19 us
    pallas_call x1, Pallas kernels, extract(): pl.pallas_call(_extract_kernel, out_shape=(jax.ShapeDtypeStruct((fields +...  3.96 us
    unnamed x23, local copies, waits for them, and re-layouts  2.42 us
    gather x2, local copies, waits for them, and re-layouts, per_device(): water_temp = flat_temp[:, berg_cells]  2.25 us
    slice x3, local copies, waits for them, and re-layouts, per_device(): flat_temp = x[0].reshape(levels, rows * cols)  2.21 us
  transfers between devices with their start and end apart: 12, of which 0 were waited for; matrix products, arithmetic and copies ran while one was open for 19% of the time, Pallas kernels for 4%

profile of v1, /device:TPU:7, one launch (start us, length us, event | category | flops | bytes accessed | tf_op | source)
XLA Modules:
  0.0 99.3 jit_solution(17348865273023823730)
XLA Ops:
  0.6 0.8 fusion.30
  1.4 1.0 %copy.16 = f32[75,384]{0,1:T(8,128)S(1)} copy(f32[75,384]{1,0:T(8,128)} %param.13) | data formatting | bytes 230400 | tf_op args[4]
  2.4 0.8 broadcast_in_dim.12
  3.2 0.1 pad_maximum_fusion
  3.4 0.0 copy-start.8
  3.4 0.6 gather_fusion
  3.9 3.5 %collective-permute-start = (f32[76,32]{0,1:T(8,128)S(1)}, f32[76,32]{0,1:T(8,128)S(1)}, u32[]{:S(2)}, u32[]{:S(2)}) collective-permute-start(f32[76,32]{0,1:T(8,128)S(1)} %bitcast.99), channel_id=1, source_target_pairs={{0,16},{16,32},{32,48},{48,64},{64,80},{80,96},{96,112},{112,128},... | collective-permute-start | bytes 29192 | tf_op jit(solution)/shard_map/ppermute | solution.py:140
  7.5 0.8 fusion.31
  8.3 0.6 gather_fusion.1
  8.8 10.5 %collective-permute-start.1 = (f32[76,32]{0,1:T(8,128)S(1)}, f32[76,32]{0,1:T(8,128)S(1)}, u32[]{:S(2)}, u32[]{:S(2)}) collective-permute-start(f32[76,32]{0,1:T(8,128)S(1)} %bitcast.100), channel_id=1, source_target_pairs={{0,496},{16,0},{32,16},{48,32},{64,48},{80,64},{96,80},{112,96},{1... | collective-permute-start | bytes 29192 | tf_op jit(solution)/shard_map/ppermute | solution.py:140
  19.4 4.0 %shard_map.104 = (f32[6,75,128]{2,1,0:T(8,128)}, f32[5,75,128]{2,1,0:T(8,128)}, f32[6,600]{1,0:T(8,128)}, f32[5,600]{1,0:T(8,128)}) custom-call(f32[5,600,128]{2,1,0:T(8,128)} %bitcast.92, f32[2,600,128]{2,1,0:T(8,128)} %bitcast.94), custom_call_target="tpu_custom_call" | custom-call | tf_op jit(solution)/shard_map/pallas_call | solution.py:101
  23.3 1.9 %collective-permute-start.4 = (f32[6,600]{1,0:T(8,128)}, f32[6,600]{1,0:T(8,128)S(1)}, u32[]{:S(2)}, u32[]{:S(2)}) collective-permute-start(f32[6,600]{1,0:T(8,128)} %get-tuple-element.13), channel_id=1, source_target_pairs={{0,16},{16,32},{32,48},{48,64},{64,80},{80,96},{96,112},{112,128},... | collective-permute-start | bytes 43208 | tf_op jit(solution)/shard_map/ppermute | solution.py:140
  25.2 2.9 %collective-permute-start.2 = (f32[5,75,128]{2,1,0:T(8,128)}, f32[5,75,128]{2,1,0:T(8,128)S(1)}, u32[]{:S(2)}, u32[]{:S(2)}) collective-permute-start(f32[5,75,128]{2,1,0:T(8,128)} %get-tuple-element.11), channel_id=1, source_target_pairs={{1,0},{2,1},{3,2},{4,3},{5,4},{6,5},{7,6},{8,7},{9,8},{10,9},{11,1... | collective-permute-start | bytes 576008 | tf_op jit(solution)/shard_map/ppermute | solution.py:140
  28.1 6.3 %collective-permute-start.3 = (f32[6,75,128]{2,1,0:T(8,128)}, f32[6,75,128]{2,1,0:T(8,128)S(1)}, u32[]{:S(2)}, u32[]{:S(2)}) collective-permute-start(f32[6,75,128]{2,1,0:T(8,128)} %get-tuple-element.12), channel_id=1, source_target_pairs={{0,1},{1,2},{2,3},{3,4},{4,5},{5,6},{6,7},{7,8},{8,9},{9,10},{10,1... | collective-permute-start | bytes 691208 | tf_op jit(solution)/shard_map/ppermute | solution.py:140
  34.5 1.0 slice.41
  35.5 0.2 copy.18
  35.7 1.1 %gather_fusion.2 = f32[384,75]{1,0:T(8,128)S(1)} fusion(f32[75,1024]{0,1:T(8,128)S(1)} %bitcast.97, s32[1024]{0:T(1024)S(1)} %pad_clamp_fusion.3), kind=kCustom, calls=%fused_computation.2 | custom fusion | bytes 231936 | tf_op jit(solution)/shard_map/gather | solution.py:172
  36.8 0.0 copy-start.9
  36.9 0.0 collective-permute-done
  36.9 0.8 scatter_custom_fusion
  37.7 0.0 collective-permute-done.1
  37.7 0.8 scatter_custom_fusion.1
  38.5 0.2 sqrt_reduce_fusion.1
  38.7 0.3 fusion.36
  38.9 0.2 reshape_divide_fusion
  39.1 0.1 pad_maximum_fusion.1
  39.3 0.6 gather_fusion.4
  39.8 0.6 gather_fusion.3
  40.4 1.9 %collective-permute-start.6 = (f32[76,32]{0,1:T(8,128)S(1)}, f32[76,32]{0,1:T(8,128)S(1)}, u32[]{:S(2)}, u32[]{:S(2)}) collective-permute-start(f32[76,32]{0,1:T(8,128)S(1)} %bitcast.102), channel_id=1, source_target_pairs={{0,16},{16,32},{32,48},{48,64},{64,80},{80,96},{96,112},{112,128},... | collective-permute-start | bytes 29192 | tf_op jit(solution)/shard_map/ppermute | solution.py:140
  42.3 5.5 %collective-permute-start.7 = (f32[76,32]{0,1:T(8,128)S(1)}, f32[76,32]{0,1:T(8,128)S(1)}, u32[]{:S(2)}, u32[]{:S(2)}) collective-permute-start(f32[76,32]{0,1:T(8,128)S(1)} %bitcast.101), channel_id=1, source_target_pairs={{0,496},{16,0},{32,16},{48,32},{64,48},{80,64},{96,80},{112,96},{1... | collective-permute-start | bytes 29192 | tf_op jit(solution)/shard_map/ppermute | solution.py:140
  47.8 0.1 broadcast_in_dim.8
  47.9 0.1 broadcast_in_dim.9
  48.0 2.1 %scatter_custom_fusion.2 = f32[75,1024]{0,1:T(8,128)S(1)} fusion(s32[384]{0:T(512)S(1)} %get-tuple-element.23, f32[]{:T(128)} %constant.7.clone.1, f32[384,75]{1,0:T(8,128)S(1)} %gather_fusion.2, f32[384]{0:T(512)S(1)} %sqrt_reduce_fusion.1, f32[76,384]{0,1:T(8,128)S(1)} %scatter_custom_fusion.1), kind=kCustom, calls=%fused_computation.16 | custom fusion | flops 288000 | bytes 702468 | tf_op jit(solution)/shard_map/scatter-add | solution.py:174
  50.1 0.2 copy.19
  50.3 0.8 reshape.208.src_ref
  51.1 3.4 %collective-permute-start.5 = (f32[5,600]{1,0:T(8,128)S(1)}, f32[5,600]{1,0:T(8,128)S(1)}, u32[]{:S(2)}, u32[]{:S(2)}) collective-permute-start(f32[5,600]{1,0:T(8,128)S(1)} %copy-done.10), channel_id=1, source_target_pairs={{0,496},{16,0},{32,16},{48,32},{64,48},{80,64},{96,80},{112,96},{1... | collective-permute-start | bytes 36008 | tf_op jit(solution)/shard_map/ppermute | solution.py:140
  54.5 0.8 scatter_custom_fusion.3
  55.3 0.8 scatter_custom_fusion.4
  56.1 0.3 slice_reduce_fusion
  56.3 0.0 collective-permute-done.5.fe_ref
  56.3 0.0 collective-permute-done.4.fw_ref.cw_ref
  56.4 0.0 collective-permute-done.3.fs_ref.cs_ref
  56.4 0.9 broadcast_in_dim.10.d_ref
  57.3 10.7 %shard_map.105 = (f32[5,600,128]{2,1,0:T(8,128)}, f32[5,75,128]{2,1,0:T(8,128)}, f32[5,75,128]{2,1,0:T(8,128)}, f32[5,600]{1,0:T(8,128)}, f32[5,600]{1,0:T(8,128)}) custom-call(f32[5]{0:T(128)} %coef_ref.3, f32[600,128]{1,0:T(8,128)} %broadcast_in_dim.10.d_ref, f32[5,600,128]{2,1,0:T(8,128)} %bitcast.93, f32[2,600,128]{2,1,0:T(8,128)} %bitcast.95, ...), custom_call_target="tpu_custom_call" | custom-call | tf_op jit(solution)/shard_map/pallas_call | solution.py:125
  68.0 1.9 %collective-permute-start.10 = (f32[5,600]{1,0:T(8,128)}, f32[5,600]{1,0:T(8,128)S(1)}, u32[]{:S(2)}, u32[]{:S(2)}) collective-permute-start(f32[5,600]{1,0:T(8,128)} %get-tuple-element.18), channel_id=1, source_target_pairs={{0,16},{16,32},{32,48},{48,64},{64,80},{80,96},{96,112},{112,128},... | collective-permute-start | bytes 36008 | tf_op jit(solution)/shard_map/ppermute | solution.py:140
  69.9 5.5 %collective-permute-start.11 = (f32[5,600]{1,0:T(8,128)}, f32[5,600]{1,0:T(8,128)S(1)}, u32[]{:S(2)}, u32[]{:S(2)}) collective-permute-start(f32[5,600]{1,0:T(8,128)} %get-tuple-element.19), channel_id=1, source_target_pairs={{0,496},{16,0},{32,16},{48,32},{64,48},{80,64},{96,80},{112,96},{1... | collective-permute-start | bytes 36008 | tf_op jit(solution)/shard_map/ppermute | solution.py:140
  75.4 1.9 %collective-permute-start.8 = (f32[5,75,128]{2,1,0:T(8,128)}, f32[5,75,128]{2,1,0:T(8,128)S(1)}, u32[]{:S(2)}, u32[]{:S(2)}) collective-permute-start(f32[5,75,128]{2,1,0:T(8,128)} %get-tuple-element.16), channel_id=1, source_target_pairs={{1,0},{2,1},{3,2},{4,3},{5,4},{6,5},{7,6},{8,7},{9,8},{10,9},{11,1... | collective-permute-start | bytes 576008 | tf_op jit(solution)/shard_map/ppermute | solution.py:140
  77.3 7.3 %collective-permute-start.9 = (f32[5,75,128]{2,1,0:T(8,128)}, f32[5,75,128]{2,1,0:T(8,128)S(1)}, u32[]{:S(2)}, u32[]{:S(2)}) collective-permute-start(f32[5,75,128]{2,1,0:T(8,128)} %get-tuple-element.17), channel_id=1, source_target_pairs={{0,1},{1,2},{2,3},{3,4},{4,5},{5,6},{6,7},{7,8},{8,9},{9,10},{10,1... | collective-permute-start | bytes 576008 | tf_op jit(solution)/shard_map/ppermute | solution.py:140
  84.6 1.0 slice.47
  85.6 0.1 reshape_squeeze.7
  85.6 0.2 copy.21
  85.8 1.1 %gather_fusion.5 = f32[384,75]{1,0:T(8,128)S(1)} fusion(f32[75,1024]{0,1:T(8,128)S(1)} %copy.21, s32[1024]{0:T(1024)S(1)} %pad_clamp_fusion), kind=kCustom, calls=%fused_computation.5 | custom fusion | bytes 231936 | tf_op jit(solution)/shard_map/gather | solution.py:172
  87.0 0.2 fusion.32
  87.2 0.6 add_divide_fusion
  87.8 2.1 %scatter_custom_fusion.5 = f32[75,1024]{0,1:T(8,128)S(1)} fusion(s32[384]{0:T(512)S(1)} %get-tuple-element.22, f32[]{:T(128)} %constant.7.clone.1, f32[76,384]{0,1:T(8,128)S(1)} %scatter_custom_fusion.4, f32[384,75]{1,0:T(8,128)S(1)} %gather_fusion.5, f32[384]{0:T(512)S(1)} %get-tuple-element.21), kind=kCustom, calls=%fused_computation.14 | custom fusion | flops 288000 | bytes 702468 | tf_op jit(solution)/shard_map/scatter-add | solution.py:174
  89.9 0.2 copy.22
  90.1 0.8 reshape.209.src_ref
  90.9 0.0 collective-permute-done.11.fe_ref
  90.9 0.0 collective-permute-done.8.fn_ref
  91.0 0.6 copy-done.6
  91.5 0.0 copy-done.7
  91.5 0.1 copy-done.2
  91.6 0.7 copy-done.3
  92.3 6.9 %shard_map.106 = f32[5,600,128]{2,1,0:T(8,128)} custom-call(f32[5]{0:T(128)} %coef_ref.3, f32[600,128]{1,0:T(8,128)} %broadcast_in_dim.10.d_ref, f32[5,600,128]{2,1,0:T(8,128)} %get-tuple-element.15.x_ref, f32[2,600,128]{2,1,0:T(8,128)} %bitcast.96, f32[600,128]{1,0:T(8,128)} %reshape.209.src_ref, f32[5,75,128]{2,1,0:T(8,128)} %copy-done.2, ...), custom_call_target="tpu_custom_call" | custom-call | tf_op jit(solution)/shard_map/pallas_call | solution.py:125
  (27 shorter events, 0.1 us)
Async XLA Ops:
  3.4 31.1 %copy-start.8 = (s32[2,384]{1,0:T(2,128)S(1)}, s32[2,384]{1,0:T(2,128)}, u32[]{:S(2)}) copy-start(s32[2,384]{1,0:T(2,128)} %param.15) | copy-start | bytes 9220
  3.9 32.9 %collective-permute-start = (f32[76,32]{0,1:T(8,128)S(1)}, f32[76,32]{0,1:T(8,128)S(1)}, u32[]{:S(2)}, u32[]{:S(2)}) collective-permute-start(f32[76,32]{0,1:T(8,128)S(1)} %bitcast.99), channel_id=1, source_target_pairs={{0,16},{16,32},{32,48},{48,64},{64,80},{80,96},{96,112},{112,128},... | collective-permute-start | bytes 29192 | tf_op jit(solution)/shard_map/ppermute | solution.py:140
  8.8 28.8 %collective-permute-start.1 = (f32[76,32]{0,1:T(8,128)S(1)}, f32[76,32]{0,1:T(8,128)S(1)}, u32[]{:S(2)}, u32[]{:S(2)}) collective-permute-start(f32[76,32]{0,1:T(8,128)S(1)} %bitcast.100), channel_id=1, source_target_pairs={{0,496},{16,0},{32,16},{48,32},{64,48},{80,64},{96,80},{112,96},{1... | collective-permute-start | bytes 29192 | tf_op jit(solution)/shard_map/ppermute | solution.py:140
  23.3 33.0 %collective-permute-start.4 = (f32[6,600]{1,0:T(8,128)}, f32[6,600]{1,0:T(8,128)S(1)}, u32[]{:S(2)}, u32[]{:S(2)}) collective-permute-start(f32[6,600]{1,0:T(8,128)} %get-tuple-element.13), channel_id=1, source_target_pairs={{0,16},{16,32},{32,48},{48,64},{64,80},{80,96},{96,112},{112,128},... | collective-permute-start | bytes 43208 | tf_op jit(solution)/shard_map/ppermute | solution.py:140
  25.2 31.1 %collective-permute-start.2 = (f32[5,75,128]{2,1,0:T(8,128)}, f32[5,75,128]{2,1,0:T(8,128)S(1)}, u32[]{:S(2)}, u32[]{:S(2)}) collective-permute-start(f32[5,75,128]{2,1,0:T(8,128)} %get-tuple-element.11), channel_id=1, source_target_pairs={{1,0},{2,1},{3,2},{4,3},{5,4},{6,5},{7,6},{8,7},{9,8},{10,9},{11,1... | collective-permute-start | bytes 576008 | tf_op jit(solution)/shard_map/ppermute | solution.py:140
  28.1 28.3 %collective-permute-start.3 = (f32[6,75,128]{2,1,0:T(8,128)}, f32[6,75,128]{2,1,0:T(8,128)S(1)}, u32[]{:S(2)}, u32[]{:S(2)}) collective-permute-start(f32[6,75,128]{2,1,0:T(8,128)} %get-tuple-element.12), channel_id=1, source_target_pairs={{0,1},{1,2},{2,3},{3,4},{4,5},{5,6},{6,7},{7,8},{8,9},{9,10},{10,1... | collective-permute-start | bytes 691208 | tf_op jit(solution)/shard_map/ppermute | solution.py:140
  36.8 11.0 %copy-start.9 = (f32[75]{0:T(128)S(1)}, f32[75]{0:T(128)}, u32[]{:S(2)}) copy-start(f32[75]{0:T(128)} %param.11) | copy-start | bytes 904
  39.3 11.9 %copy-start.10 = (f32[5,600]{1,0:T(8,128)S(1)}, f32[5,600]{1,0:T(8,128)}, u32[]{:S(2)}) copy-start(f32[5,600]{1,0:T(8,128)} %get-tuple-element.14) | copy-start | bytes 36004
  40.4 10.7 %collective-permute-start.6 = (f32[76,32]{0,1:T(8,128)S(1)}, f32[76,32]{0,1:T(8,128)S(1)}, u32[]{:S(2)}, u32[]{:S(2)}) collective-permute-start(f32[76,32]{0,1:T(8,128)S(1)} %bitcast.102), channel_id=1, source_target_pairs={{0,16},{16,32},{32,48},{48,64},{64,80},{80,96},{96,112},{112,128},... | collective-permute-start | bytes 29192 | tf_op jit(solution)/shard_map/ppermute | solution.py:140
  42.3 12.9 %collective-permute-start.7 = (f32[76,32]{0,1:T(8,128)S(1)}, f32[76,32]{0,1:T(8,128)S(1)}, u32[]{:S(2)}, u32[]{:S(2)}) collective-permute-start(f32[76,32]{0,1:T(8,128)S(1)} %bitcast.101), channel_id=1, source_target_pairs={{0,496},{16,0},{32,16},{48,32},{64,48},{80,64},{96,80},{112,96},{1... | collective-permute-start | bytes 29192 | tf_op jit(solution)/shard_map/ppermute | solution.py:140
  51.1 5.2 %collective-permute-start.5 = (f32[5,600]{1,0:T(8,128)S(1)}, f32[5,600]{1,0:T(8,128)S(1)}, u32[]{:S(2)}, u32[]{:S(2)}) collective-permute-start(f32[5,600]{1,0:T(8,128)S(1)} %copy-done.10), channel_id=1, source_target_pairs={{0,496},{16,0},{32,16},{48,32},{64,48},{80,64},{96,80},{112,96},{1... | collective-permute-start | bytes 36008 | tf_op jit(solution)/shard_map/ppermute | solution.py:140
  56.3 0.9 copy-start.5
  56.4 0.9 copy-start.4
  56.4 0.9 copy-start.1
  56.4 0.9 copy-start
  68.0 22.9 %collective-permute-start.10 = (f32[5,600]{1,0:T(8,128)}, f32[5,600]{1,0:T(8,128)S(1)}, u32[]{:S(2)}, u32[]{:S(2)}) collective-permute-start(f32[5,600]{1,0:T(8,128)} %get-tuple-element.18), channel_id=1, source_target_pairs={{0,16},{16,32},{32,48},{48,64},{64,80},{80,96},{96,112},{112,128},... | collective-permute-start | bytes 36008 | tf_op jit(solution)/shard_map/ppermute | solution.py:140
  69.9 21.0 %collective-permute-start.11 = (f32[5,600]{1,0:T(8,128)}, f32[5,600]{1,0:T(8,128)S(1)}, u32[]{:S(2)}, u32[]{:S(2)}) collective-permute-start(f32[5,600]{1,0:T(8,128)} %get-tuple-element.19), channel_id=1, source_target_pairs={{0,496},{16,0},{32,16},{48,32},{64,48},{80,64},{96,80},{112,96},{1... | collective-permute-start | bytes 36008 | tf_op jit(solution)/shard_map/ppermute | solution.py:140
  75.4 15.5 %collective-permute-start.8 = (f32[5,75,128]{2,1,0:T(8,128)}, f32[5,75,128]{2,1,0:T(8,128)S(1)}, u32[]{:S(2)}, u32[]{:S(2)}) collective-permute-start(f32[5,75,128]{2,1,0:T(8,128)} %get-tuple-element.16), channel_id=1, source_target_pairs={{1,0},{2,1},{3,2},{4,3},{5,4},{6,5},{7,6},{8,7},{9,8},{10,9},{11,1... | collective-permute-start | bytes 576008 | tf_op jit(solution)/shard_map/ppermute | solution.py:140
  77.3 13.6 %collective-permute-start.9 = (f32[5,75,128]{2,1,0:T(8,128)}, f32[5,75,128]{2,1,0:T(8,128)S(1)}, u32[]{:S(2)}, u32[]{:S(2)}) collective-permute-start(f32[5,75,128]{2,1,0:T(8,128)} %get-tuple-element.17), channel_id=1, source_target_pairs={{0,1},{1,2},{2,3},{3,4},{4,5},{5,6},{6,7},{7,8},{8,9},{9,10},{10,1... | collective-permute-start | bytes 576008 | tf_op jit(solution)/shard_map/ppermute | solution.py:140
  90.9 0.6 copy-start.6
  90.9 0.6 copy-start.7
  90.9 0.7 copy-start.2
  91.6 0.7 copy-start.3

commit v2 on v1

--- a/solution.py
+++ b/solution.py
@@ -8,40 +8,35 @@
 from jax.sharding import PartitionSpec as P
 
 STEPS = 2
-HI = lax.Precision.HIGHEST
 LANES = 128
 
 
-def _selector(rows):
-    r = lax.broadcasted_iota(jnp.int32, (rows, LANES), 0)
-    c = lax.broadcasted_iota(jnp.int32, (rows, LANES), 1)
-    return jnp.where(((r == 0) & (c == 0)) | ((r == 1) & (c == LANES - 1)), 1.0, 0.0).astype(jnp.float32)
-
-
-def _columns(block):
-    return lax.dot_general(_selector(8), block, (((1,), (1,)), ((), ())), precision=HI,
-                           preferred_element_type=jnp.float32)
-
-
-def _column_matrix(west, east):
-    count = west.shape[-1]
-    stack = jnp.concatenate([west, east, jnp.zeros((6, count), jnp.float32)], axis=0)
-    return lax.dot_general(stack, _selector(8), (((0,), (0,)), ((), ())), precision=HI,
-                           preferred_element_type=jnp.float32)
+def _columns(block, width):
+    count = block.shape[0]
+    padded = jnp.concatenate([block, jnp.zeros((width - count, LANES), jnp.float32)], axis=0)
+    return padded.T
+
+
+def _column_matrix(west, east, count):
+    width = west.shape[-1]
+    r = lax.broadcasted_iota(jnp.int32, (LANES, width), 0)
+    grid = jnp.where(r == 0, west, jnp.where(r == LANES - 1, east, 0.0))
+    return grid.T[:count]
 
 
 def _extract_kernel(x_ref, c_ref, sn_ref, ss_ref, se_ref, sw_ref):
     fields = x_ref.shape[0]
     levels = sn_ref.shape[1]
+    width = se_ref.shape[1]
     for f in range(fields):
         block = x_ref[f]
-        cols = _columns(block)
-        se_ref[f:f + 1, :] = cols[1:2]
+        cols = _columns(block, width)
+        se_ref[f:f + 1, :] = cols[LANES - 1:LANES]
         sw_ref[f:f + 1, :] = cols[0:1]
         sn_ref[f] = x_ref[f, pl.ds(7, levels, stride=8), :]
         ss_ref[f] = x_ref[f, pl.ds(0, levels, stride=8), :]
-    ucols = _columns(c_ref[0])
-    se_ref[fields:fields + 1, :] = ucols[1:2]
+    ucols = _columns(c_ref[0], width)
+    se_ref[fields:fields + 1, :] = ucols[LANES - 1:LANES]
     sn_ref[fields] = c_ref[1, pl.ds(7, levels, stride=8), :]
 
 
@@ -59,11 +54,11 @@
     u = c_ref[0]
     v = c_ref[1]
     d = d_ref[...]
-    cw = cw_ref.shape[0] - 1
-    zero_row = jnp.zeros((1, count), jnp.float32)
-    u_halo = _column_matrix(cw_ref[cw:cw + 1, :], zero_row)
+    width = cw_ref.shape[1]
+    zero_row = jnp.zeros((1, width), jnp.float32)
+    u_halo = _column_matrix(cw_ref[fields:fields + 1, :], zero_row, count)
     u_w = jnp.where(lanes == 0, u_halo, pltpu.roll(u, 1, 1))
-    hscr[pl.ds(0, levels, stride=8), :] = cs_ref[cs_ref.shape[0] - 1]
+    hscr[pl.ds(0, levels, stride=8), :] = cs_ref[fields]
     v_s = jnp.where(rows == 0, hscr[...], pltpu.roll(v, 1, 0))
     a_c = 1.0 - jnp.maximum(u, 0.0) + jnp.minimum(u_w, 0.0) - jnp.maximum(v, 0.0) + jnp.minimum(v_s, 0.0) - 4.0 * d
     a_e = d - jnp.minimum(u, 0.0)
@@ -73,7 +68,7 @@
     src = src_ref[...]
     for f in range(fields):
         c = x_ref[f]
-        halo = _column_matrix(fw_ref[f:f + 1, :], fe_ref[f:f + 1, :])
+        halo = _column_matrix(fw_ref[f:f + 1, :], fe_ref[f:f + 1, :], count)
         east = jnp.where(lanes == LANES - 1, halo, pltpu.roll(c, LANES - 1, 1))
         west = jnp.where(lanes == 0, halo, pltpu.roll(c, 1, 1))
         hscr[pl.ds(7, levels, stride=8), :] = fn_ref[f]
@@ -84,11 +79,15 @@
         out = a_c * c + a_e * east + a_w * west + a_n * north + a_s * south + coef_ref[f] * src
         o_ref[f] = out
         if with_sends:
-            cols = _columns(out)
-            se_ref[f:f + 1, :] = cols[1:2]
+            cols = _columns(out, width)
+            se_ref[f:f + 1, :] = cols[LANES - 1:LANES]
             sw_ref[f:f + 1, :] = cols[0:1]
             sn_ref[f] = o_ref[f, pl.ds(7, levels, stride=8), :]
             ss_ref[f] = o_ref[f, pl.ds(0, levels, stride=8), :]
+
+
+def _width(count):
+    return -(-count // LANES) * LANES
 
 
 def _vmem():
@@ -103,8 +102,8 @@
         out_shape=(
             jax.ShapeDtypeStruct((fields + 1, levels, LANES), jnp.float32),
             jax.ShapeDtypeStruct((fields, levels, LANES), jnp.float32),
-            jax.ShapeDtypeStruct((fields + 1, count), jnp.float32),
-            jax.ShapeDtypeStruct((fields, count), jnp.float32),
+            jax.ShapeDtypeStruct((fields + 1, _width(count)), jnp.float32),
+            jax.ShapeDtypeStruct((fields, _width(count)), jnp.float32),
         ),
         in_specs=[_vmem(), _vmem()],
         out_specs=(_vmem(), _vmem(), _vmem(), _vmem()),
@@ -119,8 +118,8 @@
         outs += [
             jax.ShapeDtypeStruct((fields, levels, LANES), jnp.float32),
             jax.ShapeDtypeStruct((fields, levels, LANES), jnp.float32),
-            jax.ShapeDtypeStruct((fields, count), jnp.float32),
-            jax.ShapeDtypeStruct((fields, count), jnp.float32),
+            jax.ShapeDtypeStruct((fields, _width(count)), jnp.float32),
+            jax.ShapeDtypeStruct((fields, _width(count)), jnp.float32),
         ]
     return pl.pallas_call(
         functools.partial(_step_kernel, with_sends),
@@ -138,6 +137,18 @@
     else:
         pairs = [(s, s + steps) for s in range(count) if 0 <= s + steps < count]
     return lax.ppermute(value, axis, pairs)
+
+
+def with_records(cols, recs):
+    flat = recs.reshape(-1)
+    width = cols.shape[1]
+    rows = -(-flat.size // width)
+    flat = jnp.pad(flat, (0, rows * width - flat.size)).reshape(rows, width)
+    return jnp.concatenate([cols, flat], axis=0)
+
+
+def records_of(message, start, shape):
+    return message[start:].reshape(-1)[: shape[0] * shape[1]].reshape(shape)
 
 
 def per_device(tracers, courant, diffusivity, melt_coef, berg_profile, berg_mass, berg_cell,
@@ -157,10 +168,10 @@
         west_out = records[:, west_slots]
         from_s = shift(sn, "lat", 1, False)
         from_n = shift(ss, "lat", -1, False)
-        from_w = shift(se, "lon", 1, True)
-        from_e = shift(sw, "lon", -1, True)
-        east_in = shift(east_out, "lon", 1, True)
-        west_in = shift(west_out, "lon", -1, True)
+        from_w = shift(with_records(se, east_out), "lon", 1, True)
+        from_e = shift(with_records(sw, west_out), "lon", -1, True)
+        east_in = records_of(from_w, se.shape[0], east_out.shape)
+        west_in = records_of(from_e, sw.shape[0], west_out.shape)
         if cs is None:
             cs, cw = from_s, from_w
         records = records.at[:, east_slots].set(east_in)

time: 99.9 us -> 83 us (0.83)
  starting transfers between devices: 52.4 us -> 39.8 us
  Pallas kernels: 21.6 us -> 13.6 us
  other arithmetic: 7.28 us -> 9.48 us
  local copies, waits for them, and re-layouts: 16.8 us -> 18.3 us
    ppermute x12 -> x8, starting transfers between devices: 52.4 us -> 39.8 us  [shift(): return lax.ppermute(value, axis, pairs)]
    pallas_call x2, Pallas kernels: 17.7 us -> 10.7 us  [step(): pl.pallas_call(functools.partial(_step_kernel, with_sends), out_shape=tup...]
    concatenate x0 -> x4, other arithmetic: none -> 2.96 us  [with_records(): return jnp.concatenate([cols, flat], axis=0)]
    pallas_call x1, Pallas kernels: 3.96 us -> 2.85 us  [extract(): pl.pallas_call(_extract_kernel, out_shape=(jax.ShapeDtypeStruct((fields +...]
  transfers between devices with their start and end apart: 12 -> 8, of which waited for: 0 -> 0; matrix products, arithmetic and copies ran while one was open for 19% -> 25% of each run, Pallas kernels for 4% -> 0%
where the time goes in v2:
time: 83 us; the launch traced here: 82.3 us
  starting transfers between devices  39.8 us (48%)
  local copies, waits for them, and re-layouts  18.3 us (22%)
  Pallas kernels  13.6 us (16%)
  other arithmetic  9.48 us (11%)
  between operations  1.14 us (1%)
    ppermute x8, starting transfers between devices, shift(): return lax.ppermute(value, axis, pairs)  39.8 us
    pallas_call x2, Pallas kernels, step(): pl.pallas_call(functools.partial(_step_kernel, with_sends), out_shape=tup...  10.7 us
    scatter-add x2, other arithmetic, per_device(): jnp.zeros((levels, rows * cols), jnp.float32).at[:, berg_cells]  4.2 us
    concatenate x4, other arithmetic, with_records(): return jnp.concatenate([cols, flat], axis=0)  2.96 us
    pallas_call x1, Pallas kernels, extract(): pl.pallas_call(_extract_kernel, out_shape=(jax.ShapeDtypeStruct((fields +...  2.85 us
    unnamed x23, local copies, waits for them, and re-layouts  2.44 us
    gather x2, local copies, waits for them, and re-layouts, per_device(): water_temp = flat_temp[:, berg_cells]  2.25 us
    slice x3, local copies, waits for them, and re-layouts, per_device(): flat_temp = x[0].reshape(levels, rows * cols)  2.21 us
  transfers between devices with their start and end apart: 8, of which 0 were waited for; matrix products, arithmetic and copies ran while one was open for 25% of the time, Pallas kernels for 0%

profile of v2, /device:TPU:7, one launch (start us, length us, event | category | flops | bytes accessed | tf_op | source)
XLA Modules:
  0.0 82.3 jit_solution(4570824019462950194)
XLA Ops:
  0.6 0.8 fusion.23
  1.4 1.0 %copy.20 = f32[75,384]{0,1:T(8,128)S(1)} copy(f32[75,384]{1,0:T(8,128)} %param.13) | data formatting | bytes 230400 | tf_op args[4]
  2.4 0.8 broadcast_in_dim.12
  3.2 0.1 pad_maximum_fusion
  3.4 0.6 gather_fusion.1
  4.0 0.1 copy.24
  4.1 0.1 reshape.250
  4.2 2.8 %shard_map.104 = (f32[6,75,128]{2,1,0:T(8,128)}, f32[5,75,128]{2,1,0:T(8,128)}, f32[6,640]{1,0:T(8,128)}, f32[5,640]{1,0:T(8,128)}) custom-call(f32[5,600,128]{2,1,0:T(8,128)} %bitcast.88, f32[2,600,128]{2,1,0:T(8,128)} %bitcast.90), custom_call_target="tpu_custom_call" | custom-call | tf_op jit(solution)/shard_map/pallas_call | solution.py:100
  7.0 0.7 pad_maximum_fusion.3
  7.8 12.1 %collective-permute-start.1 = (f32[9,640]{1,0:T(8,128)S(1)}, f32[9,640]{1,0:T(8,128)S(1)}, u32[]{:S(2)}, u32[]{:S(2)}) collective-permute-start(f32[9,640]{1,0:T(8,128)S(1)} %pad_maximum_fusion.3), channel_id=1, source_target_pairs={{0,496},{16,0},{32,16},{48,32},{64,48},{80,64},{96,80},{112,96},{1... | collective-permute-start | bytes 69128 | tf_op jit(solution)/shard_map/ppermute | solution.py:139
  19.9 0.6 gather_fusion
  20.5 0.1 copy.22
  20.6 0.1 reshape.248
  20.7 0.7 pad_maximum_fusion.2
  21.5 1.9 %collective-permute-start = (f32[10,640]{1,0:T(8,128)S(1)}, f32[10,640]{1,0:T(8,128)S(1)}, u32[]{:S(2)}, u32[]{:S(2)}) collective-permute-start(f32[10,640]{1,0:T(8,128)S(1)} %pad_maximum_fusion.2), channel_id=1, source_target_pairs={{0,16},{16,32},{32,48},{48,64},{64,80},{80,96},{96,112},{112,128},... | collective-permute-start | bytes 76808 | tf_op jit(solution)/shard_map/ppermute | solution.py:139
  23.4 2.9 %collective-permute-start.2 = (f32[5,75,128]{2,1,0:T(8,128)}, f32[5,75,128]{2,1,0:T(8,128)S(1)}, u32[]{:S(2)}, u32[]{:S(2)}) collective-permute-start(f32[5,75,128]{2,1,0:T(8,128)} %get-tuple-element.13), channel_id=1, source_target_pairs={{1,0},{2,1},{3,2},{4,3},{5,4},{6,5},{7,6},{8,7},{9,8},{10,9},{11,1... | collective-permute-start | bytes 576008 | tf_op jit(solution)/shard_map/ppermute | solution.py:139
  26.3 6.3 %collective-permute-start.3 = (f32[6,75,128]{2,1,0:T(8,128)}, f32[6,75,128]{2,1,0:T(8,128)S(1)}, u32[]{:S(2)}, u32[]{:S(2)}) collective-permute-start(f32[6,75,128]{2,1,0:T(8,128)} %get-tuple-element.14), channel_id=1, source_target_pairs={{0,1},{1,2},{2,3},{3,4},{4,5},{5,6},{6,7},{7,8},{8,9},{9,10},{10,1... | collective-permute-start | bytes 691208 | tf_op jit(solution)/shard_map/ppermute | solution.py:139
  32.6 1.0 %slice.83 = f32[1,75,8,128]{3,2,1,0:T(8,128)S(1)} slice(f32[5,75,8,128]{3,2,1,0:T(8,128)} %param.9), slice={[0:1], [0:75], [0:8], [0:128]} | slice | bytes 614400 | tf_op jit(solution)/shard_map/slice | solution.py:182
  33.7 0.1 broadcast_in_dim.9
  33.8 0.2 copy.26
  34.0 1.1 %gather_fusion.2 = f32[384,75]{1,0:T(8,128)S(1)} fusion(f32[75,1024]{0,1:T(8,128)S(1)} %bitcast.93, s32[1024]{0:T(1024)S(1)} %get-tuple-element.31), kind=kCustom, calls=%fused_computation.2 | custom fusion | bytes 231936 | tf_op jit(solution)/shard_map/gather | solution.py:183
  35.2 0.1 slice.80
  35.3 0.1 copy.25
  35.4 0.1 slice.76
  35.5 0.1 copy.23
  35.6 0.8 scatter_fusion
  36.4 0.8 scatter_fusion.1
  37.1 0.2 sqrt_reduce_fusion.1
  37.4 0.3 fusion.28
  37.6 0.2 reshape_divide_fusion
  37.8 2.1 %scatter_custom_fusion.2 = f32[75,1024]{0,1:T(8,128)S(1)} fusion(s32[384]{0:T(512)S(1)} %get-tuple-element.23, f32[]{:T(128)} %constant.7.clone.1, f32[384,75]{1,0:T(8,128)S(1)} %gather_fusion.2, f32[384]{0:T(512)S(1)} %sqrt_reduce_fusion.1, f32[76,384]{0,1:T(8,128)S(1)} %scatter_fusion.1), kind=kCustom, calls=%fused_computation.16 | custom fusion | flops 288000 | bytes 702468 | tf_op jit(solution)/shard_map/scatter-add | solution.py:185
  40.0 0.1 pad_maximum_fusion.1
  40.1 0.6 gather_fusion.4
  40.7 0.6 gather_fusion.3
  41.2 0.1 copy.29
  41.3 0.1 reshape.253
  41.4 0.1 copy.31
  41.5 0.1 reshape.255
  41.6 0.2 copy.27
  41.8 0.8 reshape.252.src_ref
  42.6 0.9 %broadcast_in_dim.10.d_ref = f32[600,128]{1,0:T(8,128)} broadcast(f32[600]{0:T(1024)S(1)} %broadcast_in_dim.9), dimensions={0} | broadcast | bytes 309600 | tf_op jit(solution)/shard_map/broadcast_in_dim | solution.py:160
  43.5 5.6 %shard_map.105 = (f32[5,600,128]{2,1,0:T(8,128)}, f32[5,75,128]{2,1,0:T(8,128)}, f32[5,75,128]{2,1,0:T(8,128)}, f32[5,640]{1,0:T(8,128)}, f32[5,640]{1,0:T(8,128)}) custom-call(f32[5]{0:T(128)} %coef_ref.3, f32[600,128]{1,0:T(8,128)} %broadcast_in_dim.10.d_ref, f32[5,600,128]{2,1,0:T(8,128)} %bitcast.89, f32[2,600,128]{2,1,0:T(8,128)} %bitcast.91, ...), custom_call_target="tpu_custom_call" | custom-call | tf_op jit(solution)/shard_map/pallas_call | solution.py:124
  49.1 0.7 pad_maximum_fusion.5
  49.9 5.5 %collective-permute-start.5 = (f32[9,640]{1,0:T(8,128)S(1)}, f32[9,640]{1,0:T(8,128)S(1)}, u32[]{:S(2)}, u32[]{:S(2)}) collective-permute-start(f32[9,640]{1,0:T(8,128)S(1)} %pad_maximum_fusion.5), channel_id=1, source_target_pairs={{0,496},{16,0},{32,16},{48,32},{64,48},{80,64},{96,80},{112,96},{1... | collective-permute-start | bytes 69128 | tf_op jit(solution)/shard_map/ppermute | solution.py:139
  55.3 0.7 pad_maximum_fusion.4
  56.1 1.9 %collective-permute-start.4 = (f32[9,640]{1,0:T(8,128)S(1)}, f32[9,640]{1,0:T(8,128)S(1)}, u32[]{:S(2)}, u32[]{:S(2)}) collective-permute-start(f32[9,640]{1,0:T(8,128)S(1)} %pad_maximum_fusion.4), channel_id=1, source_target_pairs={{0,16},{16,32},{32,48},{48,64},{64,80},{80,96},{96,112},{112,128},... | collective-permute-start | bytes 69128 | tf_op jit(solution)/shard_map/ppermute | solution.py:139
  58.0 1.9 %collective-permute-start.6 = (f32[5,75,128]{2,1,0:T(8,128)}, f32[5,75,128]{2,1,0:T(8,128)S(1)}, u32[]{:S(2)}, u32[]{:S(2)}) collective-permute-start(f32[5,75,128]{2,1,0:T(8,128)} %get-tuple-element.18), channel_id=1, source_target_pairs={{1,0},{2,1},{3,2},{4,3},{5,4},{6,5},{7,6},{8,7},{9,8},{10,9},{11,1... | collective-permute-start | bytes 576008 | tf_op jit(solution)/shard_map/ppermute | solution.py:139
  59.9 7.3 %collective-permute-start.7 = (f32[5,75,128]{2,1,0:T(8,128)}, f32[5,75,128]{2,1,0:T(8,128)S(1)}, u32[]{:S(2)}, u32[]{:S(2)}) collective-permute-start(f32[5,75,128]{2,1,0:T(8,128)} %get-tuple-element.19), channel_id=1, source_target_pairs={{0,1},{1,2},{2,3},{3,4},{4,5},{5,6},{6,7},{7,8},{8,9},{9,10},{10,1... | collective-permute-start | bytes 576008 | tf_op jit(solution)/shard_map/ppermute | solution.py:139
  67.2 1.0 %slice.95 = f32[1,600,128]{2,1,0:T(8,128)S(1)} slice(f32[5,600,128]{2,1,0:T(8,128)} %get-tuple-element.15.x_ref), slice={[0:1], [0:600], [0:128]} | slice | bytes 614400 | tf_op jit(solution)/shard_map/slice | solution.py:182
  68.3 0.2 copy.33
  68.5 1.1 %gather_fusion.5 = f32[384,75]{1,0:T(8,128)S(1)} fusion(f32[75,1024]{0,1:T(8,128)S(1)} %copy.33, s32[1024]{0:T(1024)S(1)} %get-tuple-element.30), kind=kCustom, calls=%fused_computation.5 | custom fusion | bytes 231936 | tf_op jit(solution)/shard_map/gather | solution.py:183
  69.6 0.1 slice.92
  69.8 0.1 slice.88
  70.0 0.8 scatter_fusion.2
  70.8 0.8 scatter_fusion.3
  71.6 0.3 slice_reduce_fusion
  71.8 0.3 fusion.24
  72.1 2.1 %scatter_custom_fusion.5 = f32[75,1024]{0,1:T(8,128)S(1)} fusion(s32[384]{0:T(512)S(1)} %get-tuple-element.22, f32[]{:T(128)} %constant.7.clone.1, f32[76,384]{0,1:T(8,128)S(1)} %scatter_fusion.3, f32[384,75]{1,0:T(8,128)S(1)} %gather_fusion.5, f32[384]{0:T(512)S(1)} %get-tuple-element.21), kind=kCustom, calls=%fused_computation.14 | custom fusion | flops 288000 | bytes 702468 | tf_op jit(solution)/shard_map/scatter-add | solution.py:185
  74.2 0.2 copy.34
  74.4 0.8 reshape.257.src_ref
  75.2 0.6 add_divide_fusion
  75.8 0.7 copy-done.3
  76.5 0.7 copy-done.4
  77.2 5.1 %shard_map.106 = f32[5,600,128]{2,1,0:T(8,128)} custom-call(f32[5]{0:T(128)} %coef_ref.3, f32[600,128]{1,0:T(8,128)} %broadcast_in_dim.10.d_ref, f32[5,600,128]{2,1,0:T(8,128)} %get-tuple-element.15.x_ref, f32[2,600,128]{2,1,0:T(8,128)} %bitcast.92, f32[600,128]{1,0:T(8,128)} %reshape.257.src_ref, f32[5,75,128]{2,1,0:T(8,128)} %copy-done.3, ...), custom_call_target="tpu_custom_call" | custom-call | tf_op jit(solution)/shard_map/pallas_call | solution.py:124
  (54 shorter events, 0.5 us)
Async XLA Ops:
  3.2 16.7 %copy-start.9 = (s32[2,32]{1,0:T(2,128)S(1)}, s32[2,32]{1,0:T(2,128)}, u32[]{:S(2)}) copy-start(s32[2,32]{1,0:T(2,128)} %param.16) | copy-start | bytes 772
  3.9 28.6 %copy-start.8 = (s32[2,384]{1,0:T(2,128)S(1)}, s32[2,384]{1,0:T(2,128)}, u32[]{:S(2)}) copy-start(s32[2,384]{1,0:T(2,128)} %param.15) | copy-start | bytes 9220
  4.2 29.5 %copy-start.10 = (f32[75]{0:T(128)S(1)}, f32[75]{0:T(128)}, u32[]{:S(2)}) copy-start(f32[75]{0:T(128)} %param.11) | copy-start | bytes 904
  7.8 27.4 %collective-permute-start.1 = (f32[9,640]{1,0:T(8,128)S(1)}, f32[9,640]{1,0:T(8,128)S(1)}, u32[]{:S(2)}, u32[]{:S(2)}) collective-permute-start(f32[9,640]{1,0:T(8,128)S(1)} %pad_maximum_fusion.3), channel_id=1, source_target_pairs={{0,496},{16,0},{32,16},{48,32},{64,48},{80,64},{96,80},{112,96},{1... | collective-permute-start | bytes 69128 | tf_op jit(solution)/shard_map/ppermute | solution.py:139
  21.5 13.9 %collective-permute-start = (f32[10,640]{1,0:T(8,128)S(1)}, f32[10,640]{1,0:T(8,128)S(1)}, u32[]{:S(2)}, u32[]{:S(2)}) collective-permute-start(f32[10,640]{1,0:T(8,128)S(1)} %pad_maximum_fusion.2), channel_id=1, source_target_pairs={{0,16},{16,32},{32,48},{48,64},{64,80},{80,96},{96,112},{112,128},... | collective-permute-start | bytes 76808 | tf_op jit(solution)/shard_map/ppermute | solution.py:139
  23.4 19.2 %collective-permute-start.2 = (f32[5,75,128]{2,1,0:T(8,128)}, f32[5,75,128]{2,1,0:T(8,128)S(1)}, u32[]{:S(2)}, u32[]{:S(2)}) collective-permute-start(f32[5,75,128]{2,1,0:T(8,128)} %get-tuple-element.13), channel_id=1, source_target_pairs={{1,0},{2,1},{3,2},{4,3},{5,4},{6,5},{7,6},{8,7},{9,8},{10,9},{11,1... | collective-permute-start | bytes 576008 | tf_op jit(solution)/shard_map/ppermute | solution.py:139
  26.3 16.4 %collective-permute-start.3 = (f32[6,75,128]{2,1,0:T(8,128)}, f32[6,75,128]{2,1,0:T(8,128)S(1)}, u32[]{:S(2)}, u32[]{:S(2)}) collective-permute-start(f32[6,75,128]{2,1,0:T(8,128)} %get-tuple-element.14), channel_id=1, source_target_pairs={{0,1},{1,2},{2,3},{3,4},{4,5},{5,6},{6,7},{7,8},{8,9},{9,10},{10,1... | collective-permute-start | bytes 691208 | tf_op jit(solution)/shard_map/ppermute | solution.py:139
  35.2 4.8 %copy-start.5 = (f32[9,640]{1,0:T(8,128)}, f32[9,640]{1,0:T(8,128)S(1)}, u32[]{:S(2)}) copy-start(f32[9,640]{1,0:T(8,128)S(1)} %collective-permute-done.1.fe_ref) | copy-start | bytes 69124
  35.4 4.6 %copy-start.1 = (f32[10,640]{1,0:T(8,128)}, f32[10,640]{1,0:T(8,128)S(1)}, u32[]{:S(2)}) copy-start(f32[10,640]{1,0:T(8,128)S(1)} %collective-permute-done.fw_ref.cw_ref) | copy-start | bytes 76804
  42.6 0.9 %copy-start.2 = (f32[5,75,128]{2,1,0:T(8,128)}, f32[5,75,128]{2,1,0:T(8,128)S(1)}, u32[]{:S(2)}) copy-start(f32[5,75,128]{2,1,0:T(8,128)S(1)} %collective-permute-done.2.fn_ref) | copy-start | bytes 576004
  42.6 0.9 %copy-start = (f32[6,75,128]{2,1,0:T(8,128)}, f32[6,75,128]{2,1,0:T(8,128)S(1)}, u32[]{:S(2)}) copy-start(f32[6,75,128]{2,1,0:T(8,128)S(1)} %collective-permute-done.3.fs_ref.cs_ref) | copy-start | bytes 691204
  49.9 19.7 %collective-permute-start.5 = (f32[9,640]{1,0:T(8,128)S(1)}, f32[9,640]{1,0:T(8,128)S(1)}, u32[]{:S(2)}, u32[]{:S(2)}) collective-permute-start(f32[9,640]{1,0:T(8,128)S(1)} %pad_maximum_fusion.5), channel_id=1, source_target_pairs={{0,496},{16,0},{32,16},{48,32},{64,48},{80,64},{96,80},{112,96},{1... | collective-permute-start | bytes 69128 | tf_op jit(solution)/shard_map/ppermute | solution.py:139
  56.1 13.7 %collective-permute-start.4 = (f32[9,640]{1,0:T(8,128)S(1)}, f32[9,640]{1,0:T(8,128)S(1)}, u32[]{:S(2)}, u32[]{:S(2)}) collective-permute-start(f32[9,640]{1,0:T(8,128)S(1)} %pad_maximum_fusion.4), channel_id=1, source_target_pairs={{0,16},{16,32},{32,48},{48,64},{64,80},{80,96},{96,112},{112,128},... | collective-permute-start | bytes 69128 | tf_op jit(solution)/shard_map/ppermute | solution.py:139
  58.0 17.8 %collective-permute-start.6 = (f32[5,75,128]{2,1,0:T(8,128)}, f32[5,75,128]{2,1,0:T(8,128)S(1)}, u32[]{:S(2)}, u32[]{:S(2)}) collective-permute-start(f32[5,75,128]{2,1,0:T(8,128)} %get-tuple-element.18), channel_id=1, source_target_pairs={{1,0},{2,1},{3,2},{4,3},{5,4},{6,5},{7,6},{8,7},{9,8},{10,9},{11,1... | collective-permute-start | bytes 576008 | tf_op jit(solution)/shard_map/ppermute | solution.py:139
  59.9 15.9 %collective-permute-start.7 = (f32[5,75,128]{2,1,0:T(8,128)}, f32[5,75,128]{2,1,0:T(8,128)S(1)}, u32[]{:S(2)}, u32[]{:S(2)}) collective-permute-start(f32[5,75,128]{2,1,0:T(8,128)} %get-tuple-element.19), channel_id=1, source_target_pairs={{0,1},{1,2},{2,3},{3,4},{4,5},{5,6},{6,7},{7,8},{8,9},{9,10},{10,1... | collective-permute-start | bytes 576008 | tf_op jit(solution)/shard_map/ppermute | solution.py:139
  69.6 4.6 %copy-start.6 = (f32[9,640]{1,0:T(8,128)}, f32[9,640]{1,0:T(8,128)S(1)}, u32[]{:S(2)}) copy-start(f32[9,640]{1,0:T(8,128)S(1)} %collective-permute-done.5.fe_ref) | copy-start | bytes 69124
  69.8 4.4 %copy-start.7 = (f32[9,640]{1,0:T(8,128)}, f32[9,640]{1,0:T(8,128)S(1)}, u32[]{:S(2)}) copy-start(f32[9,640]{1,0:T(8,128)S(1)} %collective-permute-done.4.fw_ref) | copy-start | bytes 69124
  75.8 0.7 copy-start.3
  76.5 0.7 copy-start.4

commit v3 on v2

v3 whole, which is shorter than its diff:
```python
import functools

import jax
import jax.numpy as jnp
from jax import lax
from jax.experimental import pallas as pl
from jax.experimental.pallas import tpu as pltpu
from jax.sharding import PartitionSpec as P

STEPS = 2
LANES = 128
HI = lax.Precision.HIGHEST
REC_ROW = 32
MSG_ROWS = 112


def _dot(a, b, dims):
    return lax.dot_general(a, b, (dims, ((), ())), precision=HI, preferred_element_type=jnp.float32)


def _pieces(count):
    return -(-count // LANES)


def _columns(block):
    count = block.shape[0]
    width = _pieces(count) * LANES
    padded = jnp.concatenate([block, jnp.zeros((width - count, LANES), jnp.float32)], axis=0)
    return padded.T


def _put_column(msg_ref, slot, vector):
    pieces = vector.shape[1] // LANES
    for j in range(pieces):
        row = slot * pieces + j
        msg_ref[row:row + 1, :] = vector[:, j * LANES:(j + 1) * LANES]


def _get_column(msg_ref, slot, pieces):
    return jnp.concatenate(
        [msg_ref[slot * pieces + j:slot * pieces + j + 1, :] for j in range(pieces)], axis=1)


def _column_matrix(west, east, count):
    width = west.shape[-1]
    r = lax.broadcasted_iota(jnp.int32, (LANES, width), 0)
    grid = jnp.where(r == 0, west, jnp.where(r == LANES - 1, east, 0.0))
    return grid.T[:count]


def _one_hot(index_row, size):
    n = index_row.shape[1]
    return jnp.where(lax.broadcasted_iota(jnp.int32, (size, n), 0) == index_row, 1.0, 0.0)


def _send_records(msg_ref, prof, mass, index_row):
    slots = prof.shape[1]
    hot = _one_hot(index_row, slots)
    levels = prof.shape[0]
    cross = index_row.shape[1]
    msg_ref[REC_ROW:REC_ROW + levels, 0:cross] = _dot(prof, hot, ((1,), (0,)))
    msg_ref[REC_ROW + levels:REC_ROW + levels + 1, 0:cross] = _dot(mass, hot, ((1,), (0,)))


def _prep_kernel(x_ref, c_ref, p_ref, m_ref, ie_ref, iw_ref, sn_ref, ss_ref, me_ref, mw_ref):
    fields, count, _ = x_ref.shape
    levels = count // 8
    me_ref[...] = jnp.zeros(me_ref.shape, jnp.float32)
    mw_ref[...] = jnp.zeros(mw_ref.shape, jnp.float32)
    for f in range(fields):
        cols = _columns(x_ref[f])
        _put_column(me_ref, f, cols[LANES - 1:LANES])
        _put_column(mw_ref, f, cols[0:1])
        sn_ref[f] = x_ref[f, pl.ds(7, levels, stride=8), :]
        ss_ref[f] = x_ref[f, pl.ds(0, levels, stride=8), :]
    ucols = _columns(c_ref[0])
    _put_column(me_ref, fields, ucols[LANES - 1:LANES])
    sn_ref[fields] = c_ref[1, pl.ds(7, levels, stride=8), :]
    prof = p_ref[...]
    mass = m_ref[...]
    _send_records(me_ref, prof, mass, ie_ref[0:1, :])
    _send_records(mw_ref, prof, mass, iw_ref[0:1, :])


def _step_kernel(step_index, with_sends, coef_ref, d_ref, x_ref, c_ref, p_ref, m_ref, cell_ref,
                 ie_ref, iw_ref, fn_ref, fs_ref, fw_ref, fe_ref, cs_ref, cw_ref, *rest):
    if with_sends:
        o_ref, po_ref, mo_ref, sn_ref, ss_ref, me_ref, mw_ref, hscr, sscr, dscr = rest
    else:
        o_ref, po_ref, mo_ref, hscr, sscr, dscr = rest
    fields, count, _ = x_ref.shape
    levels = count // 8
    pieces = _pieces(count)
    slots = p_ref.shape[1]
    cross = ie_ref.shape[1]
    cells = 8 * LANES

    hot_e = _one_hot(ie_ref[step_index:step_index + 1, :], slots)
    hot_w = _one_hot(iw_ref[step_index:step_index + 1, :], slots)
    rec_e = fw_ref[REC_ROW:REC_ROW + levels + 1, 0:cross]
    rec_w = fe_ref[REC_ROW:REC_ROW + levels + 1, 0:cross]
    placed = _dot(rec_e, hot_e, ((1,), (1,))) + _dot(rec_w, hot_w, ((1,), (1,)))
    taken = _dot(jnp.ones((8, cross), jnp.float32), hot_e + hot_w, ((1,), (1,)))[0:1]
    moved = taken > 0.5
    prof = jnp.where(moved, placed[:levels], p_ref[...])
    mass = jnp.where(moved, placed[levels:levels + 1], m_ref[...])

    temp = jnp.concatenate([x_ref[0, pl.ds(r, levels, stride=8), :] for r in range(8)], axis=1)
    hot_c = _one_hot(cell_ref[step_index:step_index + 1, :], cells)
    water = _dot(temp, hot_c, ((1,), (0,)))
    z = water + 1.8
    soft = jnp.maximum(z, 0.0) + jnp.log1p(jnp.exp(-jnp.abs(z)))
    melt = prof * soft * jnp.sqrt(mass)
    source = _dot(melt, hot_c, ((1,), (1,)))
    mass_new = mass / (1.0 + 0.05 * jnp.sum(melt, axis=0, keepdims=True))
    po_ref[...] = prof
    mo_ref[...] = mass_new
    for r in range(8):
        sscr[pl.ds(r, levels, stride=8), :] = source[:, r * LANES:(r + 1) * LANES]
        dscr[pl.ds(r, levels, stride=8), :] = jnp.broadcast_to(d_ref[...], (levels, LANES))

    rows = lax.broadcasted_iota(jnp.int32, (count, LANES), 0) % 8
    lanes = lax.broadcasted_iota(jnp.int32, (count, LANES), 1)
    u = c_ref[0]
    v = c_ref[1]
    d = dscr[...]
    zero_row = jnp.zeros((1, pieces * LANES), jnp.float32)
    u_halo = _column_matrix(_get_column(cw_ref, fields, pieces), zero_row, count)
    u_w = jnp.where(lanes == 0, u_halo, pltpu.roll(u, 1, 1))
    hscr[pl.ds(0, levels, stride=8), :] = cs_ref[fields]
    v_s = jnp.where(rows == 0, hscr[...], pltpu.roll(v, 1, 0))
    a_c = 1.0 - jnp.maximum(u, 0.0) + jnp.minimum(u_w, 0.0) - jnp.maximum(v, 0.0) + jnp.minimum(v_s, 0.0) - 4.0 * d
    a_e = d - jnp.minimum(u, 0.0)
    a_w = d + jnp.maximum(u_w, 0.0)
    a_n = d - jnp.minimum(v, 0.0)
    a_s = d + jnp.maximum(v_s, 0.0)
    src = sscr[...]
    if with_sends:
        me_ref[...] = jnp.zeros(me_ref.shape, jnp.float32)
        mw_ref[...] = jnp.zeros(mw_ref.shape, jnp.float32)
    for f in range(fields):
        c = x_ref[f]
        halo = _column_matrix(_get_column(fw_ref, f, pieces), _get_column(fe_ref, f, pieces), count)
        east = jnp.where(lanes == LANES - 1, halo, pltpu.roll(c, LANES - 1, 1))
        west = jnp.where(lanes == 0, halo, pltpu.roll(c, 1, 1))
        hscr[pl.ds(7, levels, stride=8), :] = fn_ref[f]
        hscr[pl.ds(0, levels, stride=8), :] = fs_ref[f]
        hrow = hscr[...]
        north = jnp.where(rows == 7, hrow, pltpu.roll(c, count - 1, 0))
        south = jnp.where(rows == 0, hrow, pltpu.roll(c, 1, 0))
        out = a_c * c + a_e * east + a_w * west + a_n * north + a_s * south + coef_ref[f] * src
        o_ref[f] = out
        if with_sends:
            cols = _columns(out)
            _put_column(me_ref, f, cols[LANES - 1:LANES])
            _put_column(mw_ref, f, cols[0:1])
            sn_ref[f] = o_ref[f, pl.ds(7, levels, stride=8), :]
            ss_ref[f] = o_ref[f, pl.ds(0, levels, stride=8), :]
    if with_sends:
        nxt = step_index + 1
        _send_records(me_ref, prof, mass_new, ie_ref[nxt:nxt + 1, :])
        _send_records(mw_ref, prof, mass_new, iw_ref[nxt:nxt + 1, :])


def _vmem():
    return pl.BlockSpec(memory_space=pltpu.VMEM)


def _f32(shape):
    return jax.ShapeDtypeStruct(shape, jnp.float32)


def prep(x, c, prof, mass, ie, iw):
    fields, count, _ = x.shape
    levels = count // 8
    return pl.pallas_call(
        _prep_kernel,
        out_shape=(
            _f32((fields + 1, levels, LANES)),
            _f32((fields, levels, LANES)),
            _f32((MSG_ROWS, LANES)),
            _f32((MSG_ROWS, LANES)),
        ),
        in_specs=[_vmem()] * 6,
        out_specs=tuple(_vmem() for _ in range(4)),
    )(x, c, prof, mass, ie, iw)


def step(step_index, with_sends, coef, d, x, c, prof, mass, cell, ie, iw, fn, fs, fw, fe, cs, cw):
    fields, count, _ = x.shape
    levels = count // 8
    outs = [_f32(x.shape), _f32(prof.shape), _f32(mass.shape)]
    if with_sends:
        outs += [
            _f32((fields, levels, LANES)),
            _f32((fields, levels, LANES)),
            _f32((MSG_ROWS, LANES)),
            _f32((MSG_ROWS, LANES)),
        ]
    return pl.pallas_call(
        functools.partial(_step_kernel, step_index, with_sends),
        out_shape=tuple(outs),
        in_specs=[pl.BlockSpec(memory_space=pltpu.SMEM)] + [_vmem()] * 14,
        out_specs=tuple(_vmem() for _ in outs),
        scratch_shapes=[pltpu.VMEM((count, LANES), jnp.float32)] * 3,
    )(coef, d, x, c, prof, mass, cell, ie, iw, fn, fs, fw, fe, cs, cw)


def shift(value, axis, steps, periodic):
    count = lax.axis_size(axis)
    if periodic:
        pairs = [(s, (s + steps) % count) for s in range(count)]
    else:
        pairs = [(s, s + steps) for s in range(count) if 0 <= s + steps < count]
    return lax.ppermute(value, axis, pairs)


def per_device(tracers, courant, diffusivity, melt_coef, berg_profile, berg_mass, berg_cell,
               send_east, send_west):
    fields, levels, rows, cols = tracers.shape
    count = levels * rows
    x = tracers.reshape(fields, count, cols)
    c = courant.reshape(2, count, cols)
    d = diffusivity.reshape(levels, 1)
    prof = berg_profile
    mass = berg_mass.reshape(1, -1)
    sn, ss, me, mw = prep(x, c, prof, mass, send_east, send_west)
    cs = cw = None
    for step_index in range(STEPS):
        from_s = shift(sn, "lat", 1, False)
        from_n = shift(ss, "lat", -1, False)
        from_w = shift(me, "lon", 1, True)
        from_e = shift(mw, "lon", -1, True)
        if cs is None:
            cs, cw = from_s, from_w
        with_sends = step_index < STEPS - 1
        result = step(step_index, with_sends, melt_coef, d, x, c, prof, mass, berg_cell, send_east,
                      send_west, from_n, from_s, from_w, from_e, cs, cw)
        if with_sends:
            x, prof, mass, sn, ss, me, mw = result
        else:
            x, prof, mass = result
    return (x.reshape(fields, levels, rows, cols), mass.reshape(-1))


def solution(mesh):
    in_specs = (
        P(None, None, "lat", "lon"),
        P(None, None, "lat", "lon"),
        P(),
        P(),
        P(None, ("lon", "lat")),
        P(("lon", "lat")),
        P(None, ("lon", "lat")),
        P(None, ("lon", "lat")),
        P(None, ("lon", "lat")),
    )
    out_specs = (P(None, None, "lat", "lon"), P(("lon", "lat")))
    return jax.shard_map(
        per_device, mesh=mesh, in_specs=in_specs, out_specs=out_specs, check_vma=False
    )
```

time: 83 us -> 65.8 us (0.79)
  local copies, waits for them, and re-layouts: 18.3 us -> 4.14 us
  other arithmetic: 9.48 us -> 1.23 us
  Pallas kernels: 13.6 us -> 18.5 us
  waiting for transfers between devices: 0.02 us -> 2.47 us
  starting transfers between devices: 39.8 us -> 38.3 us
    gather x10 -> x0, local copies, waits for them, and re-layouts: 4.93 us -> none  [the longest x2 2.25 us: per_device(): water_temp = flat_temp[:, berg_cells]]
    pallas_call x3, Pallas kernels: 13.6 us -> 18.5 us  [the longest x2 15.5 us: step(): pl.pallas_call(functools.partial(_step_kernel, step_index, with_sends), o...]
    scatter-add x2 -> x0, other arithmetic: 4.2 us -> none  [per_device(): jnp.zeros((levels, rows * cols), jnp.float32).at[:, berg_cells]]
    concatenate x6 -> x0, other arithmetic: 3.2 us -> none  [the longest x4 2.96 us: with_records(): return jnp.concatenate([cols, flat], axis=0)]
    slice x20 -> x0, local copies, waits for them, and re-layouts: 3.14 us -> none  [the longest x3 2.21 us: per_device(): flat_temp = x[0].reshape(levels, rows * cols)]
    scatter x4 -> x0, local copies, waits for them, and re-layouts: 3.11 us -> none  [the longest x2 1.56 us: per_device(): records = records.at[:, west_slots].set(west_in)]
    ppermute x8, waiting for transfers between devices: 0.02 us -> 2.47 us  [shift(): return lax.ppermute(value, axis, pairs)]
    broadcast_in_dim x4 -> x0, local copies, waits for them, and re-layouts: 1.82 us -> none  [the longest x3 1.03 us: per_device(): jnp.broadcast_to(diffusivity[:, None, None], (levels, rows, cols))]
  transfers between devices with their start and end apart: 8 -> 8, of which waited for: 0 -> 2; matrix products, arithmetic and copies ran while one was open for 25% -> 1% of each run, Pallas kernels for 0% -> 0%
where the time goes in v3:
time: 65.8 us; the launch traced here: 65.4 us
  starting transfers between devices  38.3 us (58%)
  Pallas kernels  18.5 us (28%)
  local copies, waits for them, and re-layouts  4.14 us (6%)
  waiting for transfers between devices  2.47 us (4%)
  other arithmetic  1.23 us (2%)
  between operations  0.77 us (1%)
    ppermute x8, starting transfers between devices, shift(): return lax.ppermute(value, axis, pairs)  38.3 us
    pallas_call x2, Pallas kernels, step(): pl.pallas_call(functools.partial(_step_kernel, step_index, with_sends), o...  15.5 us
    pallas_call x1, Pallas kernels, prep(): pl.pallas_call(_prep_kernel, out_shape=(_f32((fields + 1, levels, LANES))...  3 us
    ppermute x8, waiting for transfers between devices, shift(): return lax.ppermute(value, axis, pairs)  2.47 us
    unnamed x18, local copies, waits for them, and re-layouts  2.18 us
  transfers between devices with their start and end apart: 8, of which 2 were waited for; matrix products, arithmetic and copies ran while one was open for 1% of the time, Pallas kernels for 0%

profile of v3, /device:TPU:7, one launch (start us, length us, event | category | flops | bytes accessed | tf_op | source)
XLA Modules:
  0.0 65.4 jit_solution(12022970135180967988)
XLA Ops:
  0.6 0.0 copy-start.8
  0.6 1.3 %reshape.25.m_ref = f32[1,384]{1,0:T(1,128)} reshape(f32[384]{0:T(512)} %param.14) | data formatting | bytes 3072 | tf_op jit(solution)/shard_map/reshape | solution.py:226
  1.9 3.0 %shard_map.104 = (f32[6,75,128]{2,1,0:T(8,128)}, f32[5,75,128]{2,1,0:T(8,128)}, f32[112,128]{1,0:T(8,128)}, f32[112,128]{1,0:T(8,128)}) custom-call(f32[5,600,128]{2,1,0:T(8,128)} %bitcast.4, f32[2,600,128]{2,1,0:T(8,128)} %bitcast.6, f32[75,384]{1,0:T(8,128)} %p_ref.3, f32[1,384]{1,0:T(1,128)} %reshape.25.m_ref, s32[2,32]{1,0:T(2,128)} %ie_ref.5, ...), custom_call_target="tpu_custom_call" | custom-call | tf_op jit(solution)/shard_map/pallas_call | solution.py:176
  4.9 5.3 %collective-permute-start.1 = (f32[6,75,128]{2,1,0:T(8,128)}, f32[6,75,128]{2,1,0:T(8,128)S(1)}, u32[]{:S(2)}, u32[]{:S(2)}) collective-permute-start(f32[6,75,128]{2,1,0:T(8,128)} %get-tuple-element.16), channel_id=1, source_target_pairs={{0,1},{1,2},{2,3},{3,4},{4,5},{5,6},{6,7},{7,8},{8,9},{9,10},{10,1... | collective-permute-start | bytes 691208 | tf_op jit(solution)/shard_map/ppermute | solution.py:215
  10.2 1.9 %collective-permute-start = (f32[5,75,128]{2,1,0:T(8,128)}, f32[5,75,128]{2,1,0:T(8,128)S(1)}, u32[]{:S(2)}, u32[]{:S(2)}) collective-permute-start(f32[5,75,128]{2,1,0:T(8,128)} %get-tuple-element.15), channel_id=1, source_target_pairs={{1,0},{2,1},{3,2},{4,3},{5,4},{6,5},{7,6},{8,7},{9,8},{10,9},{11,1... | collective-permute-start | bytes 576008 | tf_op jit(solution)/shard_map/ppermute | solution.py:215
  12.1 3.5 %collective-permute-start.2 = (f32[112,128]{1,0:T(8,128)}, f32[112,128]{1,0:T(8,128)S(1)}, u32[]{:S(2)}, u32[]{:S(2)}) collective-permute-start(f32[112,128]{1,0:T(8,128)} %get-tuple-element.17), channel_id=1, source_target_pairs={{0,16},{16,32},{32,48},{48,64},{64,80},{80,96},{96,112},{112,128},... | collective-permute-start | bytes 172040 | tf_op jit(solution)/shard_map/ppermute | solution.py:215
  15.7 9.6 %collective-permute-start.3 = (f32[112,128]{1,0:T(8,128)}, f32[112,128]{1,0:T(8,128)S(1)}, u32[]{:S(2)}, u32[]{:S(2)}) collective-permute-start(f32[112,128]{1,0:T(8,128)} %get-tuple-element.18), channel_id=1, source_target_pairs={{0,496},{16,0},{32,16},{48,32},{64,48},{80,64},{96,80},{112,96},{1... | collective-permute-start | bytes 172040 | tf_op jit(solution)/shard_map/ppermute | solution.py:215
  25.3 0.0 copy-done.8
  25.3 0.7 %copy.12.d_ref = f32[75,1]{1,0:T(8,128)} copy(f32[75,1]{0,1:T(1,128)S(1)} %bitcast.9) | data formatting | bytes 600 | tf_op jit(solution)/shard_map/reshape | solution.py:224
  26.0 0.0 collective-permute-done.2.fw_ref.cw_ref
  26.0 0.0 copy-start.1
  26.0 0.9 %collective-permute-done.3.fe_ref = f32[112,128]{1,0:T(8,128)S(1)} collective-permute-done((f32[112,128]{1,0:T(8,128)}, f32[112,128]{1,0:T(8,128)S(1)}, u32[]{:S(2)}, u32[]{:S(2)}) %collective-permute-start.3) | collective-permute-done | bytes 57376 | tf_op jit(solution)/shard_map/ppermute | solution.py:215
  26.9 0.0 copy-start.7
  26.9 0.0 collective-permute-done.fn_ref
  26.9 0.0 copy-start.4
  26.9 0.0 collective-permute-done.1.fs_ref.cs_ref
  26.9 0.0 copy-done.1
  27.0 0.6 copy-done.7
  27.6 0.1 copy-done.4
  27.6 0.0 copy-start
  27.7 0.7 %copy-done = f32[6,75,128]{2,1,0:T(8,128)} copy-done((f32[6,75,128]{2,1,0:T(8,128)}, f32[6,75,128]{2,1,0:T(8,128)S(1)}, u32[]{:S(2)}) %copy-start) | copy-done | bytes 230424
  28.4 8.0 %shard_map.105 = (f32[5,600,128]{2,1,0:T(8,128)}, f32[75,384]{1,0:T(8,128)}, f32[1,384]{1,0:T(1,128)}, f32[5,75,128]{2,1,0:T(8,128)}, f32[5,75,128]{2,1,0:T(8,12...) custom-call(f32[5]{0:T(128)} %coef_ref.3, f32[75,1]{1,0:T(8,128)} %copy.12.d_ref, f32[5,600,128]{2,1,0:T(8,128)} %bitcast.5, ...), custom_call_target="tpu_custom_call" | custom-call | tf_op jit(solution)/shard_map/pallas_call | solution.py:200
  36.3 2.7 %collective-permute-start.4 = (f32[5,75,128]{2,1,0:T(8,128)}, f32[5,75,128]{2,1,0:T(8,128)S(1)}, u32[]{:S(2)}, u32[]{:S(2)}) collective-permute-start(f32[5,75,128]{2,1,0:T(8,128)} %get-tuple-element.22), channel_id=1, source_target_pairs={{1,0},{2,1},{3,2},{4,3},{5,4},{6,5},{7,6},{8,7},{9,8},{10,9},{11,1... | collective-permute-start | bytes 576008 | tf_op jit(solution)/shard_map/ppermute | solution.py:215
  39.0 7.9 %collective-permute-start.5 = (f32[5,75,128]{2,1,0:T(8,128)}, f32[5,75,128]{2,1,0:T(8,128)S(1)}, u32[]{:S(2)}, u32[]{:S(2)}) collective-permute-start(f32[5,75,128]{2,1,0:T(8,128)} %get-tuple-element.23), channel_id=1, source_target_pairs={{0,1},{1,2},{2,3},{3,4},{4,5},{5,6},{6,7},{7,8},{8,9},{9,10},{10,1... | collective-permute-start | bytes 576008 | tf_op jit(solution)/shard_map/ppermute | solution.py:215
  46.9 1.9 %collective-permute-start.6 = (f32[112,128]{1,0:T(8,128)}, f32[112,128]{1,0:T(8,128)S(1)}, u32[]{:S(2)}, u32[]{:S(2)}) collective-permute-start(f32[112,128]{1,0:T(8,128)} %get-tuple-element.24), channel_id=1, source_target_pairs={{0,16},{16,32},{32,48},{48,64},{64,80},{80,96},{96,112},{112,128},... | collective-permute-start | bytes 172040 | tf_op jit(solution)/shard_map/ppermute | solution.py:215
  48.8 5.5 %collective-permute-start.7 = (f32[112,128]{1,0:T(8,128)}, f32[112,128]{1,0:T(8,128)S(1)}, u32[]{:S(2)}, u32[]{:S(2)}) collective-permute-start(f32[112,128]{1,0:T(8,128)} %get-tuple-element.25), channel_id=1, source_target_pairs={{0,496},{16,0},{32,16},{48,32},{64,48},{80,64},{96,80},{112,96},{1... | collective-permute-start | bytes 172040 | tf_op jit(solution)/shard_map/ppermute | solution.py:215
  54.3 0.0 collective-permute-done.6.fw_ref
  54.3 0.0 copy-start.5
  54.3 1.5 %collective-permute-done.7.fe_ref = f32[112,128]{1,0:T(8,128)S(1)} collective-permute-done((f32[112,128]{1,0:T(8,128)}, f32[112,128]{1,0:T(8,128)S(1)}, u32[]{:S(2)}, u32[]{:S(2)}) %collective-permute-start.7) | collective-permute-done | bytes 57376 | tf_op jit(solution)/shard_map/ppermute | solution.py:215
  55.8 0.0 copy-start.6
  55.8 0.0 collective-permute-done.4.fn_ref
  55.8 0.0 copy-start.2
  55.8 0.0 collective-permute-done.5.fs_ref
  55.9 0.0 copy-start.3
  55.9 0.0 copy-done.5
  55.9 0.6 copy-done.6
  56.5 0.1 copy-done.2
  56.6 0.1 copy-done.3
  56.6 7.5 %shard_map.106 = (f32[5,600,128]{2,1,0:T(8,128)}, f32[75,384]{1,0:T(8,128)}, f32[1,384]{1,0:T(1,128)}) custom-call(f32[5]{0:T(128)} %coef_ref.3, f32[75,1]{1,0:T(8,128)} %copy.12.d_ref, f32[5,600,128]{2,1,0:T(8,128)} %get-tuple-element.19.x_ref, f32[2,600,128]{2,1,0:T(8,128)} %bitcast.8, f32[75,384]{1,0:T(8,128)} %get-tuple-element.20.p_ref, ...), custom_call_target="tpu_custom_call" | custom-call | tf_op jit(solution)/shard_map/pallas_call | solution.py:200
  64.2 1.2 %reduce = f32[384]{0:T(512)} reduce(f32[1,384]{1,0:T(1,128)} %get-tuple-element.27, f32[]{:T(128)} %constant.7), dimensions={0}, to_apply=%get-tuple-element.27.reduce_sub_computation | reduce | bytes 3076 | tf_op jit(solution)/shard_map/pallas_call | solution.py:200
Async XLA Ops:
  0.6 24.7 %copy-start.8 = (f32[75]{0:T(128)S(1)}, f32[75]{0:T(128)}, u32[]{:S(2)}) copy-start(f32[75]{0:T(128)} %param.11) | copy-start | bytes 904
  4.9 22.1 %collective-permute-start.1 = (f32[6,75,128]{2,1,0:T(8,128)}, f32[6,75,128]{2,1,0:T(8,128)S(1)}, u32[]{:S(2)}, u32[]{:S(2)}) collective-permute-start(f32[6,75,128]{2,1,0:T(8,128)} %get-tuple-element.16), channel_id=1, source_target_pairs={{0,1},{1,2},{2,3},{3,4},{4,5},{5,6},{6,7},{7,8},{8,9},{9,10},{10,1... | collective-permute-start | bytes 691208 | tf_op jit(solution)/shard_map/ppermute | solution.py:215
  10.2 16.8 %collective-permute-start = (f32[5,75,128]{2,1,0:T(8,128)}, f32[5,75,128]{2,1,0:T(8,128)S(1)}, u32[]{:S(2)}, u32[]{:S(2)}) collective-permute-start(f32[5,75,128]{2,1,0:T(8,128)} %get-tuple-element.15), channel_id=1, source_target_pairs={{1,0},{2,1},{3,2},{4,3},{5,4},{6,5},{7,6},{8,7},{9,8},{10,9},{11,1... | collective-permute-start | bytes 576008 | tf_op jit(solution)/shard_map/ppermute | solution.py:215
  12.1 13.9 %collective-permute-start.2 = (f32[112,128]{1,0:T(8,128)}, f32[112,128]{1,0:T(8,128)S(1)}, u32[]{:S(2)}, u32[]{:S(2)}) collective-permute-start(f32[112,128]{1,0:T(8,128)} %get-tuple-element.17), channel_id=1, source_target_pairs={{0,16},{16,32},{32,48},{48,64},{64,80},{80,96},{96,112},{112,128},... | collective-permute-start | bytes 172040 | tf_op jit(solution)/shard_map/ppermute | solution.py:215
  15.7 11.3 %collective-permute-start.3 = (f32[112,128]{1,0:T(8,128)}, f32[112,128]{1,0:T(8,128)S(1)}, u32[]{:S(2)}, u32[]{:S(2)}) collective-permute-start(f32[112,128]{1,0:T(8,128)} %get-tuple-element.18), channel_id=1, source_target_pairs={{0,496},{16,0},{32,16},{48,32},{64,48},{80,64},{96,80},{112,96},{1... | collective-permute-start | bytes 172040 | tf_op jit(solution)/shard_map/ppermute | solution.py:215
  26.0 0.9 %copy-start.1 = (f32[112,128]{1,0:T(8,128)}, f32[112,128]{1,0:T(8,128)S(1)}, u32[]{:S(2)}) copy-start(f32[112,128]{1,0:T(8,128)S(1)} %collective-permute-done.2.fw_ref.cw_ref) | copy-start | bytes 172036
  26.9 0.6 copy-start.7
  26.9 0.7 %copy-start.4 = (f32[5,75,128]{2,1,0:T(8,128)}, f32[5,75,128]{2,1,0:T(8,128)S(1)}, u32[]{:S(2)}) copy-start(f32[5,75,128]{2,1,0:T(8,128)S(1)} %collective-permute-done.fn_ref) | copy-start | bytes 576004
  27.6 0.7 %copy-start = (f32[6,75,128]{2,1,0:T(8,128)}, f32[6,75,128]{2,1,0:T(8,128)S(1)}, u32[]{:S(2)}) copy-start(f32[6,75,128]{2,1,0:T(8,128)S(1)} %collective-permute-done.1.fs_ref.cs_ref) | copy-start | bytes 691204
  36.3 19.5 %collective-permute-start.4 = (f32[5,75,128]{2,1,0:T(8,128)}, f32[5,75,128]{2,1,0:T(8,128)S(1)}, u32[]{:S(2)}, u32[]{:S(2)}) collective-permute-start(f32[5,75,128]{2,1,0:T(8,128)} %get-tuple-element.22), channel_id=1, source_target_pairs={{1,0},{2,1},{3,2},{4,3},{5,4},{6,5},{7,6},{8,7},{9,8},{10,9},{11,1... | collective-permute-start | bytes 576008 | tf_op jit(solution)/shard_map/ppermute | solution.py:215
  39.0 16.8 %collective-permute-start.5 = (f32[5,75,128]{2,1,0:T(8,128)}, f32[5,75,128]{2,1,0:T(8,128)S(1)}, u32[]{:S(2)}, u32[]{:S(2)}) collective-permute-start(f32[5,75,128]{2,1,0:T(8,128)} %get-tuple-element.23), channel_id=1, source_target_pairs={{0,1},{1,2},{2,3},{3,4},{4,5},{5,6},{6,7},{7,8},{8,9},{9,10},{10,1... | collective-permute-start | bytes 576008 | tf_op jit(solution)/shard_map/ppermute | solution.py:215
  46.9 7.4 %collective-permute-start.6 = (f32[112,128]{1,0:T(8,128)}, f32[112,128]{1,0:T(8,128)S(1)}, u32[]{:S(2)}, u32[]{:S(2)}) collective-permute-start(f32[112,128]{1,0:T(8,128)} %get-tuple-element.24), channel_id=1, source_target_pairs={{0,16},{16,32},{32,48},{48,64},{64,80},{80,96},{96,112},{112,128},... | collective-permute-start | bytes 172040 | tf_op jit(solution)/shard_map/ppermute | solution.py:215
  48.8 7.0 %collective-permute-start.7 = (f32[112,128]{1,0:T(8,128)}, f32[112,128]{1,0:T(8,128)S(1)}, u32[]{:S(2)}, u32[]{:S(2)}) collective-permute-start(f32[112,128]{1,0:T(8,128)} %get-tuple-element.25), channel_id=1, source_target_pairs={{0,496},{16,0},{32,16},{48,32},{64,48},{80,64},{96,80},{112,96},{1... | collective-permute-start | bytes 172040 | tf_op jit(solution)/shard_map/ppermute | solution.py:215
  54.3 1.6 %copy-start.5 = (f32[112,128]{1,0:T(8,128)}, f32[112,128]{1,0:T(8,128)S(1)}, u32[]{:S(2)}) copy-start(f32[112,128]{1,0:T(8,128)S(1)} %collective-permute-done.6.fw_ref) | copy-start | bytes 172036
  55.8 0.6 copy-start.6
  55.8 0.7 %copy-start.2 = (f32[5,75,128]{2,1,0:T(8,128)}, f32[5,75,128]{2,1,0:T(8,128)S(1)}, u32[]{:S(2)}) copy-start(f32[5,75,128]{2,1,0:T(8,128)S(1)} %collective-permute-done.4.fn_ref) | copy-start | bytes 576004
  55.9 0.8 %copy-start.3 = (f32[5,75,128]{2,1,0:T(8,128)}, f32[5,75,128]{2,1,0:T(8,128)S(1)}, u32[]{:S(2)}) copy-start(f32[5,75,128]{2,1,0:T(8,128)S(1)} %collective-permute-done.5.fs_ref) | copy-start | bytes 576004

commit v4 on v3

--- a/solution.py
+++ b/solution.py
@@ -77,7 +77,7 @@
     _put_column(me_ref, fields, ucols[LANES - 1:LANES])
     sn_ref[fields] = c_ref[1, pl.ds(7, levels, stride=8), :]
     prof = p_ref[...]
-    mass = m_ref[...]
+    mass = m_ref[...].reshape(1, -1)
     _send_records(me_ref, prof, mass, ie_ref[0:1, :])
     _send_records(mw_ref, prof, mass, iw_ref[0:1, :])
 
@@ -103,7 +103,7 @@
     taken = _dot(jnp.ones((8, cross), jnp.float32), hot_e + hot_w, ((1,), (1,)))[0:1]
     moved = taken > 0.5
     prof = jnp.where(moved, placed[:levels], p_ref[...])
-    mass = jnp.where(moved, placed[levels:levels + 1], m_ref[...])
+    mass = jnp.where(moved, placed[levels:levels + 1], m_ref[...].reshape(1, -1))
 
     temp = jnp.concatenate([x_ref[0, pl.ds(r, levels, stride=8), :] for r in range(8)], axis=1)
     hot_c = _one_hot(cell_ref[step_index:step_index + 1, :], cells)
@@ -114,10 +114,11 @@
     source = _dot(melt, hot_c, ((1,), (1,)))
     mass_new = mass / (1.0 + 0.05 * jnp.sum(melt, axis=0, keepdims=True))
     po_ref[...] = prof
-    mo_ref[...] = mass_new
+    mo_ref[...] = mass_new.reshape(-1)
     for r in range(8):
         sscr[pl.ds(r, levels, stride=8), :] = source[:, r * LANES:(r + 1) * LANES]
-        dscr[pl.ds(r, levels, stride=8), :] = jnp.broadcast_to(d_ref[...], (levels, LANES))
+    for l in range(levels):
+        dscr[l * 8:(l + 1) * 8, :] = jnp.full((8, LANES), d_ref[l], jnp.float32)
 
     rows = lax.broadcasted_iota(jnp.int32, (count, LANES), 0) % 8
     lanes = lax.broadcasted_iota(jnp.int32, (count, LANES), 1)
@@ -127,6 +128,7 @@
     zero_row = jnp.zeros((1, pieces * LANES), jnp.float32)
     u_halo = _column_matrix(_get_column(cw_ref, fields, pieces), zero_row, count)
     u_w = jnp.where(lanes == 0, u_halo, pltpu.roll(u, 1, 1))
+    hscr[...] = jnp.zeros(hscr.shape, jnp.float32)
     hscr[pl.ds(0, levels, stride=8), :] = cs_ref[fields]
     v_s = jnp.where(rows == 0, hscr[...], pltpu.roll(v, 1, 0))
     a_c = 1.0 - jnp.maximum(u, 0.0) + jnp.minimum(u_w, 0.0) - jnp.maximum(v, 0.0) + jnp.minimum(v_s, 0.0) - 4.0 * d
@@ -134,6 +136,16 @@
     a_w = d + jnp.maximum(u_w, 0.0)
     a_n = d - jnp.minimum(v, 0.0)
     a_s = d + jnp.maximum(v_s, 0.0)
+    last_lane = lanes == LANES - 1
+    first_lane = lanes == 0
+    top_row = rows == 7
+    bottom_row = rows == 0
+    a_ew = jnp.where(last_lane, a_e, jnp.where(first_lane, a_w, 0.0))
+    a_ns = jnp.where(top_row, a_n, jnp.where(bottom_row, a_s, 0.0))
+    a_e = jnp.where(last_lane, 0.0, a_e)
+    a_w = jnp.where(first_lane, 0.0, a_w)
+    a_n = jnp.where(top_row, 0.0, a_n)
+    a_s = jnp.where(bottom_row, 0.0, a_s)
     src = sscr[...]
     if with_sends:
         me_ref[...] = jnp.zeros(me_ref.shape, jnp.float32)
@@ -141,14 +153,12 @@
     for f in range(fields):
         c = x_ref[f]
         halo = _column_matrix(_get_column(fw_ref, f, pieces), _get_column(fe_ref, f, pieces), count)
-        east = jnp.where(lanes == LANES - 1, halo, pltpu.roll(c, LANES - 1, 1))
-        west = jnp.where(lanes == 0, halo, pltpu.roll(c, 1, 1))
         hscr[pl.ds(7, levels, stride=8), :] = fn_ref[f]
         hscr[pl.ds(0, levels, stride=8), :] = fs_ref[f]
         hrow = hscr[...]
-        north = jnp.where(rows == 7, hrow, pltpu.roll(c, count - 1, 0))
-        south = jnp.where(rows == 0, hrow, pltpu.roll(c, 1, 0))
-        out = a_c * c + a_e * east + a_w * west + a_n * north + a_s * south + coef_ref[f] * src
+        out = (a_c * c + a_e * pltpu.roll(c, LANES - 1, 1) + a_w * pltpu.roll(c, 1, 1)
+               + a_n * pltpu.roll(c, count - 1, 0) + a_s * pltpu.roll(c, 1, 0)
+               + a_ew * halo + a_ns * hrow + coef_ref[f] * src)
         o_ref[f] = out
         if with_sends:
             cols = _columns(out)
@@ -200,7 +210,7 @@
     return pl.pallas_call(
         functools.partial(_step_kernel, step_index, with_sends),
         out_shape=tuple(outs),
-        in_specs=[pl.BlockSpec(memory_space=pltpu.SMEM)] + [_vmem()] * 14,
+        in_specs=[pl.BlockSpec(memory_space=pltpu.SMEM)] * 2 + [_vmem()] * 13,
         out_specs=tuple(_vmem() for _ in outs),
         scratch_shapes=[pltpu.VMEM((count, LANES), jnp.float32)] * 3,
     )(coef, d, x, c, prof, mass, cell, ie, iw, fn, fs, fw, fe, cs, cw)
@@ -221,9 +231,9 @@
     count = levels * rows
     x = tracers.reshape(fields, count, cols)
     c = courant.reshape(2, count, cols)
-    d = diffusivity.reshape(levels, 1)
+    d = diffusivity
     prof = berg_profile
-    mass = berg_mass.reshape(1, -1)
+    mass = berg_mass
     sn, ss, me, mw = prep(x, c, prof, mass, send_east, send_west)
     cs = cw = None
     for step_index in range(STEPS):
@@ -240,7 +250,7 @@
             x, prof, mass, sn, ss, me, mw = result
         else:
             x, prof, mass = result
-    return (x.reshape(fields, levels, rows, cols), mass.reshape(-1))
+    return (x.reshape(fields, levels, rows, cols), mass)
 
 
 def solution(mesh):

time: 65.8 us -> 63.1 us (0.959)
  local copies, waits for them, and re-layouts: 4.14 us -> 2.12 us
  other arithmetic: 1.23 us -> 0 us
  waiting for transfers between devices: 2.47 us -> 3.19 us
    reshape x2 -> x0, local copies, waits for them, and re-layouts: 1.96 us -> none  [the longest x1 1.25 us: per_device(): mass = berg_mass.reshape(1, -1)]
    pallas_call x1 -> x0, other arithmetic: 1.23 us -> none  [step(): pl.pallas_call(functools.partial(_step_kernel, step_index, with_sends), o...]
    ppermute x8, waiting for transfers between devices: 2.47 us -> 3.19 us  [shift(): return lax.ppermute(value, axis, pairs)]
    unnamed x18 -> x16, local copies, waits for them, and re-layouts: 2.18 us -> 2.12 us
  transfers between devices with their start and end apart: 8 -> 8, of which waited for: 2 -> 3; matrix products, arithmetic and copies ran while one was open for 1% -> 0% of each run, Pallas kernels for 0% -> 0%
where the time goes in v4:
time: 63.1 us; the launch traced here: 62.7 us
  starting transfers between devices  38.3 us (61%)
  Pallas kernels  18.4 us (29%)
  waiting for transfers between devices  3.19 us (5%)
  local copies, waits for them, and re-layouts  2.12 us (3%)
  between operations  0.75 us (1%)
    ppermute x8, starting transfers between devices, shift(): return lax.ppermute(value, axis, pairs)  38.3 us
    pallas_call x2, Pallas kernels, step(): pl.pallas_call(functools.partial(_step_kernel, step_index, with_sends), o...  15.4 us
    ppermute x8, waiting for transfers between devices, shift(): return lax.ppermute(value, axis, pairs)  3.19 us
    pallas_call x1, Pallas kernels, prep(): pl.pallas_call(_prep_kernel, out_shape=(_f32((fields + 1, levels, LANES))...  3.01 us
    unnamed x16, local copies, waits for them, and re-layouts  2.12 us
  transfers between devices with their start and end apart: 8, of which 3 were waited for; matrix products, arithmetic and copies ran while one was open for 0% of the time, Pallas kernels for 0%

profile of v4, /device:TPU:7, one launch (start us, length us, event | category | flops | bytes accessed | tf_op | source)
XLA Modules:
  0.0 62.7 jit_solution(13382237283710177462)
XLA Ops:
  0.6 3.0 %shard_map.104 = (f32[6,75,128]{2,1,0:T(8,128)}, f32[5,75,128]{2,1,0:T(8,128)}, f32[112,128]{1,0:T(8,128)}, f32[112,128]{1,0:T(8,128)}) custom-call(f32[5,600,128]{2,1,0:T(8,128)} %bitcast.3, f32[2,600,128]{2,1,0:T(8,128)} %bitcast.5, f32[75,384]{1,0:T(8,128)} %p_ref.3, f32[384]{0:T(512)} %m_ref.3, s32[2,32]{1,0:T(2,128)} %ie_ref.5, s32[2,32]{1,0:T(2,128)} %iw_ref.5), custom_call_target="tpu_custom_call" | custom-call | tf_op jit(solution)/shard_map/pallas_call | solution.py:186
  3.6 5.3 %collective-permute-start.1 = (f32[6,75,128]{2,1,0:T(8,128)}, f32[6,75,128]{2,1,0:T(8,128)S(1)}, u32[]{:S(2)}, u32[]{:S(2)}) collective-permute-start(f32[6,75,128]{2,1,0:T(8,128)} %get-tuple-element.16), channel_id=1, source_target_pairs={{0,1},{1,2},{2,3},{3,4},{4,5},{5,6},{6,7},{7,8},{8,9},{9,10},{10,1... | collective-permute-start | bytes 691208 | tf_op jit(solution)/shard_map/ppermute | solution.py:225
  8.9 1.9 %collective-permute-start = (f32[5,75,128]{2,1,0:T(8,128)}, f32[5,75,128]{2,1,0:T(8,128)S(1)}, u32[]{:S(2)}, u32[]{:S(2)}) collective-permute-start(f32[5,75,128]{2,1,0:T(8,128)} %get-tuple-element.15), channel_id=1, source_target_pairs={{1,0},{2,1},{3,2},{4,3},{5,4},{6,5},{7,6},{8,7},{9,8},{10,9},{11,1... | collective-permute-start | bytes 576008 | tf_op jit(solution)/shard_map/ppermute | solution.py:225
  10.9 3.5 %collective-permute-start.2 = (f32[112,128]{1,0:T(8,128)}, f32[112,128]{1,0:T(8,128)S(1)}, u32[]{:S(2)}, u32[]{:S(2)}) collective-permute-start(f32[112,128]{1,0:T(8,128)} %get-tuple-element.17), channel_id=1, source_target_pairs={{0,16},{16,32},{32,48},{48,64},{64,80},{80,96},{96,112},{112,128},... | collective-permute-start | bytes 172040 | tf_op jit(solution)/shard_map/ppermute | solution.py:225
  14.4 9.6 %collective-permute-start.3 = (f32[112,128]{1,0:T(8,128)}, f32[112,128]{1,0:T(8,128)S(1)}, u32[]{:S(2)}, u32[]{:S(2)}) collective-permute-start(f32[112,128]{1,0:T(8,128)} %get-tuple-element.18), channel_id=1, source_target_pairs={{0,496},{16,0},{32,16},{48,32},{64,48},{80,64},{96,80},{112,96},{1... | collective-permute-start | bytes 172040 | tf_op jit(solution)/shard_map/ppermute | solution.py:225
  24.0 0.6 %collective-permute-done.2.fw_ref.cw_ref = f32[112,128]{1,0:T(8,128)S(1)} collective-permute-done((f32[112,128]{1,0:T(8,128)}, f32[112,128]{1,0:T(8,128)S(1)}, u32[]{:S(2)}, u32[]{:S(2)}) %collective-permute-start.2) | collective-permute-done | bytes 57376 | tf_op jit(solution)/shard_map/ppermute | solution.py:225
  24.7 0.0 copy-start.1
  24.7 1.0 %collective-permute-done.3.fe_ref = f32[112,128]{1,0:T(8,128)S(1)} collective-permute-done((f32[112,128]{1,0:T(8,128)}, f32[112,128]{1,0:T(8,128)S(1)}, u32[]{:S(2)}, u32[]{:S(2)}) %collective-permute-start.3) | collective-permute-done | bytes 57376 | tf_op jit(solution)/shard_map/ppermute | solution.py:225
  25.7 0.0 copy-start.7
  25.7 0.0 collective-permute-done.fn_ref
  25.7 0.0 copy-start.4
  25.7 0.0 collective-permute-done.1.fs_ref.cs_ref
  25.7 0.0 copy-done.1
  25.7 0.6 copy-done.7
  26.3 0.1 copy-done.4
  26.4 0.0 copy-start
  26.4 0.7 %copy-done = f32[6,75,128]{2,1,0:T(8,128)} copy-done((f32[6,75,128]{2,1,0:T(8,128)}, f32[6,75,128]{2,1,0:T(8,128)S(1)}, u32[]{:S(2)}) %copy-start) | copy-done | bytes 230424
  27.1 8.0 %shard_map.105 = (f32[5,600,128]{2,1,0:T(8,128)}, f32[75,384]{1,0:T(8,128)}, f32[384]{0:T(512)}, f32[5,75,128]{2,1,0:T(8,128)}, f32[5,75,128]{2,1,0:T(8,128)}, /*index=5*/f32[112,128]{1,0:T(8,128)}, f32[112,128]{1,0:T(8,128)}) custom-call(f32[5]{0:T(128)} %coef_ref.3, f32[75]{0:T(128)} %d_ref.3, f32[5,600,128]{2,1,0:T(8,128)} %bitcast.4, ...), custom_call_target="tpu_custom_call" | custom-call | tf_op jit(solution)/shard_map/pallas_call | solution.py:210
  35.1 2.7 %collective-permute-start.4 = (f32[5,75,128]{2,1,0:T(8,128)}, f32[5,75,128]{2,1,0:T(8,128)S(1)}, u32[]{:S(2)}, u32[]{:S(2)}) collective-permute-start(f32[5,75,128]{2,1,0:T(8,128)} %get-tuple-element.22), channel_id=1, source_target_pairs={{1,0},{2,1},{3,2},{4,3},{5,4},{6,5},{7,6},{8,7},{9,8},{10,9},{11,1... | collective-permute-start | bytes 576008 | tf_op jit(solution)/shard_map/ppermute | solution.py:225
  37.7 7.9 %collective-permute-start.5 = (f32[5,75,128]{2,1,0:T(8,128)}, f32[5,75,128]{2,1,0:T(8,128)S(1)}, u32[]{:S(2)}, u32[]{:S(2)}) collective-permute-start(f32[5,75,128]{2,1,0:T(8,128)} %get-tuple-element.23), channel_id=1, source_target_pairs={{0,1},{1,2},{2,3},{3,4},{4,5},{5,6},{6,7},{7,8},{8,9},{9,10},{10,1... | collective-permute-start | bytes 576008 | tf_op jit(solution)/shard_map/ppermute | solution.py:225
  45.6 1.9 %collective-permute-start.6 = (f32[112,128]{1,0:T(8,128)}, f32[112,128]{1,0:T(8,128)S(1)}, u32[]{:S(2)}, u32[]{:S(2)}) collective-permute-start(f32[112,128]{1,0:T(8,128)} %get-tuple-element.24), channel_id=1, source_target_pairs={{0,16},{16,32},{32,48},{48,64},{64,80},{80,96},{96,112},{112,128},... | collective-permute-start | bytes 172040 | tf_op jit(solution)/shard_map/ppermute | solution.py:225
  47.5 5.5 %collective-permute-start.7 = (f32[112,128]{1,0:T(8,128)}, f32[112,128]{1,0:T(8,128)S(1)}, u32[]{:S(2)}, u32[]{:S(2)}) collective-permute-start(f32[112,128]{1,0:T(8,128)} %get-tuple-element.25), channel_id=1, source_target_pairs={{0,496},{16,0},{32,16},{48,32},{64,48},{80,64},{96,80},{112,96},{1... | collective-permute-start | bytes 172040 | tf_op jit(solution)/shard_map/ppermute | solution.py:225
  53.0 0.0 collective-permute-done.6.fw_ref
  53.0 0.0 copy-start.5
  53.0 1.5 %collective-permute-done.7.fe_ref = f32[112,128]{1,0:T(8,128)S(1)} collective-permute-done((f32[112,128]{1,0:T(8,128)}, f32[112,128]{1,0:T(8,128)S(1)}, u32[]{:S(2)}, u32[]{:S(2)}) %collective-permute-start.7) | collective-permute-done | bytes 57376 | tf_op jit(solution)/shard_map/ppermute | solution.py:225
  54.6 0.0 copy-start.6
  54.6 0.0 collective-permute-done.4.fn_ref
  54.6 0.0 copy-start.2
  54.6 0.0 collective-permute-done.5.fs_ref
  54.6 0.0 copy-start.3
  54.6 0.0 copy-done.5
  54.6 0.6 copy-done.6
  55.2 0.1 copy-done.2
  55.3 0.1 copy-done.3
  55.3 7.4 %shard_map.106 = (f32[5,600,128]{2,1,0:T(8,128)}, f32[75,384]{1,0:T(8,128)}, f32[384]{0:T(512)}) custom-call(f32[5]{0:T(128)} %coef_ref.3, f32[75]{0:T(128)} %d_ref.3, f32[5,600,128]{2,1,0:T(8,128)} %get-tuple-element.19.x_ref, f32[2,600,128]{2,1,0:T(8,128)} %bitcast.7, f32[75,384]{1,0:T(8,128)} %get-tuple-element.20.p_ref, f32[384]{0:T(512)} %get-tuple-element.21.m_ref, ...), custom_call_target="tpu_custom_call" | custom-call | tf_op jit(solution)/shard_map/pallas_call | solution.py:210
Async XLA Ops:
  3.6 22.1 %collective-permute-start.1 = (f32[6,75,128]{2,1,0:T(8,128)}, f32[6,75,128]{2,1,0:T(8,128)S(1)}, u32[]{:S(2)}, u32[]{:S(2)}) collective-permute-start(f32[6,75,128]{2,1,0:T(8,128)} %get-tuple-element.16), channel_id=1, source_target_pairs={{0,1},{1,2},{2,3},{3,4},{4,5},{5,6},{6,7},{7,8},{8,9},{9,10},{10,1... | collective-permute-start | bytes 691208 | tf_op jit(solution)/shard_map/ppermute | solution.py:225
  8.9 16.8 %collective-permute-start = (f32[5,75,128]{2,1,0:T(8,128)}, f32[5,75,128]{2,1,0:T(8,128)S(1)}, u32[]{:S(2)}, u32[]{:S(2)}) collective-permute-start(f32[5,75,128]{2,1,0:T(8,128)} %get-tuple-element.15), channel_id=1, source_target_pairs={{1,0},{2,1},{3,2},{4,3},{5,4},{6,5},{7,6},{8,7},{9,8},{10,9},{11,1... | collective-permute-start | bytes 576008 | tf_op jit(solution)/shard_map/ppermute | solution.py:225
  10.9 13.8 %collective-permute-start.2 = (f32[112,128]{1,0:T(8,128)}, f32[112,128]{1,0:T(8,128)S(1)}, u32[]{:S(2)}, u32[]{:S(2)}) collective-permute-start(f32[112,128]{1,0:T(8,128)} %get-tuple-element.17), channel_id=1, source_target_pairs={{0,16},{16,32},{32,48},{48,64},{64,80},{80,96},{96,112},{112,128},... | collective-permute-start | bytes 172040 | tf_op jit(solution)/shard_map/ppermute | solution.py:225
  14.4 11.3 %collective-permute-start.3 = (f32[112,128]{1,0:T(8,128)}, f32[112,128]{1,0:T(8,128)S(1)}, u32[]{:S(2)}, u32[]{:S(2)}) collective-permute-start(f32[112,128]{1,0:T(8,128)} %get-tuple-element.18), channel_id=1, source_target_pairs={{0,496},{16,0},{32,16},{48,32},{64,48},{80,64},{96,80},{112,96},{1... | collective-permute-start | bytes 172040 | tf_op jit(solution)/shard_map/ppermute | solution.py:225
  24.7 1.0 %copy-start.1 = (f32[112,128]{1,0:T(8,128)}, f32[112,128]{1,0:T(8,128)S(1)}, u32[]{:S(2)}) copy-start(f32[112,128]{1,0:T(8,128)S(1)} %collective-permute-done.2.fw_ref.cw_ref) | copy-start | bytes 172036
  25.7 0.6 copy-start.7
  25.7 0.7 %copy-start.4 = (f32[5,75,128]{2,1,0:T(8,128)}, f32[5,75,128]{2,1,0:T(8,128)S(1)}, u32[]{:S(2)}) copy-start(f32[5,75,128]{2,1,0:T(8,128)S(1)} %collective-permute-done.fn_ref) | copy-start | bytes 576004
  26.4 0.7 %copy-start = (f32[6,75,128]{2,1,0:T(8,128)}, f32[6,75,128]{2,1,0:T(8,128)S(1)}, u32[]{:S(2)}) copy-start(f32[6,75,128]{2,1,0:T(8,128)S(1)} %collective-permute-done.1.fs_ref.cs_ref) | copy-start | bytes 691204
  35.1 19.5 %collective-permute-start.4 = (f32[5,75,128]{2,1,0:T(8,128)}, f32[5,75,128]{2,1,0:T(8,128)S(1)}, u32[]{:S(2)}, u32[]{:S(2)}) collective-permute-start(f32[5,75,128]{2,1,0:T(8,128)} %get-tuple-element.22), channel_id=1, source_target_pairs={{1,0},{2,1},{3,2},{4,3},{5,4},{6,5},{7,6},{8,7},{9,8},{10,9},{11,1... | collective-permute-start | bytes 576008 | tf_op jit(solution)/shard_map/ppermute | solution.py:225
  37.7 16.8 %collective-permute-start.5 = (f32[5,75,128]{2,1,0:T(8,128)}, f32[5,75,128]{2,1,0:T(8,128)S(1)}, u32[]{:S(2)}, u32[]{:S(2)}) collective-permute-start(f32[5,75,128]{2,1,0:T(8,128)} %get-tuple-element.23), channel_id=1, source_target_pairs={{0,1},{1,2},{2,3},{3,4},{4,5},{5,6},{6,7},{7,8},{8,9},{9,10},{10,1... | collective-permute-start | bytes 576008 | tf_op jit(solution)/shard_map/ppermute | solution.py:225
  45.6 7.4 %collective-permute-start.6 = (f32[112,128]{1,0:T(8,128)}, f32[112,128]{1,0:T(8,128)S(1)}, u32[]{:S(2)}, u32[]{:S(2)}) collective-permute-start(f32[112,128]{1,0:T(8,128)} %get-tuple-element.24), channel_id=1, source_target_pairs={{0,16},{16,32},{32,48},{48,64},{64,80},{80,96},{96,112},{112,128},... | collective-permute-start | bytes 172040 | tf_op jit(solution)/shard_map/ppermute | solution.py:225
  47.5 7.0 %collective-permute-start.7 = (f32[112,128]{1,0:T(8,128)}, f32[112,128]{1,0:T(8,128)S(1)}, u32[]{:S(2)}, u32[]{:S(2)}) collective-permute-start(f32[112,128]{1,0:T(8,128)} %get-tuple-element.25), channel_id=1, source_target_pairs={{0,496},{16,0},{32,16},{48,32},{64,48},{80,64},{96,80},{112,96},{1... | collective-permute-start | bytes 172040 | tf_op jit(solution)/shard_map/ppermute | solution.py:225
  53.0 1.6 %copy-start.5 = (f32[112,128]{1,0:T(8,128)}, f32[112,128]{1,0:T(8,128)S(1)}, u32[]{:S(2)}) copy-start(f32[112,128]{1,0:T(8,128)S(1)} %collective-permute-done.6.fw_ref) | copy-start | bytes 172036
  54.6 0.6 copy-start.6
  54.6 0.7 %copy-start.2 = (f32[5,75,128]{2,1,0:T(8,128)}, f32[5,75,128]{2,1,0:T(8,128)S(1)}, u32[]{:S(2)}) copy-start(f32[5,75,128]{2,1,0:T(8,128)S(1)} %collective-permute-done.4.fn_ref) | copy-start | bytes 576004
  54.6 0.8 %copy-start.3 = (f32[5,75,128]{2,1,0:T(8,128)}, f32[5,75,128]{2,1,0:T(8,128)S(1)}, u32[]{:S(2)}) copy-start(f32[5,75,128]{2,1,0:T(8,128)S(1)} %collective-permute-done.5.fs_ref) | copy-start | bytes 576004

commit v5 on v4

--- a/solution.py
+++ b/solution.py
@@ -18,6 +18,21 @@
     return lax.dot_general(a, b, (dims, ((), ())), precision=HI, preferred_element_type=jnp.float32)
 
 
+def _split3(a):
+    hi = a.astype(jnp.bfloat16)
+    rest = a - hi.astype(jnp.float32)
+    mid = rest.astype(jnp.bfloat16)
+    lo = (rest - mid.astype(jnp.float32)).astype(jnp.bfloat16)
+    return jnp.concatenate([hi, mid, lo], axis=0)
+
+
+def _select(a, hot, dims):
+    m = a.shape[0]
+    part = lax.dot_general(_split3(a), hot.astype(jnp.bfloat16), (dims, ((), ())),
+                           preferred_element_type=jnp.float32)
+    return (part[:m] + part[m:2 * m]) + part[2 * m:]
+
+
 def _pieces(count):
     return -(-count // LANES)
 
@@ -58,8 +73,9 @@
     hot = _one_hot(index_row, slots)
     levels = prof.shape[0]
     cross = index_row.shape[1]
-    msg_ref[REC_ROW:REC_ROW + levels, 0:cross] = _dot(prof, hot, ((1,), (0,)))
-    msg_ref[REC_ROW + levels:REC_ROW + levels + 1, 0:cross] = _dot(mass, hot, ((1,), (0,)))
+    rec = _select(jnp.concatenate([prof, mass, jnp.zeros((4, slots), jnp.float32)], axis=0), hot,
+                  ((1,), (0,)))
+    msg_ref[REC_ROW:REC_ROW + levels + 1, 0:cross] = rec[:levels + 1]
 
 
 def _prep_kernel(x_ref, c_ref, p_ref, m_ref, ie_ref, iw_ref, sn_ref, ss_ref, me_ref, mw_ref):
@@ -97,21 +113,22 @@
 
     hot_e = _one_hot(ie_ref[step_index:step_index + 1, :], slots)
     hot_w = _one_hot(iw_ref[step_index:step_index + 1, :], slots)
-    rec_e = fw_ref[REC_ROW:REC_ROW + levels + 1, 0:cross]
-    rec_w = fe_ref[REC_ROW:REC_ROW + levels + 1, 0:cross]
-    placed = _dot(rec_e, hot_e, ((1,), (1,))) + _dot(rec_w, hot_w, ((1,), (1,)))
-    taken = _dot(jnp.ones((8, cross), jnp.float32), hot_e + hot_w, ((1,), (1,)))[0:1]
+    rec_e = fw_ref[REC_ROW:REC_ROW + levels + 5, 0:cross]
+    rec_w = fe_ref[REC_ROW:REC_ROW + levels + 5, 0:cross]
+    placed = _select(rec_e, hot_e, ((1,), (1,))) + _select(rec_w, hot_w, ((1,), (1,)))
+    taken = lax.dot_general(jnp.ones((8, cross), jnp.bfloat16), (hot_e + hot_w).astype(jnp.bfloat16),
+                            (((1,), (1,)), ((), ())), preferred_element_type=jnp.float32)[0:1]
     moved = taken > 0.5
     prof = jnp.where(moved, placed[:levels], p_ref[...])
     mass = jnp.where(moved, placed[levels:levels + 1], m_ref[...].reshape(1, -1))
 
     temp = jnp.concatenate([x_ref[0, pl.ds(r, levels, stride=8), :] for r in range(8)], axis=1)
     hot_c = _one_hot(cell_ref[step_index:step_index + 1, :], cells)
-    water = _dot(temp, hot_c, ((1,), (0,)))
+    water = _select(temp, hot_c, ((1,), (0,)))
     z = water + 1.8
     soft = jnp.maximum(z, 0.0) + jnp.log1p(jnp.exp(-jnp.abs(z)))
     melt = prof * soft * jnp.sqrt(mass)
-    source = _dot(melt, hot_c, ((1,), (1,)))
+    source = _select(melt, hot_c, ((1,), (1,)))
     mass_new = mass / (1.0 + 0.05 * jnp.sum(melt, axis=0, keepdims=True))
     po_ref[...] = prof
     mo_ref[...] = mass_new.reshape(-1)

time: 63.1 us -> 59.8 us (0.948)
  Pallas kernels: 18.4 us -> 15 us
    pallas_call x2, Pallas kernels: 15.4 us -> 12.1 us  [step(): pl.pallas_call(functools.partial(_step_kernel, step_index, with_sends), o...]
where the time goes in v5:
time: 59.8 us; the launch traced here: 59.4 us
  starting transfers between devices  38.3 us (64%)
  Pallas kernels  15 us (25%)
  waiting for transfers between devices  3.19 us (5%)
  local copies, waits for them, and re-layouts  2.12 us (4%)
  between operations  0.75 us (1%)
    ppermute x8, starting transfers between devices, shift(): return lax.ppermute(value, axis, pairs)  38.3 us
    pallas_call x2, Pallas kernels, step(): pl.pallas_call(functools.partial(_step_kernel, step_index, with_sends), o...  12.1 us
    ppermute x8, waiting for transfers between devices, shift(): return lax.ppermute(value, axis, pairs)  3.19 us
    pallas_call x1, Pallas kernels, prep(): pl.pallas_call(_prep_kernel, out_shape=(_f32((fields + 1, levels, LANES))...  2.96 us
    unnamed x16, local copies, waits for them, and re-layouts  2.12 us
  transfers between devices with their start and end apart: 8, of which 3 were waited for; matrix products, arithmetic and copies ran while one was open for 0% of the time, Pallas kernels for 0%

profile of v5, /device:TPU:7, one launch (start us, length us, event | category | flops | bytes accessed | tf_op | source)
XLA Modules:
  0.0 59.4 jit_solution(1937542065113913093)
XLA Ops:
  0.6 3.0 %shard_map.104 = (f32[6,75,128]{2,1,0:T(8,128)}, f32[5,75,128]{2,1,0:T(8,128)}, f32[112,128]{1,0:T(8,128)}, f32[112,128]{1,0:T(8,128)}) custom-call(f32[5,600,128]{2,1,0:T(8,128)} %bitcast.3, f32[2,600,128]{2,1,0:T(8,128)} %bitcast.5, f32[75,384]{1,0:T(8,128)} %p_ref.3, f32[384]{0:T(512)} %m_ref.3, s32[2,32]{1,0:T(2,128)} %ie_ref.5, s32[2,32]{1,0:T(2,128)} %iw_ref.5), custom_call_target="tpu_custom_call" | custom-call | tf_op jit(solution)/shard_map/pallas_call | solution.py:203
  3.6 5.3 %collective-permute-start.1 = (f32[6,75,128]{2,1,0:T(8,128)}, f32[6,75,128]{2,1,0:T(8,128)S(1)}, u32[]{:S(2)}, u32[]{:S(2)}) collective-permute-start(f32[6,75,128]{2,1,0:T(8,128)} %get-tuple-element.16), channel_id=1, source_target_pairs={{0,1},{1,2},{2,3},{3,4},{4,5},{5,6},{6,7},{7,8},{8,9},{9,10},{10,1... | collective-permute-start | bytes 691208 | tf_op jit(solution)/shard_map/ppermute | solution.py:242
  8.9 1.9 %collective-permute-start = (f32[5,75,128]{2,1,0:T(8,128)}, f32[5,75,128]{2,1,0:T(8,128)S(1)}, u32[]{:S(2)}, u32[]{:S(2)}) collective-permute-start(f32[5,75,128]{2,1,0:T(8,128)} %get-tuple-element.15), channel_id=1, source_target_pairs={{1,0},{2,1},{3,2},{4,3},{5,4},{6,5},{7,6},{8,7},{9,8},{10,9},{11,1... | collective-permute-start | bytes 576008 | tf_op jit(solution)/shard_map/ppermute | solution.py:242
  10.8 3.6 %collective-permute-start.2 = (f32[112,128]{1,0:T(8,128)}, f32[112,128]{1,0:T(8,128)S(1)}, u32[]{:S(2)}, u32[]{:S(2)}) collective-permute-start(f32[112,128]{1,0:T(8,128)} %get-tuple-element.17), channel_id=1, source_target_pairs={{0,16},{16,32},{32,48},{48,64},{64,80},{80,96},{96,112},{112,128},... | collective-permute-start | bytes 172040 | tf_op jit(solution)/shard_map/ppermute | solution.py:242
  14.4 9.6 %collective-permute-start.3 = (f32[112,128]{1,0:T(8,128)}, f32[112,128]{1,0:T(8,128)S(1)}, u32[]{:S(2)}, u32[]{:S(2)}) collective-permute-start(f32[112,128]{1,0:T(8,128)} %get-tuple-element.18), channel_id=1, source_target_pairs={{0,496},{16,0},{32,16},{48,32},{64,48},{80,64},{96,80},{112,96},{1... | collective-permute-start | bytes 172040 | tf_op jit(solution)/shard_map/ppermute | solution.py:242
  24.0 0.6 %collective-permute-done.2.fw_ref.cw_ref = f32[112,128]{1,0:T(8,128)S(1)} collective-permute-done((f32[112,128]{1,0:T(8,128)}, f32[112,128]{1,0:T(8,128)S(1)}, u32[]{:S(2)}, u32[]{:S(2)}) %collective-permute-start.2) | collective-permute-done | bytes 57376 | tf_op jit(solution)/shard_map/ppermute | solution.py:242
  24.6 0.0 copy-start.1
  24.6 1.0 %collective-permute-done.3.fe_ref = f32[112,128]{1,0:T(8,128)S(1)} collective-permute-done((f32[112,128]{1,0:T(8,128)}, f32[112,128]{1,0:T(8,128)S(1)}, u32[]{:S(2)}, u32[]{:S(2)}) %collective-permute-start.3) | collective-permute-done | bytes 57376 | tf_op jit(solution)/shard_map/ppermute | solution.py:242
  25.6 0.0 copy-start.7
  25.6 0.0 collective-permute-done.fn_ref
  25.6 0.0 copy-start.4
  25.6 0.0 collective-permute-done.1.fs_ref.cs_ref
  25.6 0.0 copy-done.1
  25.7 0.6 copy-done.7
  26.2 0.1 copy-done.4
  26.3 0.0 copy-start
  26.3 0.7 %copy-done = f32[6,75,128]{2,1,0:T(8,128)} copy-done((f32[6,75,128]{2,1,0:T(8,128)}, f32[6,75,128]{2,1,0:T(8,128)S(1)}, u32[]{:S(2)}) %copy-start) | copy-done | bytes 230424
  27.0 6.5 %shard_map.105 = (f32[5,600,128]{2,1,0:T(8,128)}, f32[75,384]{1,0:T(8,128)}, f32[384]{0:T(512)}, f32[5,75,128]{2,1,0:T(8,128)}, f32[5,75,128]{2,1,0:T(8,128)}, /*index=5*/f32[112,128]{1,0:T(8,128)}, f32[112,128]{1,0:T(8,128)}) custom-call(f32[5]{0:T(128)} %coef_ref.3, f32[75]{0:T(128)} %d_ref.3, f32[5,600,128]{2,1,0:T(8,128)} %bitcast.4, ...), custom_call_target="tpu_custom_call" | custom-call | tf_op jit(solution)/shard_map/pallas_call | solution.py:227
  33.5 2.7 %collective-permute-start.4 = (f32[5,75,128]{2,1,0:T(8,128)}, f32[5,75,128]{2,1,0:T(8,128)S(1)}, u32[]{:S(2)}, u32[]{:S(2)}) collective-permute-start(f32[5,75,128]{2,1,0:T(8,128)} %get-tuple-element.22), channel_id=1, source_target_pairs={{1,0},{2,1},{3,2},{4,3},{5,4},{6,5},{7,6},{8,7},{9,8},{10,9},{11,1... | collective-permute-start | bytes 576008 | tf_op jit(solution)/shard_map/ppermute | solution.py:242
  36.2 7.9 %collective-permute-start.5 = (f32[5,75,128]{2,1,0:T(8,128)}, f32[5,75,128]{2,1,0:T(8,128)S(1)}, u32[]{:S(2)}, u32[]{:S(2)}) collective-permute-start(f32[5,75,128]{2,1,0:T(8,128)} %get-tuple-element.23), channel_id=1, source_target_pairs={{0,1},{1,2},{2,3},{3,4},{4,5},{5,6},{6,7},{7,8},{8,9},{9,10},{10,1... | collective-permute-start | bytes 576008 | tf_op jit(solution)/shard_map/ppermute | solution.py:242
  44.1 1.9 %collective-permute-start.6 = (f32[112,128]{1,0:T(8,128)}, f32[112,128]{1,0:T(8,128)S(1)}, u32[]{:S(2)}, u32[]{:S(2)}) collective-permute-start(f32[112,128]{1,0:T(8,128)} %get-tuple-element.24), channel_id=1, source_target_pairs={{0,16},{16,32},{32,48},{48,64},{64,80},{80,96},{96,112},{112,128},... | collective-permute-start | bytes 172040 | tf_op jit(solution)/shard_map/ppermute | solution.py:242
  46.0 5.5 %collective-permute-start.7 = (f32[112,128]{1,0:T(8,128)}, f32[112,128]{1,0:T(8,128)S(1)}, u32[]{:S(2)}, u32[]{:S(2)}) collective-permute-start(f32[112,128]{1,0:T(8,128)} %get-tuple-element.25), channel_id=1, source_target_pairs={{0,496},{16,0},{32,16},{48,32},{64,48},{80,64},{96,80},{112,96},{1... | collective-permute-start | bytes 172040 | tf_op jit(solution)/shard_map/ppermute | solution.py:242
  51.5 0.0 collective-permute-done.6.fw_ref
  51.5 0.0 copy-start.5
  51.5 1.5 %collective-permute-done.7.fe_ref = f32[112,128]{1,0:T(8,128)S(1)} collective-permute-done((f32[112,128]{1,0:T(8,128)}, f32[112,128]{1,0:T(8,128)S(1)}, u32[]{:S(2)}, u32[]{:S(2)}) %collective-permute-start.7) | collective-permute-done | bytes 57376 | tf_op jit(solution)/shard_map/ppermute | solution.py:242
  53.0 0.0 copy-start.6
  53.0 0.0 collective-permute-done.4.fn_ref
  53.0 0.0 copy-start.2
  53.0 0.0 collective-permute-done.5.fs_ref
  53.0 0.0 copy-start.3
  53.0 0.0 copy-done.5
  53.1 0.6 copy-done.6
  53.6 0.1 copy-done.2
  53.7 0.1 copy-done.3
  53.8 5.6 %shard_map.106 = (f32[5,600,128]{2,1,0:T(8,128)}, f32[75,384]{1,0:T(8,128)}, f32[384]{0:T(512)}) custom-call(f32[5]{0:T(128)} %coef_ref.3, f32[75]{0:T(128)} %d_ref.3, f32[5,600,128]{2,1,0:T(8,128)} %get-tuple-element.19.x_ref, f32[2,600,128]{2,1,0:T(8,128)} %bitcast.7, f32[75,384]{1,0:T(8,128)} %get-tuple-element.20.p_ref, f32[384]{0:T(512)} %get-tuple-element.21.m_ref, ...), custom_call_target="tpu_custom_call" | custom-call | tf_op jit(solution)/shard_map/pallas_call | solution.py:227
Async XLA Ops:
  3.6 22.1 %collective-permute-start.1 = (f32[6,75,128]{2,1,0:T(8,128)}, f32[6,75,128]{2,1,0:T(8,128)S(1)}, u32[]{:S(2)}, u32[]{:S(2)}) collective-permute-start(f32[6,75,128]{2,1,0:T(8,128)} %get-tuple-element.16), channel_id=1, source_target_pairs={{0,1},{1,2},{2,3},{3,4},{4,5},{5,6},{6,7},{7,8},{8,9},{9,10},{10,1... | collective-permute-start | bytes 691208 | tf_op jit(solution)/shard_map/ppermute | solution.py:242
  8.9 16.8 %collective-permute-start = (f32[5,75,128]{2,1,0:T(8,128)}, f32[5,75,128]{2,1,0:T(8,128)S(1)}, u32[]{:S(2)}, u32[]{:S(2)}) collective-permute-start(f32[5,75,128]{2,1,0:T(8,128)} %get-tuple-element.15), channel_id=1, source_target_pairs={{1,0},{2,1},{3,2},{4,3},{5,4},{6,5},{7,6},{8,7},{9,8},{10,9},{11,1... | collective-permute-start | bytes 576008 | tf_op jit(solution)/shard_map/ppermute | solution.py:242
  10.8 13.8 %collective-permute-start.2 = (f32[112,128]{1,0:T(8,128)}, f32[112,128]{1,0:T(8,128)S(1)}, u32[]{:S(2)}, u32[]{:S(2)}) collective-permute-start(f32[112,128]{1,0:T(8,128)} %get-tuple-element.17), channel_id=1, source_target_pairs={{0,16},{16,32},{32,48},{48,64},{64,80},{80,96},{96,112},{112,128},... | collective-permute-start | bytes 172040 | tf_op jit(solution)/shard_map/ppermute | solution.py:242
  14.4 11.3 %collective-permute-start.3 = (f32[112,128]{1,0:T(8,128)}, f32[112,128]{1,0:T(8,128)S(1)}, u32[]{:S(2)}, u32[]{:S(2)}) collective-permute-start(f32[112,128]{1,0:T(8,128)} %get-tuple-element.18), channel_id=1, source_target_pairs={{0,496},{16,0},{32,16},{48,32},{64,48},{80,64},{96,80},{112,96},{1... | collective-permute-start | bytes 172040 | tf_op jit(solution)/shard_map/ppermute | solution.py:242
  24.6 1.0 %copy-start.1 = (f32[112,128]{1,0:T(8,128)}, f32[112,128]{1,0:T(8,128)S(1)}, u32[]{:S(2)}) copy-start(f32[112,128]{1,0:T(8,128)S(1)} %collective-permute-done.2.fw_ref.cw_ref) | copy-start | bytes 172036
  25.6 0.6 %copy-start.7 = (f32[112,128]{1,0:T(8,128)}, f32[112,128]{1,0:T(8,128)S(1)}, u32[]{:S(2)}) copy-start(f32[112,128]{1,0:T(8,128)S(1)} %collective-permute-done.3.fe_ref) | copy-start | bytes 172036
  25.6 0.7 %copy-start.4 = (f32[5,75,128]{2,1,0:T(8,128)}, f32[5,75,128]{2,1,0:T(8,128)S(1)}, u32[]{:S(2)}) copy-start(f32[5,75,128]{2,1,0:T(8,128)S(1)} %collective-permute-done.fn_ref) | copy-start | bytes 576004
  26.3 0.7 %copy-start = (f32[6,75,128]{2,1,0:T(8,128)}, f32[6,75,128]{2,1,0:T(8,128)S(1)}, u32[]{:S(2)}) copy-start(f32[6,75,128]{2,1,0:T(8,128)S(1)} %collective-permute-done.1.fs_ref.cs_ref) | copy-start | bytes 691204
  33.5 19.5 %collective-permute-start.4 = (f32[5,75,128]{2,1,0:T(8,128)}, f32[5,75,128]{2,1,0:T(8,128)S(1)}, u32[]{:S(2)}, u32[]{:S(2)}) collective-permute-start(f32[5,75,128]{2,1,0:T(8,128)} %get-tuple-element.22), channel_id=1, source_target_pairs={{1,0},{2,1},{3,2},{4,3},{5,4},{6,5},{7,6},{8,7},{9,8},{10,9},{11,1... | collective-permute-start | bytes 576008 | tf_op jit(solution)/shard_map/ppermute | solution.py:242
  36.2 16.8 %collective-permute-start.5 = (f32[5,75,128]{2,1,0:T(8,128)}, f32[5,75,128]{2,1,0:T(8,128)S(1)}, u32[]{:S(2)}, u32[]{:S(2)}) collective-permute-start(f32[5,75,128]{2,1,0:T(8,128)} %get-tuple-element.23), channel_id=1, source_target_pairs={{0,1},{1,2},{2,3},{3,4},{4,5},{5,6},{6,7},{7,8},{8,9},{9,10},{10,1... | collective-permute-start | bytes 576008 | tf_op jit(solution)/shard_map/ppermute | solution.py:242
  44.1 7.4 %collective-permute-start.6 = (f32[112,128]{1,0:T(8,128)}, f32[112,128]{1,0:T(8,128)S(1)}, u32[]{:S(2)}, u32[]{:S(2)}) collective-permute-start(f32[112,128]{1,0:T(8,128)} %get-tuple-element.24), channel_id=1, source_target_pairs={{0,16},{16,32},{32,48},{48,64},{64,80},{80,96},{96,112},{112,128},... | collective-permute-start | bytes 172040 | tf_op jit(solution)/shard_map/ppermute | solution.py:242
  46.0 7.0 %collective-permute-start.7 = (f32[112,128]{1,0:T(8,128)}, f32[112,128]{1,0:T(8,128)S(1)}, u32[]{:S(2)}, u32[]{:S(2)}) collective-permute-start(f32[112,128]{1,0:T(8,128)} %get-tuple-element.25), channel_id=1, source_target_pairs={{0,496},{16,0},{32,16},{48,32},{64,48},{80,64},{96,80},{112,96},{1... | collective-permute-start | bytes 172040 | tf_op jit(solution)/shard_map/ppermute | solution.py:242
  51.5 1.6 %copy-start.5 = (f32[112,128]{1,0:T(8,128)}, f32[112,128]{1,0:T(8,128)S(1)}, u32[]{:S(2)}) copy-start(f32[112,128]{1,0:T(8,128)S(1)} %collective-permute-done.6.fw_ref) | copy-start | bytes 172036
  53.0 0.6 %copy-start.6 = (f32[112,128]{1,0:T(8,128)}, f32[112,128]{1,0:T(8,128)S(1)}, u32[]{:S(2)}) copy-start(f32[112,128]{1,0:T(8,128)S(1)} %collective-permute-done.7.fe_ref) | copy-start | bytes 172036
  53.0 0.7 %copy-start.2 = (f32[5,75,128]{2,1,0:T(8,128)}, f32[5,75,128]{2,1,0:T(8,128)S(1)}, u32[]{:S(2)}) copy-start(f32[5,75,128]{2,1,0:T(8,128)S(1)} %collective-permute-done.4.fn_ref) | copy-start | bytes 576004
  53.0 0.8 %copy-start.3 = (f32[5,75,128]{2,1,0:T(8,128)}, f32[5,75,128]{2,1,0:T(8,128)S(1)}, u32[]{:S(2)}) copy-start(f32[5,75,128]{2,1,0:T(8,128)S(1)} %collective-permute-done.5.fs_ref) | copy-start | bytes 576004

commit v6 on v5

v6 whole, which is shorter than its diff:
```python
import functools

import jax
import jax.numpy as jnp
from jax import lax
from jax.experimental import pallas as pl
from jax.experimental.pallas import tpu as pltpu
from jax.sharding import PartitionSpec as P

STEPS = 2
LANES = 128
HI = lax.Precision.HIGHEST
REC_ROW = 32
MSG_ROWS = 112


def _dot(a, b, dims):
    return lax.dot_general(a, b, (dims, ((), ())), precision=HI, preferred_element_type=jnp.float32)


def _split3(a):
    hi = a.astype(jnp.bfloat16)
    rest = a - hi.astype(jnp.float32)
    mid = rest.astype(jnp.bfloat16)
    lo = (rest - mid.astype(jnp.float32)).astype(jnp.bfloat16)
    return jnp.concatenate([hi, mid, lo], axis=0)


def _select(a, hot, dims):
    m = a.shape[0]
    part = lax.dot_general(_split3(a), hot.astype(jnp.bfloat16), (dims, ((), ())),
                           preferred_element_type=jnp.float32)
    return (part[:m] + part[m:2 * m]) + part[2 * m:]


def _pieces(count):
    return -(-count // LANES)


def _columns(block):
    count = block.shape[0]
    width = _pieces(count) * LANES
    padded = jnp.concatenate([block, jnp.zeros((width - count, LANES), jnp.float32)], axis=0)
    return padded.T


def _put_column(msg_ref, slot, vector):
    pieces = vector.shape[1] // LANES
    for j in range(pieces):
        row = slot * pieces + j
        msg_ref[pl.ds(row, 1), :] = vector[:, j * LANES:(j + 1) * LANES]


def _get_column(msg_ref, slot, pieces):
    return jnp.concatenate(
        [msg_ref[pl.ds(slot * pieces + j, 1), :] for j in range(pieces)], axis=1)


def _column_matrix(west, east, count):
    width = west.shape[-1]
    r = lax.broadcasted_iota(jnp.int32, (LANES, width), 0)
    grid = jnp.where(r == 0, west, jnp.where(r == LANES - 1, east, 0.0))
    return grid.T[:count]


def _one_hot(index_row, size):
    n = index_row.shape[1]
    return jnp.where(lax.broadcasted_iota(jnp.int32, (size, n), 0) == index_row, 1.0, 0.0)


def _send_records(msg_ref, prof, mass, index_row):
    slots = prof.shape[1]
    hot = _one_hot(index_row, slots)
    levels = prof.shape[0]
    cross = index_row.shape[1]
    rec = _select(jnp.concatenate([prof, mass, jnp.zeros((4, slots), jnp.float32)], axis=0), hot,
                  ((1,), (0,)))
    msg_ref[REC_ROW:REC_ROW + levels + 1, 0:cross] = rec[:levels + 1]


def _prep_kernel(fields, x_ref, c_ref, p_ref, m_ref, ie_ref, iw_ref, sn_ref, ss_ref, me_ref, mw_ref):
    f = pl.program_id(0)
    count = x_ref.shape[1]
    levels = count // 8

    @pl.when(f == 0)
    def _():
        me_ref[...] = jnp.zeros(me_ref.shape, jnp.float32)
        mw_ref[...] = jnp.zeros(mw_ref.shape, jnp.float32)
        ucols = _columns(c_ref[0])
        _put_column(me_ref, fields, ucols[LANES - 1:LANES])
        sn_ref[fields] = c_ref[1, pl.ds(7, levels, stride=8), :]
        prof = p_ref[...]
        mass = m_ref[...].reshape(1, -1)
        _send_records(me_ref, prof, mass, ie_ref[0:1, :])
        _send_records(mw_ref, prof, mass, iw_ref[0:1, :])

    cols = _columns(x_ref[0])
    _put_column(me_ref, f, cols[LANES - 1:LANES])
    _put_column(mw_ref, f, cols[0:1])
    sn_ref[f] = x_ref[0, pl.ds(7, levels, stride=8), :]
    ss_ref[f] = x_ref[0, pl.ds(0, levels, stride=8), :]


def _step_kernel(fields, step_index, with_sends, coef_ref, d_ref, x_ref, c_ref, p_ref, m_ref, cell_ref,
                 ie_ref, iw_ref, fn_ref, fs_ref, fw_ref, fe_ref, cs_ref, cw_ref, *rest):
    if with_sends:
        o_ref, po_ref, mo_ref, sn_ref, ss_ref, me_ref, mw_ref = rest[:7]
    else:
        o_ref, po_ref, mo_ref = rest[:3]
    hscr, sscr, dscr, k_c, k_e, k_w, k_n, k_s, k_ew, k_ns = rest[-10:]
    f = pl.program_id(0)
    count = x_ref.shape[1]
    levels = count // 8
    pieces = _pieces(count)
    slots = p_ref.shape[1]
    cross = ie_ref.shape[1]
    cells = 8 * LANES

    @pl.when(f == 0)
    def _():
        hot_e = _one_hot(ie_ref[step_index:step_index + 1, :], slots)
        hot_w = _one_hot(iw_ref[step_index:step_index + 1, :], slots)
        rec_e = fw_ref[REC_ROW:REC_ROW + levels + 5, 0:cross]
        rec_w = fe_ref[REC_ROW:REC_ROW + levels + 5, 0:cross]
        placed = _select(rec_e, hot_e, ((1,), (1,))) + _select(rec_w, hot_w, ((1,), (1,)))
        taken = lax.dot_general(jnp.ones((8, cross), jnp.bfloat16), (hot_e + hot_w).astype(jnp.bfloat16),
                                (((1,), (1,)), ((), ())), preferred_element_type=jnp.float32)[0:1]
        moved = taken > 0.5
        prof = jnp.where(moved, placed[:levels], p_ref[...])
        mass = jnp.where(moved, placed[levels:levels + 1], m_ref[...].reshape(1, -1))

        temp = jnp.concatenate([x_ref[0, pl.ds(r, levels, stride=8), :] for r in range(8)], axis=1)
        hot_c = _one_hot(cell_ref[step_index:step_index + 1, :], cells)
        water = _select(temp, hot_c, ((1,), (0,)))
        z = water + 1.8
        soft = jnp.maximum(z, 0.0) + jnp.log1p(jnp.exp(-jnp.abs(z)))
        melt = prof * soft * jnp.sqrt(mass)
        source = _select(melt, hot_c, ((1,), (1,)))
        mass_new = mass / (1.0 + 0.05 * jnp.sum(melt, axis=0, keepdims=True))
        po_ref[...] = prof
        mo_ref[...] = mass_new.reshape(-1)
        for r in range(8):
            sscr[pl.ds(r, levels, stride=8), :] = source[:, r * LANES:(r + 1) * LANES]
        for l in range(levels):
            dscr[l * 8:(l + 1) * 8, :] = jnp.full((8, LANES), d_ref[l], jnp.float32)

        rows = lax.broadcasted_iota(jnp.int32, (count, LANES), 0) % 8
        lanes = lax.broadcasted_iota(jnp.int32, (count, LANES), 1)
        u = c_ref[0]
        v = c_ref[1]
        d = dscr[...]
        zero_row = jnp.zeros((1, pieces * LANES), jnp.float32)
        u_halo = _column_matrix(_get_column(cw_ref, fields, pieces), zero_row, count)
        u_w = jnp.where(lanes == 0, u_halo, pltpu.roll(u, 1, 1))
        hscr[...] = jnp.zeros(hscr.shape, jnp.float32)
        hscr[pl.ds(0, levels, stride=8), :] = cs_ref[0]
        v_s = jnp.where(rows == 0, hscr[...], pltpu.roll(v, 1, 0))
        a_c = 1.0 - jnp.maximum(u, 0.0) + jnp.minimum(u_w, 0.0) - jnp.maximum(v, 0.0) + jnp.minimum(v_s, 0.0) - 4.0 * d
        a_e = d - jnp.minimum(u, 0.0)
        a_w = d + jnp.maximum(u_w, 0.0)
        a_n = d - jnp.minimum(v, 0.0)
        a_s = d + jnp.maximum(v_s, 0.0)
        last_lane = lanes == LANES - 1
        first_lane = lanes == 0
        top_row = rows == 7
        bottom_row = rows == 0
        k_c[...] = a_c
        k_ew[...] = jnp.where(last_lane, a_e, jnp.where(first_lane, a_w, 0.0))
        k_ns[...] = jnp.where(top_row, a_n, jnp.where(bottom_row, a_s, 0.0))
        k_e[...] = jnp.where(last_lane, 0.0, a_e)
        k_w[...] = jnp.where(first_lane, 0.0, a_w)
        k_n[...] = jnp.where(top_row, 0.0, a_n)
        k_s[...] = jnp.where(bottom_row, 0.0, a_s)
        if with_sends:
            me_ref[...] = jnp.zeros(me_ref.shape, jnp.float32)
            mw_ref[...] = jnp.zeros(mw_ref.shape, jnp.float32)
            nxt = step_index + 1
            _send_records(me_ref, prof, mass_new, ie_ref[nxt:nxt + 1, :])
            _send_records(mw_ref, prof, mass_new, iw_ref[nxt:nxt + 1, :])

    c = x_ref[0]
    halo = _column_matrix(_get_column(fw_ref, f, pieces), _get_column(fe_ref, f, pieces), count)
    hscr[pl.ds(7, levels, stride=8), :] = fn_ref[0]
    hscr[pl.ds(0, levels, stride=8), :] = fs_ref[0]
    hrow = hscr[...]
    out = (k_c[...] * c + k_e[...] * pltpu.roll(c, LANES - 1, 1) + k_w[...] * pltpu.roll(c, 1, 1)
           + k_n[...] * pltpu.roll(c, count - 1, 0) + k_s[...] * pltpu.roll(c, 1, 0)
           + k_ew[...] * halo + k_ns[...] * hrow + coef_ref[f] * sscr[...])
    o_ref[0] = out
    if with_sends:
        cols = _columns(out)
        _put_column(me_ref, f, cols[LANES - 1:LANES])
        _put_column(mw_ref, f, cols[0:1])
        sn_ref[0] = o_ref[0, pl.ds(7, levels, stride=8), :]
        ss_ref[0] = o_ref[0, pl.ds(0, levels, stride=8), :]


def _vmem():
    return pl.BlockSpec(memory_space=pltpu.VMEM)


def _f32(shape):
    return jax.ShapeDtypeStruct(shape, jnp.float32)


def _whole(shape):
    return pl.BlockSpec(shape, lambda f: (0,) * len(shape))


def _field(shape):
    return pl.BlockSpec((1,) + tuple(shape[1:]), lambda f: (f,) + (0,) * (len(shape) - 1))


def prep(x, c, prof, mass, ie, iw):
    fields, count, _ = x.shape
    levels = count // 8
    out_shape = (
        _f32((fields + 1, levels, LANES)),
        _f32((fields, levels, LANES)),
        _f32((MSG_ROWS, LANES)),
        _f32((MSG_ROWS, LANES)),
    )
    return pl.pallas_call(
        functools.partial(_prep_kernel, fields),
        grid=(fields,),
        out_shape=out_shape,
        in_specs=[_field(x.shape)] + [_whole(a.shape) for a in (c, prof, mass, ie, iw)],
        out_specs=tuple(_whole(o.shape) for o in out_shape),
    )(x, c, prof, mass, ie, iw)


def step(step_index, with_sends, coef, d, x, c, prof, mass, cell, ie, iw, fn, fs, fw, fe, cs, cw):
    fields, count, _ = x.shape
    levels = count // 8
    outs = [_f32(x.shape), _f32(prof.shape), _f32(mass.shape)]
    out_specs = [_field(x.shape), _whole(prof.shape), _whole(mass.shape)]
    if with_sends:
        outs += [
            _f32((fields, levels, LANES)),
            _f32((fields, levels, LANES)),
            _f32((MSG_ROWS, LANES)),
            _f32((MSG_ROWS, LANES)),
        ]
        out_specs += [_field(outs[3].shape), _field(outs[4].shape), _whole(outs[5].shape),
                      _whole(outs[6].shape)]
    smem = pl.BlockSpec(memory_space=pltpu.SMEM)
    in_specs = [smem, smem, _field(x.shape)] + [_whole(a.shape) for a in (c, prof, mass, cell, ie, iw)]
    in_specs += [_field(fn.shape), _field(fs.shape), _whole(fw.shape), _whole(fe.shape),
                 pl.BlockSpec((1, levels, LANES), lambda f: (fields, 0, 0)), _whole(cw.shape)]
    return pl.pallas_call(
        functools.partial(_step_kernel, fields, step_index, with_sends),
        grid=(fields,),
        out_shape=tuple(outs),
        in_specs=in_specs,
        out_specs=tuple(out_specs),
        scratch_shapes=[pltpu.VMEM((count, LANES), jnp.float32)] * 10,
    )(coef, d, x, c, prof, mass, cell, ie, iw, fn, fs, fw, fe, cs, cw)


def shift(value, axis, steps, periodic):
    count = lax.axis_size(axis)
    if periodic:
        pairs = [(s, (s + steps) % count) for s in range(count)]
    else:
        pairs = [(s, s + steps) for s in range(count) if 0 <= s + steps < count]
    return lax.ppermute(value, axis, pairs)


def per_device(tracers, courant, diffusivity, melt_coef, berg_profile, berg_mass, berg_cell,
               send_east, send_west):
    fields, levels, rows, cols = tracers.shape
    count = levels * rows
    x = tracers.reshape(fields, count, cols)
    c = courant.reshape(2, count, cols)
    d = diffusivity
    prof = berg_profile
    mass = berg_mass
    sn, ss, me, mw = prep(x, c, prof, mass, send_east, send_west)
    cs = cw = None
    for step_index in range(STEPS):
        from_s = shift(sn, "lat", 1, False)
        from_n = shift(ss, "lat", -1, False)
        from_w = shift(me, "lon", 1, True)
        from_e = shift(mw, "lon", -1, True)
        if cs is None:
            cs, cw = from_s, from_w
        with_sends = step_index < STEPS - 1
        result = step(step_index, with_sends, melt_coef, d, x, c, prof, mass, berg_cell, send_east,
                      send_west, from_n, from_s, from_w, from_e, cs, cw)
        if with_sends:
            x, prof, mass, sn, ss, me, mw = result
        else:
            x, prof, mass = result
    return (x.reshape(fields, levels, rows, cols), mass)


def solution(mesh):
    in_specs = (
        P(None, None, "lat", "lon"),
        P(None, None, "lat", "lon"),
        P(),
        P(),
        P(None, ("lon", "lat")),
        P(("lon", "lat")),
        P(None, ("lon", "lat")),
        P(None, ("lon", "lat")),
        P(None, ("lon", "lat")),
    )
    out_specs = (P(None, None, "lat", "lon"), P(("lon", "lat")))
    return jax.shard_map(
        per_device, mesh=mesh, in_specs=in_specs, out_specs=out_specs, check_vma=False
    )
```

time: 59.8 us -> 64.3 us (1.075)
  Pallas kernels: 15 us -> 19.4 us
    pallas_call x3, Pallas kernels: 15 us -> 19.4 us  [the longest x2 14.6 us: step(): pl.pallas_call(functools.partial(_step_kernel, fields, step_index, with_s...]
where the time goes in v6:
time: 64.3 us; the launch traced here: 63.7 us
  starting transfers between devices  38.3 us (60%)
  Pallas kernels  19.4 us (30%)
  waiting for transfers between devices  3.19 us (5%)
  local copies, waits for them, and re-layouts  2.12 us (3%)
  between operations  0.75 us (1%)
    ppermute x8, starting transfers between devices, shift(): return lax.ppermute(value, axis, pairs)  38.3 us
    pallas_call x2, Pallas kernels, step(): pl.pallas_call(functools.partial(_step_kernel, fields, step_index, with_s...  14.6 us
    pallas_call x1, Pallas kernels, prep(): pl.pallas_call(functools.partial(_prep_kernel, fields), grid=(fields,), o...  4.74 us
    ppermute x8, waiting for transfers between devices, shift(): return lax.ppermute(value, axis, pairs)  3.19 us
    unnamed x16, local copies, waits for them, and re-layouts  2.12 us
  transfers between devices with their start and end apart: 8, of which 3 were waited for; matrix products, arithmetic and copies ran while one was open for 0% of the time, Pallas kernels for 0%

profile of v6, /device:TPU:7, one launch (start us, length us, event | category | flops | bytes accessed | tf_op | source)
XLA Modules:
  0.0 63.7 jit_solution(4772338836799841763)
XLA Ops:
  0.6 4.7 %shard_map.104 = (f32[6,75,128]{2,1,0:T(8,128)}, f32[5,75,128]{2,1,0:T(8,128)}, f32[112,128]{1,0:T(8,128)}, f32[112,128]{1,0:T(8,128)}) custom-call(f32[5,600,128]{2,1,0:T(8,128)} %bitcast.3, f32[2,600,128]{2,1,0:T(8,128)} %bitcast.5, f32[75,384]{1,0:T(8,128)} %p_ref.3, f32[384]{0:T(512)} %m_ref.3, s32[2,32]{1,0:T(2,128)} %ie_ref.5, s32[2,32]{1,0:T(2,128)} %iw_ref.5), custom_call_target="tpu_custom_call" | custom-call | tf_op jit(solution)/shard_map/pallas_call | solution.py:224
  5.4 5.3 %collective-permute-start.1 = (f32[6,75,128]{2,1,0:T(8,128)}, f32[6,75,128]{2,1,0:T(8,128)S(1)}, u32[]{:S(2)}, u32[]{:S(2)}) collective-permute-start(f32[6,75,128]{2,1,0:T(8,128)} %get-tuple-element.16), channel_id=1, source_target_pairs={{0,1},{1,2},{2,3},{3,4},{4,5},{5,6},{6,7},{7,8},{8,9},{9,10},{10,1... | collective-permute-start | bytes 691208 | tf_op jit(solution)/shard_map/ppermute | solution.py:267
  10.7 1.9 %collective-permute-start = (f32[5,75,128]{2,1,0:T(8,128)}, f32[5,75,128]{2,1,0:T(8,128)S(1)}, u32[]{:S(2)}, u32[]{:S(2)}) collective-permute-start(f32[5,75,128]{2,1,0:T(8,128)} %get-tuple-element.15), channel_id=1, source_target_pairs={{1,0},{2,1},{3,2},{4,3},{5,4},{6,5},{7,6},{8,7},{9,8},{10,9},{11,1... | collective-permute-start | bytes 576008 | tf_op jit(solution)/shard_map/ppermute | solution.py:267
  12.6 3.5 %collective-permute-start.2 = (f32[112,128]{1,0:T(8,128)}, f32[112,128]{1,0:T(8,128)S(1)}, u32[]{:S(2)}, u32[]{:S(2)}) collective-permute-start(f32[112,128]{1,0:T(8,128)} %get-tuple-element.17), channel_id=1, source_target_pairs={{0,16},{16,32},{32,48},{48,64},{64,80},{80,96},{96,112},{112,128},... | collective-permute-start | bytes 172040 | tf_op jit(solution)/shard_map/ppermute | solution.py:267
  16.1 9.6 %collective-permute-start.3 = (f32[112,128]{1,0:T(8,128)}, f32[112,128]{1,0:T(8,128)S(1)}, u32[]{:S(2)}, u32[]{:S(2)}) collective-permute-start(f32[112,128]{1,0:T(8,128)} %get-tuple-element.18), channel_id=1, source_target_pairs={{0,496},{16,0},{32,16},{48,32},{64,48},{80,64},{96,80},{112,96},{1... | collective-permute-start | bytes 172040 | tf_op jit(solution)/shard_map/ppermute | solution.py:267
  25.8 0.6 %collective-permute-done.2.fw_ref.cw_ref = f32[112,128]{1,0:T(8,128)S(1)} collective-permute-done((f32[112,128]{1,0:T(8,128)}, f32[112,128]{1,0:T(8,128)S(1)}, u32[]{:S(2)}, u32[]{:S(2)}) %collective-permute-start.2) | collective-permute-done | bytes 57376 | tf_op jit(solution)/shard_map/ppermute | solution.py:267
  26.4 0.0 copy-start.1
  26.4 1.0 %collective-permute-done.3.fe_ref = f32[112,128]{1,0:T(8,128)S(1)} collective-permute-done((f32[112,128]{1,0:T(8,128)}, f32[112,128]{1,0:T(8,128)S(1)}, u32[]{:S(2)}, u32[]{:S(2)}) %collective-permute-start.3) | collective-permute-done | bytes 57376 | tf_op jit(solution)/shard_map/ppermute | solution.py:267
  27.4 0.0 copy-start.7
  27.4 0.0 collective-permute-done.fn_ref
  27.4 0.0 copy-start.4
  27.4 0.0 collective-permute-done.1.fs_ref.cs_ref
  27.4 0.0 copy-done.1
  27.4 0.6 copy-done.7
  28.0 0.1 copy-done.4
  28.1 0.0 copy-start
  28.1 0.7 %copy-done = f32[6,75,128]{2,1,0:T(8,128)} copy-done((f32[6,75,128]{2,1,0:T(8,128)}, f32[6,75,128]{2,1,0:T(8,128)S(1)}, u32[]{:S(2)}) %copy-start) | copy-done | bytes 230424
  28.8 7.4 %shard_map.105 = (f32[5,600,128]{2,1,0:T(8,128)}, f32[75,384]{1,0:T(8,128)}, f32[384]{0:T(512)}, f32[5,75,128]{2,1,0:T(8,128)}, f32[5,75,128]{2,1,0:T(8,128)}, /*index=5*/f32[112,128]{1,0:T(8,128)}, f32[112,128]{1,0:T(8,128)}) custom-call(f32[5]{0:T(128)} %coef_ref.3, f32[75]{0:T(128)} %d_ref.3, f32[5,600,128]{2,1,0:T(8,128)} %bitcast.4, ...), custom_call_target="tpu_custom_call" | custom-call | tf_op jit(solution)/shard_map/pallas_call | solution.py:251
  36.2 2.7 %collective-permute-start.4 = (f32[5,75,128]{2,1,0:T(8,128)}, f32[5,75,128]{2,1,0:T(8,128)S(1)}, u32[]{:S(2)}, u32[]{:S(2)}) collective-permute-start(f32[5,75,128]{2,1,0:T(8,128)} %get-tuple-element.22), channel_id=1, source_target_pairs={{1,0},{2,1},{3,2},{4,3},{5,4},{6,5},{7,6},{8,7},{9,8},{10,9},{11,1... | collective-permute-start | bytes 576008 | tf_op jit(solution)/shard_map/ppermute | solution.py:267
  38.9 7.9 %collective-permute-start.5 = (f32[5,75,128]{2,1,0:T(8,128)}, f32[5,75,128]{2,1,0:T(8,128)S(1)}, u32[]{:S(2)}, u32[]{:S(2)}) collective-permute-start(f32[5,75,128]{2,1,0:T(8,128)} %get-tuple-element.23), channel_id=1, source_target_pairs={{0,1},{1,2},{2,3},{3,4},{4,5},{5,6},{6,7},{7,8},{8,9},{9,10},{10,1... | collective-permute-start | bytes 576008 | tf_op jit(solution)/shard_map/ppermute | solution.py:267
  46.8 1.9 %collective-permute-start.6 = (f32[112,128]{1,0:T(8,128)}, f32[112,128]{1,0:T(8,128)S(1)}, u32[]{:S(2)}, u32[]{:S(2)}) collective-permute-start(f32[112,128]{1,0:T(8,128)} %get-tuple-element.24), channel_id=1, source_target_pairs={{0,16},{16,32},{32,48},{48,64},{64,80},{80,96},{96,112},{112,128},... | collective-permute-start | bytes 172040 | tf_op jit(solution)/shard_map/ppermute | solution.py:267
  48.7 5.5 %collective-permute-start.7 = (f32[112,128]{1,0:T(8,128)}, f32[112,128]{1,0:T(8,128)S(1)}, u32[]{:S(2)}, u32[]{:S(2)}) collective-permute-start(f32[112,128]{1,0:T(8,128)} %get-tuple-element.25), channel_id=1, source_target_pairs={{0,496},{16,0},{32,16},{48,32},{64,48},{80,64},{96,80},{112,96},{1... | collective-permute-start | bytes 172040 | tf_op jit(solution)/shard_map/ppermute | solution.py:267
  54.2 0.0 collective-permute-done.6.fw_ref
  54.2 0.0 copy-start.5
  54.2 1.5 %collective-permute-done.7.fe_ref = f32[112,128]{1,0:T(8,128)S(1)} collective-permute-done((f32[112,128]{1,0:T(8,128)}, f32[112,128]{1,0:T(8,128)S(1)}, u32[]{:S(2)}, u32[]{:S(2)}) %collective-permute-start.7) | collective-permute-done | bytes 57376 | tf_op jit(solution)/shard_map/ppermute | solution.py:267
  55.7 0.0 copy-start.6
  55.7 0.0 collective-permute-done.4.fn_ref
  55.7 0.0 copy-start.2
  55.7 0.0 collective-permute-done.5.fs_ref
  55.7 0.0 copy-start.3
  55.7 0.0 copy-done.5
  55.8 0.6 copy-done.6
  56.3 0.1 copy-done.2
  56.4 0.1 copy-done.3
  56.5 7.2 %shard_map.106 = (f32[5,600,128]{2,1,0:T(8,128)}, f32[75,384]{1,0:T(8,128)}, f32[384]{0:T(512)}) custom-call(f32[5]{0:T(128)} %coef_ref.3, f32[75]{0:T(128)} %d_ref.3, f32[5,600,128]{2,1,0:T(8,128)} %get-tuple-element.19.x_ref, f32[2,600,128]{2,1,0:T(8,128)} %bitcast.7, f32[75,384]{1,0:T(8,128)} %get-tuple-element.20.p_ref, f32[384]{0:T(512)} %get-tuple-element.21.m_ref, ...), custom_call_target="tpu_custom_call" | custom-call | tf_op jit(solution)/shard_map/pallas_call | solution.py:251
Async XLA Ops:
  5.4 22.1 %collective-permute-start.1 = (f32[6,75,128]{2,1,0:T(8,128)}, f32[6,75,128]{2,1,0:T(8,128)S(1)}, u32[]{:S(2)}, u32[]{:S(2)}) collective-permute-start(f32[6,75,128]{2,1,0:T(8,128)} %get-tuple-element.16), channel_id=1, source_target_pairs={{0,1},{1,2},{2,3},{3,4},{4,5},{5,6},{6,7},{7,8},{8,9},{9,10},{10,1... | collective-permute-start | bytes 691208 | tf_op jit(solution)/shard_map/ppermute | solution.py:267
  10.7 16.8 %collective-permute-start = (f32[5,75,128]{2,1,0:T(8,128)}, f32[5,75,128]{2,1,0:T(8,128)S(1)}, u32[]{:S(2)}, u32[]{:S(2)}) collective-permute-start(f32[5,75,128]{2,1,0:T(8,128)} %get-tuple-element.15), channel_id=1, source_target_pairs={{1,0},{2,1},{3,2},{4,3},{5,4},{6,5},{7,6},{8,7},{9,8},{10,9},{11,1... | collective-permute-start | bytes 576008 | tf_op jit(solution)/shard_map/ppermute | solution.py:267
  12.6 13.8 %collective-permute-start.2 = (f32[112,128]{1,0:T(8,128)}, f32[112,128]{1,0:T(8,128)S(1)}, u32[]{:S(2)}, u32[]{:S(2)}) collective-permute-start(f32[112,128]{1,0:T(8,128)} %get-tuple-element.17), channel_id=1, source_target_pairs={{0,16},{16,32},{32,48},{48,64},{64,80},{80,96},{96,112},{112,128},... | collective-permute-start | bytes 172040 | tf_op jit(solution)/shard_map/ppermute | solution.py:267
  16.1 11.3 %collective-permute-start.3 = (f32[112,128]{1,0:T(8,128)}, f32[112,128]{1,0:T(8,128)S(1)}, u32[]{:S(2)}, u32[]{:S(2)}) collective-permute-start(f32[112,128]{1,0:T(8,128)} %get-tuple-element.18), channel_id=1, source_target_pairs={{0,496},{16,0},{32,16},{48,32},{64,48},{80,64},{96,80},{112,96},{1... | collective-permute-start | bytes 172040 | tf_op jit(solution)/shard_map/ppermute | solution.py:267
  26.4 1.0 %copy-start.1 = (f32[112,128]{1,0:T(8,128)}, f32[112,128]{1,0:T(8,128)S(1)}, u32[]{:S(2)}) copy-start(f32[112,128]{1,0:T(8,128)S(1)} %collective-permute-done.2.fw_ref.cw_ref) | copy-start | bytes 172036
  27.4 0.6 copy-start.7
  27.4 0.7 %copy-start.4 = (f32[5,75,128]{2,1,0:T(8,128)}, f32[5,75,128]{2,1,0:T(8,128)S(1)}, u32[]{:S(2)}) copy-start(f32[5,75,128]{2,1,0:T(8,128)S(1)} %collective-permute-done.fn_ref) | copy-start | bytes 576004
  28.1 0.7 %copy-start = (f32[6,75,128]{2,1,0:T(8,128)}, f32[6,75,128]{2,1,0:T(8,128)S(1)}, u32[]{:S(2)}) copy-start(f32[6,75,128]{2,1,0:T(8,128)S(1)} %collective-permute-done.1.fs_ref.cs_ref) | copy-start | bytes 691204
  36.2 19.5 %collective-permute-start.4 = (f32[5,75,128]{2,1,0:T(8,128)}, f32[5,75,128]{2,1,0:T(8,128)S(1)}, u32[]{:S(2)}, u32[]{:S(2)}) collective-permute-start(f32[5,75,128]{2,1,0:T(8,128)} %get-tuple-element.22), channel_id=1, source_target_pairs={{1,0},{2,1},{3,2},{4,3},{5,4},{6,5},{7,6},{8,7},{9,8},{10,9},{11,1... | collective-permute-start | bytes 576008 | tf_op jit(solution)/shard_map/ppermute | solution.py:267
  38.9 16.8 %collective-permute-start.5 = (f32[5,75,128]{2,1,0:T(8,128)}, f32[5,75,128]{2,1,0:T(8,128)S(1)}, u32[]{:S(2)}, u32[]{:S(2)}) collective-permute-start(f32[5,75,128]{2,1,0:T(8,128)} %get-tuple-element.23), channel_id=1, source_target_pairs={{0,1},{1,2},{2,3},{3,4},{4,5},{5,6},{6,7},{7,8},{8,9},{9,10},{10,1... | collective-permute-start | bytes 576008 | tf_op jit(solution)/shard_map/ppermute | solution.py:267
  46.8 7.4 %collective-permute-start.6 = (f32[112,128]{1,0:T(8,128)}, f32[112,128]{1,0:T(8,128)S(1)}, u32[]{:S(2)}, u32[]{:S(2)}) collective-permute-start(f32[112,128]{1,0:T(8,128)} %get-tuple-element.24), channel_id=1, source_target_pairs={{0,16},{16,32},{32,48},{48,64},{64,80},{80,96},{96,112},{112,128},... | collective-permute-start | bytes 172040 | tf_op jit(solution)/shard_map/ppermute | solution.py:267
  48.7 7.0 %collective-permute-start.7 = (f32[112,128]{1,0:T(8,128)}, f32[112,128]{1,0:T(8,128)S(1)}, u32[]{:S(2)}, u32[]{:S(2)}) collective-permute-start(f32[112,128]{1,0:T(8,128)} %get-tuple-element.25), channel_id=1, source_target_pairs={{0,496},{16,0},{32,16},{48,32},{64,48},{80,64},{96,80},{112,96},{1... | collective-permute-start | bytes 172040 | tf_op jit(solution)/shard_map/ppermute | solution.py:267
  54.2 1.6 %copy-start.5 = (f32[112,128]{1,0:T(8,128)}, f32[112,128]{1,0:T(8,128)S(1)}, u32[]{:S(2)}) copy-start(f32[112,128]{1,0:T(8,128)S(1)} %collective-permute-done.6.fw_ref) | copy-start | bytes 172036
  55.7 0.6 copy-start.6
  55.7 0.7 %copy-start.2 = (f32[5,75,128]{2,1,0:T(8,128)}, f32[5,75,128]{2,1,0:T(8,128)S(1)}, u32[]{:S(2)}) copy-start(f32[5,75,128]{2,1,0:T(8,128)S(1)} %collective-permute-done.4.fn_ref) | copy-start | bytes 576004
  55.7 0.8 %copy-start.3 = (f32[5,75,128]{2,1,0:T(8,128)}, f32[5,75,128]{2,1,0:T(8,128)S(1)}, u32[]{:S(2)}) copy-start(f32[5,75,128]{2,1,0:T(8,128)S(1)} %collective-permute-done.5.fs_ref) | copy-start | bytes 576004

commit v7 on v5

--- a/solution.py
+++ b/solution.py
@@ -98,23 +98,42 @@
     _send_records(mw_ref, prof, mass, iw_ref[0:1, :])
 
 
-def _step_kernel(step_index, with_sends, coef_ref, d_ref, x_ref, c_ref, p_ref, m_ref, cell_ref,
-                 ie_ref, iw_ref, fn_ref, fs_ref, fw_ref, fe_ref, cs_ref, cw_ref, *rest):
+def _step_kernel(step_index, with_sends, coef_ref, d_ref, p_ref, m_ref, cell_ref, ie_ref, iw_ref,
+                 x_hbm, c_hbm, fn_hbm, fs_hbm, fw_hbm, fe_hbm, cs_hbm, cw_hbm, *rest):
     if with_sends:
-        o_ref, po_ref, mo_ref, sn_ref, ss_ref, me_ref, mw_ref, hscr, sscr, dscr = rest
+        o_hbm, po_ref, mo_ref, sn_ref, ss_ref, me_ref, mw_ref = rest[:7]
     else:
-        o_ref, po_ref, mo_ref, hscr, sscr, dscr = rest
-    fields, count, _ = x_ref.shape
+        o_hbm, po_ref, mo_ref = rest[:3]
+    (xv, cv, fnv, fsv, fwv, fev, csv, cwv, ov, hscr, sscr, dscr, sem) = rest[-13:]
+    fields, count, _ = xv.shape
     levels = count // 8
     pieces = _pieces(count)
     slots = p_ref.shape[1]
     cross = ie_ref.shape[1]
     cells = 8 * LANES
 
+    def fetch(src, dst, k):
+        cp = pltpu.make_async_copy(src, dst, sem.at[k])
+        cp.start()
+        return cp
+
+    c_fw = fetch(fw_hbm, fwv, 0)
+    c_fe = fetch(fe_hbm, fev, 1)
+    c_x = [fetch(x_hbm.at[0], xv.at[0], 2)]
+    c_c = fetch(c_hbm, cv, 3)
+    c_cs = fetch(cs_hbm.at[fields], csv, 4)
+    c_cw = fetch(cw_hbm, cwv, 5)
+    c_fn = fetch(fn_hbm, fnv, 6)
+    c_fs = fetch(fs_hbm.at[pl.ds(0, fields)], fsv, 7)
+    for f in range(1, fields):
+        c_x.append(fetch(x_hbm.at[f], xv.at[f], 7 + f))
+
+    c_fw.wait()
+    c_fe.wait()
     hot_e = _one_hot(ie_ref[step_index:step_index + 1, :], slots)
     hot_w = _one_hot(iw_ref[step_index:step_index + 1, :], slots)
-    rec_e = fw_ref[REC_ROW:REC_ROW + levels + 5, 0:cross]
-    rec_w = fe_ref[REC_ROW:REC_ROW + levels + 5, 0:cross]
+    rec_e = fwv[REC_ROW:REC_ROW + levels + 5, 0:cross]
+    rec_w = fev[REC_ROW:REC_ROW + levels + 5, 0:cross]
     placed = _select(rec_e, hot_e, ((1,), (1,))) + _select(rec_w, hot_w, ((1,), (1,)))
     taken = lax.dot_general(jnp.ones((8, cross), jnp.bfloat16), (hot_e + hot_w).astype(jnp.bfloat16),
                             (((1,), (1,)), ((), ())), preferred_element_type=jnp.float32)[0:1]
@@ -122,7 +141,8 @@
     prof = jnp.where(moved, placed[:levels], p_ref[...])
     mass = jnp.where(moved, placed[levels:levels + 1], m_ref[...].reshape(1, -1))
 
-    temp = jnp.concatenate([x_ref[0, pl.ds(r, levels, stride=8), :] for r in range(8)], axis=1)
+    c_x[0].wait()
+    temp = jnp.concatenate([xv[0, pl.ds(r, levels, stride=8), :] for r in range(8)], axis=1)
     hot_c = _one_hot(cell_ref[step_index:step_index + 1, :], cells)
     water = _select(temp, hot_c, ((1,), (0,)))
     z = water + 1.8
@@ -136,17 +156,26 @@
         sscr[pl.ds(r, levels, stride=8), :] = source[:, r * LANES:(r + 1) * LANES]
     for l in range(levels):
         dscr[l * 8:(l + 1) * 8, :] = jnp.full((8, LANES), d_ref[l], jnp.float32)
-
+    if with_sends:
+        me_ref[...] = jnp.zeros(me_ref.shape, jnp.float32)
+        mw_ref[...] = jnp.zeros(mw_ref.shape, jnp.float32)
+        nxt = step_index + 1
+        _send_records(me_ref, prof, mass_new, ie_ref[nxt:nxt + 1, :])
+        _send_records(mw_ref, prof, mass_new, iw_ref[nxt:nxt + 1, :])
+
+    c_c.wait()
+    c_cs.wait()
+    c_cw.wait()
     rows = lax.broadcasted_iota(jnp.int32, (count, LANES), 0) % 8
     lanes = lax.broadcasted_iota(jnp.int32, (count, LANES), 1)
-    u = c_ref[0]
-    v = c_ref[1]
+    u = cv[0]
+    v = cv[1]
     d = dscr[...]
     zero_row = jnp.zeros((1, pieces * LANES), jnp.float32)
-    u_halo = _column_matrix(_get_column(cw_ref, fields, pieces), zero_row, count)
+    u_halo = _column_matrix(_get_column(cwv, fields, pieces), zero_row, count)
     u_w = jnp.where(lanes == 0, u_halo, pltpu.roll(u, 1, 1))
     hscr[...] = jnp.zeros(hscr.shape, jnp.float32)
-    hscr[pl.ds(0, levels, stride=8), :] = cs_ref[fields]
+    hscr[pl.ds(0, levels, stride=8), :] = csv[...]
     v_s = jnp.where(rows == 0, hscr[...], pltpu.roll(v, 1, 0))
     a_c = 1.0 - jnp.maximum(u, 0.0) + jnp.minimum(u_w, 0.0) - jnp.maximum(v, 0.0) + jnp.minimum(v_s, 0.0) - 4.0 * d
     a_e = d - jnp.minimum(u, 0.0)
@@ -164,29 +193,32 @@
     a_n = jnp.where(top_row, 0.0, a_n)
     a_s = jnp.where(bottom_row, 0.0, a_s)
     src = sscr[...]
-    if with_sends:
-        me_ref[...] = jnp.zeros(me_ref.shape, jnp.float32)
-        mw_ref[...] = jnp.zeros(mw_ref.shape, jnp.float32)
+    c_fn.wait()
+    c_fs.wait()
+    outs = []
     for f in range(fields):
-        c = x_ref[f]
-        halo = _column_matrix(_get_column(fw_ref, f, pieces), _get_column(fe_ref, f, pieces), count)
-        hscr[pl.ds(7, levels, stride=8), :] = fn_ref[f]
-        hscr[pl.ds(0, levels, stride=8), :] = fs_ref[f]
+        if f > 0:
+            c_x[f].wait()
+        c = xv[f]
+        halo = _column_matrix(_get_column(fwv, f, pieces), _get_column(fev, f, pieces), count)
+        hscr[pl.ds(7, levels, stride=8), :] = fnv[f]
+        hscr[pl.ds(0, levels, stride=8), :] = fsv[f]
         hrow = hscr[...]
         out = (a_c * c + a_e * pltpu.roll(c, LANES - 1, 1) + a_w * pltpu.roll(c, 1, 1)
                + a_n * pltpu.roll(c, count - 1, 0) + a_s * pltpu.roll(c, 1, 0)
                + a_ew * halo + a_ns * hrow + coef_ref[f] * src)
-        o_ref[f] = out
+        ov[f] = out
+        cp = pltpu.make_async_copy(ov.at[f], o_hbm.at[f], sem.at[7 + fields + f])
+        cp.start()
+        outs.append(cp)
         if with_sends:
             cols = _columns(out)
             _put_column(me_ref, f, cols[LANES - 1:LANES])
             _put_column(mw_ref, f, cols[0:1])
-            sn_ref[f] = o_ref[f, pl.ds(7, levels, stride=8), :]
-            ss_ref[f] = o_ref[f, pl.ds(0, levels, stride=8), :]
-    if with_sends:
-        nxt = step_index + 1
-        _send_records(me_ref, prof, mass_new, ie_ref[nxt:nxt + 1, :])
-        _send_records(mw_ref, prof, mass_new, iw_ref[nxt:nxt + 1, :])
+            sn_ref[f] = ov[f, pl.ds(7, levels, stride=8), :]
+            ss_ref[f] = ov[f, pl.ds(0, levels, stride=8), :]
+    for cp in outs:
+        cp.wait()
 
 
 def _vmem():
@@ -216,7 +248,9 @@
 def step(step_index, with_sends, coef, d, x, c, prof, mass, cell, ie, iw, fn, fs, fw, fe, cs, cw):
     fields, count, _ = x.shape
     levels = count // 8
+    anyspace = pl.BlockSpec(memory_space=pl.ANY)
     outs = [_f32(x.shape), _f32(prof.shape), _f32(mass.shape)]
+    out_specs = [anyspace, _vmem(), _vmem()]
     if with_sends:
         outs += [
             _f32((fields, levels, LANES)),
@@ -224,13 +258,30 @@
             _f32((MSG_ROWS, LANES)),
             _f32((MSG_ROWS, LANES)),
         ]
+        out_specs += [_vmem()] * 4
+    smem = pl.BlockSpec(memory_space=pltpu.SMEM)
+    scratch = [
+        pltpu.VMEM(x.shape, jnp.float32),
+        pltpu.VMEM(c.shape, jnp.float32),
+        pltpu.VMEM((fields, levels, LANES), jnp.float32),
+        pltpu.VMEM((fields, levels, LANES), jnp.float32),
+        pltpu.VMEM(fw.shape, jnp.float32),
+        pltpu.VMEM(fe.shape, jnp.float32),
+        pltpu.VMEM((levels, LANES), jnp.float32),
+        pltpu.VMEM(cw.shape, jnp.float32),
+        pltpu.VMEM(x.shape, jnp.float32),
+        pltpu.VMEM((count, LANES), jnp.float32),
+        pltpu.VMEM((count, LANES), jnp.float32),
+        pltpu.VMEM((count, LANES), jnp.float32),
+        pltpu.SemaphoreType.DMA((7 + 2 * fields,)),
+    ]
     return pl.pallas_call(
         functools.partial(_step_kernel, step_index, with_sends),
         out_shape=tuple(outs),
-        in_specs=[pl.BlockSpec(memory_space=pltpu.SMEM)] * 2 + [_vmem()] * 13,
-        out_specs=tuple(_vmem() for _ in outs),
-        scratch_shapes=[pltpu.VMEM((count, LANES), jnp.float32)] * 3,
-    )(coef, d, x, c, prof, mass, cell, ie, iw, fn, fs, fw, fe, cs, cw)
+        in_specs=[smem, smem] + [_vmem()] * 5 + [anyspace] * 8,
+        out_specs=tuple(out_specs),
+        scratch_shapes=scratch,
+    )(coef, d, prof, mass, cell, ie, iw, x, c, fn, fs, fw, fe, cs, cw)
 
 
 def shift(value, axis, steps, periodic):

time: 59.8 us -> 63.1 us (1.055)
  Pallas kernels: 15 us -> 18.3 us
    pallas_call x2, Pallas kernels: 12.1 us -> 15.4 us  [step(): pl.pallas_call(functools.partial(_step_kernel, step_index, with_sends), o...]
where the time goes in v7:
time: 63.1 us; the launch traced here: 62.7 us
  starting transfers between devices  38.3 us (61%)
  Pallas kernels  18.3 us (29%)
  waiting for transfers between devices  3.19 us (5%)
  local copies, waits for them, and re-layouts  2.12 us (3%)
  between operations  0.76 us (1%)
    ppermute x8, starting transfers between devices, shift(): return lax.ppermute(value, axis, pairs)  38.3 us
    pallas_call x2, Pallas kernels, step(): pl.pallas_call(functools.partial(_step_kernel, step_index, with_sends), o...  15.4 us
    ppermute x8, waiting for transfers between devices, shift(): return lax.ppermute(value, axis, pairs)  3.19 us
    pallas_call x1, Pallas kernels, prep(): pl.pallas_call(_prep_kernel, out_shape=(_f32((fields + 1, levels, LANES))...  2.96 us
    unnamed x16, local copies, waits for them, and re-layouts  2.12 us
  transfers between devices with their start and end apart: 8, of which 3 were waited for; matrix products, arithmetic and copies ran while one was open for 0% of the time, Pallas kernels for 0%

profile of v7, /device:TPU:7, one launch (start us, length us, event | category | flops | bytes accessed | tf_op | source)
XLA Modules:
  0.0 62.7 jit_solution(6496506566506140930)
XLA Ops:
  0.6 3.0 %shard_map.104 = (f32[6,75,128]{2,1,0:T(8,128)}, f32[5,75,128]{2,1,0:T(8,128)}, f32[112,128]{1,0:T(8,128)}, f32[112,128]{1,0:T(8,128)}) custom-call(f32[5,600,128]{2,1,0:T(8,128)} %bitcast.3, f32[2,600,128]{2,1,0:T(8,128)} %bitcast.5, f32[75,384]{1,0:T(8,128)} %p_ref.3, f32[384]{0:T(512)} %m_ref.3, s32[2,32]{1,0:T(2,128)} %ie_ref.5, s32[2,32]{1,0:T(2,128)} %iw_ref.5), custom_call_target="tpu_custom_call" | custom-call | tf_op jit(solution)/shard_map/pallas_call | solution.py:235
  3.6 5.3 %collective-permute-start.1 = (f32[6,75,128]{2,1,0:T(8,128)}, f32[6,75,128]{2,1,0:T(8,128)S(1)}, u32[]{:S(2)}, u32[]{:S(2)}) collective-permute-start(f32[6,75,128]{2,1,0:T(8,128)} %get-tuple-element.16), channel_id=1, source_target_pairs={{0,1},{1,2},{2,3},{3,4},{4,5},{5,6},{6,7},{7,8},{8,9},{9,10},{10,1... | collective-permute-start | bytes 691208 | tf_op jit(solution)/shard_map/ppermute | solution.py:293
  8.9 1.9 %collective-permute-start = (f32[5,75,128]{2,1,0:T(8,128)}, f32[5,75,128]{2,1,0:T(8,128)S(1)}, u32[]{:S(2)}, u32[]{:S(2)}) collective-permute-start(f32[5,75,128]{2,1,0:T(8,128)} %get-tuple-element.15), channel_id=1, source_target_pairs={{1,0},{2,1},{3,2},{4,3},{5,4},{6,5},{7,6},{8,7},{9,8},{10,9},{11,1... | collective-permute-start | bytes 576008 | tf_op jit(solution)/shard_map/ppermute | solution.py:293
  10.8 3.6 %collective-permute-start.2 = (f32[112,128]{1,0:T(8,128)}, f32[112,128]{1,0:T(8,128)S(1)}, u32[]{:S(2)}, u32[]{:S(2)}) collective-permute-start(f32[112,128]{1,0:T(8,128)} %get-tuple-element.17), channel_id=1, source_target_pairs={{0,16},{16,32},{32,48},{48,64},{64,80},{80,96},{96,112},{112,128},... | collective-permute-start | bytes 172040 | tf_op jit(solution)/shard_map/ppermute | solution.py:293
  14.4 9.6 %collective-permute-start.3 = (f32[112,128]{1,0:T(8,128)}, f32[112,128]{1,0:T(8,128)S(1)}, u32[]{:S(2)}, u32[]{:S(2)}) collective-permute-start(f32[112,128]{1,0:T(8,128)} %get-tuple-element.18), channel_id=1, source_target_pairs={{0,496},{16,0},{32,16},{48,32},{64,48},{80,64},{96,80},{112,96},{1... | collective-permute-start | bytes 172040 | tf_op jit(solution)/shard_map/ppermute | solution.py:293
  24.0 0.6 %collective-permute-done.2.fw_hbm.cw_hbm = f32[112,128]{1,0:T(8,128)S(1)} collective-permute-done((f32[112,128]{1,0:T(8,128)}, f32[112,128]{1,0:T(8,128)S(1)}, u32[]{:S(2)}, u32[]{:S(2)}) %collective-permute-start.2) | collective-permute-done | bytes 57376 | tf_op jit(solution)/shard_map/ppermute | solution.py:293
  24.6 0.0 copy-start.1
  24.6 1.0 %collective-permute-done.3.fe_hbm = f32[112,128]{1,0:T(8,128)S(1)} collective-permute-done((f32[112,128]{1,0:T(8,128)}, f32[112,128]{1,0:T(8,128)S(1)}, u32[]{:S(2)}, u32[]{:S(2)}) %collective-permute-start.3) | collective-permute-done | bytes 57376 | tf_op jit(solution)/shard_map/ppermute | solution.py:293
  25.6 0.0 copy-start.7
  25.6 0.0 collective-permute-done.fn_hbm
  25.6 0.0 copy-start.4
  25.6 0.0 collective-permute-done.1.fs_hbm.cs_hbm
  25.6 0.0 copy-done.1
  25.7 0.6 copy-done.7
  26.2 0.1 copy-done.4
  26.3 0.0 copy-start
  26.3 0.7 %copy-done = f32[6,75,128]{2,1,0:T(8,128)} copy-done((f32[6,75,128]{2,1,0:T(8,128)}, f32[6,75,128]{2,1,0:T(8,128)S(1)}, u32[]{:S(2)}) %copy-start) | copy-done | bytes 230424
  27.0 8.1 %shard_map.105 = (f32[5,600,128]{2,1,0:T(8,128)}, f32[75,384]{1,0:T(8,128)}, f32[384]{0:T(512)}, f32[5,75,128]{2,1,0:T(8,128)}, f32[5,75,128]{2,1,0:T(8,128)}, /*index=5*/f32[112,128]{1,0:T(8,128)}, f32[112,128]{1,0:T(8,128)}) custom-call(f32[5]{0:T(128)} %coef_ref.3, f32[75]{0:T(128)} %d_ref.3, f32[75,384]{1,0:T(8,128)} %p_ref.3, f32[384]{0:T(512)} %m_ref.3, ...), custom_call_target="tpu_custom_call" | custom-call | tf_op jit(solution)/shard_map/pallas_call | solution.py:278
  35.1 2.7 %collective-permute-start.4 = (f32[5,75,128]{2,1,0:T(8,128)}, f32[5,75,128]{2,1,0:T(8,128)S(1)}, u32[]{:S(2)}, u32[]{:S(2)}) collective-permute-start(f32[5,75,128]{2,1,0:T(8,128)} %get-tuple-element.22), channel_id=1, source_target_pairs={{1,0},{2,1},{3,2},{4,3},{5,4},{6,5},{7,6},{8,7},{9,8},{10,9},{11,1... | collective-permute-start | bytes 576008 | tf_op jit(solution)/shard_map/ppermute | solution.py:293
  37.8 7.9 %collective-permute-start.5 = (f32[5,75,128]{2,1,0:T(8,128)}, f32[5,75,128]{2,1,0:T(8,128)S(1)}, u32[]{:S(2)}, u32[]{:S(2)}) collective-permute-start(f32[5,75,128]{2,1,0:T(8,128)} %get-tuple-element.23), channel_id=1, source_target_pairs={{0,1},{1,2},{2,3},{3,4},{4,5},{5,6},{6,7},{7,8},{8,9},{9,10},{10,1... | collective-permute-start | bytes 576008 | tf_op jit(solution)/shard_map/ppermute | solution.py:293
  45.7 1.9 %collective-permute-start.6 = (f32[112,128]{1,0:T(8,128)}, f32[112,128]{1,0:T(8,128)S(1)}, u32[]{:S(2)}, u32[]{:S(2)}) collective-permute-start(f32[112,128]{1,0:T(8,128)} %get-tuple-element.24), channel_id=1, source_target_pairs={{0,16},{16,32},{32,48},{48,64},{64,80},{80,96},{96,112},{112,128},... | collective-permute-start | bytes 172040 | tf_op jit(solution)/shard_map/ppermute | solution.py:293
  47.6 5.5 %collective-permute-start.7 = (f32[112,128]{1,0:T(8,128)}, f32[112,128]{1,0:T(8,128)S(1)}, u32[]{:S(2)}, u32[]{:S(2)}) collective-permute-start(f32[112,128]{1,0:T(8,128)} %get-tuple-element.25), channel_id=1, source_target_pairs={{0,496},{16,0},{32,16},{48,32},{64,48},{80,64},{96,80},{112,96},{1... | collective-permute-start | bytes 172040 | tf_op jit(solution)/shard_map/ppermute | solution.py:293
  53.1 0.0 collective-permute-done.6.fw_hbm
  53.1 0.0 copy-start.5
  53.1 1.5 %collective-permute-done.7.fe_hbm = f32[112,128]{1,0:T(8,128)S(1)} collective-permute-done((f32[112,128]{1,0:T(8,128)}, f32[112,128]{1,0:T(8,128)S(1)}, u32[]{:S(2)}, u32[]{:S(2)}) %collective-permute-start.7) | collective-permute-done | bytes 57376 | tf_op jit(solution)/shard_map/ppermute | solution.py:293
  54.6 0.0 copy-start.6
  54.6 0.0 collective-permute-done.4.fn_hbm
  54.6 0.0 copy-start.2
  54.6 0.0 collective-permute-done.5.fs_hbm
  54.6 0.0 copy-start.3
  54.6 0.0 copy-done.5
  54.7 0.6 copy-done.6
  55.2 0.1 copy-done.2
  55.3 0.1 copy-done.3
  55.4 7.3 %shard_map.106 = (f32[5,600,128]{2,1,0:T(8,128)}, f32[75,384]{1,0:T(8,128)}, f32[384]{0:T(512)}) custom-call(f32[5]{0:T(128)} %coef_ref.3, f32[75]{0:T(128)} %d_ref.3, f32[75,384]{1,0:T(8,128)} %get-tuple-element.19.p_ref, f32[384]{0:T(512)} %get-tuple-element.20.m_ref, s32[2,384]{1,0:T(2,128)} %cell_ref.3, s32[2,32]{1,0:T(2,128)} %ie_ref.5, ...), custom_call_target="tpu_custom_call" | custom-call | tf_op jit(solution)/shard_map/pallas_call | solution.py:278
Async XLA Ops:
  3.6 22.1 %collective-permute-start.1 = (f32[6,75,128]{2,1,0:T(8,128)}, f32[6,75,128]{2,1,0:T(8,128)S(1)}, u32[]{:S(2)}, u32[]{:S(2)}) collective-permute-start(f32[6,75,128]{2,1,0:T(8,128)} %get-tuple-element.16), channel_id=1, source_target_pairs={{0,1},{1,2},{2,3},{3,4},{4,5},{5,6},{6,7},{7,8},{8,9},{9,10},{10,1... | collective-permute-start | bytes 691208 | tf_op jit(solution)/shard_map/ppermute | solution.py:293
  8.9 16.8 %collective-permute-start = (f32[5,75,128]{2,1,0:T(8,128)}, f32[5,75,128]{2,1,0:T(8,128)S(1)}, u32[]{:S(2)}, u32[]{:S(2)}) collective-permute-start(f32[5,75,128]{2,1,0:T(8,128)} %get-tuple-element.15), channel_id=1, source_target_pairs={{1,0},{2,1},{3,2},{4,3},{5,4},{6,5},{7,6},{8,7},{9,8},{10,9},{11,1... | collective-permute-start | bytes 576008 | tf_op jit(solution)/shard_map/ppermute | solution.py:293
  10.8 13.8 %collective-permute-start.2 = (f32[112,128]{1,0:T(8,128)}, f32[112,128]{1,0:T(8,128)S(1)}, u32[]{:S(2)}, u32[]{:S(2)}) collective-permute-start(f32[112,128]{1,0:T(8,128)} %get-tuple-element.17), channel_id=1, source_target_pairs={{0,16},{16,32},{32,48},{48,64},{64,80},{80,96},{96,112},{112,128},... | collective-permute-start | bytes 172040 | tf_op jit(solution)/shard_map/ppermute | solution.py:293
  14.4 11.3 %collective-permute-start.3 = (f32[112,128]{1,0:T(8,128)}, f32[112,128]{1,0:T(8,128)S(1)}, u32[]{:S(2)}, u32[]{:S(2)}) collective-permute-start(f32[112,128]{1,0:T(8,128)} %get-tuple-element.18), channel_id=1, source_target_pairs={{0,496},{16,0},{32,16},{48,32},{64,48},{80,64},{96,80},{112,96},{1... | collective-permute-start | bytes 172040 | tf_op jit(solution)/shard_map/ppermute | solution.py:293
  24.6 1.0 %copy-start.1 = (f32[112,128]{1,0:T(8,128)}, f32[112,128]{1,0:T(8,128)S(1)}, u32[]{:S(2)}) copy-start(f32[112,128]{1,0:T(8,128)S(1)} %collective-permute-done.2.fw_hbm.cw_hbm) | copy-start | bytes 172036
  25.6 0.6 copy-start.7
  25.6 0.7 %copy-start.4 = (f32[5,75,128]{2,1,0:T(8,128)}, f32[5,75,128]{2,1,0:T(8,128)S(1)}, u32[]{:S(2)}) copy-start(f32[5,75,128]{2,1,0:T(8,128)S(1)} %collective-permute-done.fn_hbm) | copy-start | bytes 576004
  26.3 0.7 %copy-start = (f32[6,75,128]{2,1,0:T(8,128)}, f32[6,75,128]{2,1,0:T(8,128)S(1)}, u32[]{:S(2)}) copy-start(f32[6,75,128]{2,1,0:T(8,128)S(1)} %collective-permute-done.1.fs_hbm.cs_hbm) | copy-start | bytes 691204
  35.1 19.5 %collective-permute-start.4 = (f32[5,75,128]{2,1,0:T(8,128)}, f32[5,75,128]{2,1,0:T(8,128)S(1)}, u32[]{:S(2)}, u32[]{:S(2)}) collective-permute-start(f32[5,75,128]{2,1,0:T(8,128)} %get-tuple-element.22), channel_id=1, source_target_pairs={{1,0},{2,1},{3,2},{4,3},{5,4},{6,5},{7,6},{8,7},{9,8},{10,9},{11,1... | collective-permute-start | bytes 576008 | tf_op jit(solution)/shard_map/ppermute | solution.py:293
  37.8 16.8 %collective-permute-start.5 = (f32[5,75,128]{2,1,0:T(8,128)}, f32[5,75,128]{2,1,0:T(8,128)S(1)}, u32[]{:S(2)}, u32[]{:S(2)}) collective-permute-start(f32[5,75,128]{2,1,0:T(8,128)} %get-tuple-element.23), channel_id=1, source_target_pairs={{0,1},{1,2},{2,3},{3,4},{4,5},{5,6},{6,7},{7,8},{8,9},{9,10},{10,1... | collective-permute-start | bytes 576008 | tf_op jit(solution)/shard_map/ppermute | solution.py:293
  45.7 7.4 %collective-permute-start.6 = (f32[112,128]{1,0:T(8,128)}, f32[112,128]{1,0:T(8,128)S(1)}, u32[]{:S(2)}, u32[]{:S(2)}) collective-permute-start(f32[112,128]{1,0:T(8,128)} %get-tuple-element.24), channel_id=1, source_target_pairs={{0,16},{16,32},{32,48},{48,64},{64,80},{80,96},{96,112},{112,128},... | collective-permute-start | bytes 172040 | tf_op jit(solution)/shard_map/ppermute | solution.py:293
  47.6 7.0 %collective-permute-start.7 = (f32[112,128]{1,0:T(8,128)}, f32[112,128]{1,0:T(8,128)S(1)}, u32[]{:S(2)}, u32[]{:S(2)}) collective-permute-start(f32[112,128]{1,0:T(8,128)} %get-tuple-element.25), channel_id=1, source_target_pairs={{0,496},{16,0},{32,16},{48,32},{64,48},{80,64},{96,80},{112,96},{1... | collective-permute-start | bytes 172040 | tf_op jit(solution)/shard_map/ppermute | solution.py:293
  53.1 1.6 %copy-start.5 = (f32[112,128]{1,0:T(8,128)}, f32[112,128]{1,0:T(8,128)S(1)}, u32[]{:S(2)}) copy-start(f32[112,128]{1,0:T(8,128)S(1)} %collective-permute-done.6.fw_hbm) | copy-start | bytes 172036
  54.6 0.6 copy-start.6
  54.6 0.7 %copy-start.2 = (f32[5,75,128]{2,1,0:T(8,128)}, f32[5,75,128]{2,1,0:T(8,128)S(1)}, u32[]{:S(2)}) copy-start(f32[5,75,128]{2,1,0:T(8,128)S(1)} %collective-permute-done.4.fn_hbm) | copy-start | bytes 576004
  54.6 0.8 %copy-start.3 = (f32[5,75,128]{2,1,0:T(8,128)}, f32[5,75,128]{2,1,0:T(8,128)S(1)}, u32[]{:S(2)}) copy-start(f32[5,75,128]{2,1,0:T(8,128)S(1)} %collective-permute-done.5.fs_hbm) | copy-start | bytes 576004
